TPU v7x, 256 devices: a whole 4x4x8 slice. The times are simulated.
256 devices in a mesh: ctx: 16 (over z_lo, x, core), tp: 16 (over z_hi, y).
Axes of the slice: x: 4, y: 4, z: 8 (z_hi: 4, z_lo: 2; z = z_hi * 2 + z_lo), core: 2. Of those that a mesh axis runs over, the one named last changes fastest.
Arguments:
- tokens: bfloat16 [8192, 8192], P('ctx'), may hold values from -40 to 40
- doc_lengths: int32 [8], replicated, may hold values from 1 to 4096, 8192 in all
- w_query: bfloat16 [8192, 4096], P('ctx', 'tp'), may hold values from -0.0625 to 0.0625
- w_key: bfloat16 [8192, 512], P('ctx', 'tp'), may hold values from -0.0625 to 0.0625
- w_value: bfloat16 [8192, 512], P('ctx', 'tp'), may hold values from -0.0625 to 0.0625
- w_output: bfloat16 [4096, 8192], P('tp', 'ctx'), may hold values from -0.09375 to 0.09375
Outputs:
- layer_out: bfloat16 [8192, 8192], P(('ctx', 'tp'))
Inputs may be any that keep to these rules, and one draw needn't show every extreme that they name: `doc_lengths`: the 8 documents lie in order in the sequence, their lengths sum to 8192 and the longest has exactly 4096 tokens.
All inputs are finite; a program needn't handle non-finite values.
Results may differ from a plain program's by a relative error of at most 0.015.
Values may be sent and summed in bfloat16 or wider, within the bound.
No kernel may reach another device: no remote copies, remote signals or barrier semaphores. Data moves between devices by JAX's collectives and lax.ppermute only.
A program may use at most 64 MiB of HBM per device.

v0:
```python
import math

import jax
import jax.numpy as jnp
from jax import lax
from jax.sharding import PartitionSpec as P

HD = 128
HEADS = 32
KVH = 4


rope_base = 500000.0
neg_large = -1e30


def rotate(field, positions):
    half_dim = field.shape[-1] // 2
    inverse_freq = rope_base ** (-2.0 * jnp.arange(half_dim, dtype=jnp.float32) / field.shape[-1])
    angles = positions.astype(jnp.float32)[:, None] * inverse_freq[None, :]
    cosine = jnp.cos(angles)[:, None, :]
    sine_part = jnp.sin(angles)[:, None, :]
    first_half = field[..., :half_dim]
    second_half = field[..., half_dim:]
    return jnp.concatenate(
        [
            first_half * cosine - second_half * sine_part,
            second_half * cosine + first_half * sine_part,
        ],
        axis=-1,
    )


def doc_of(positions, doc_starts):
    return jnp.sum((positions[:, None] >= doc_starts[None, :]).astype(jnp.int32), axis=1)


def on_device(tokens, doc_lengths, w_query, w_key, w_value, w_output):
    tok_rows = tokens.shape[0]
    first_row = lax.axis_index("ctx") * tok_rows
    positions = first_row + jnp.arange(tok_rows, dtype=jnp.int32)
    doc_starts = jnp.cumsum(doc_lengths) - doc_lengths
    doc_ids = doc_of(positions, doc_starts)
    query_sum = jnp.dot(
        tokens,
        lax.all_gather(w_query, "ctx", axis=0, tiled=True),
        preferred_element_type=jnp.float32,
    )
    key_sum = jnp.dot(
        tokens, lax.all_gather(w_key, "ctx", axis=0, tiled=True), preferred_element_type=jnp.float32
    )
    value_sum = jnp.dot(
        tokens,
        lax.all_gather(w_value, "ctx", axis=0, tiled=True),
        preferred_element_type=jnp.float32,
    )
    heads_dev = w_query.shape[1] // HD
    query = rotate(query_sum.reshape(tok_rows, heads_dev, HD), positions).astype(jnp.bfloat16)
    query = jnp.transpose(query, (1, 0, 2))
    key_all, value_all = (
        lax.all_gather(key_sum.astype(jnp.bfloat16), "tp", axis=1, tiled=True),
        lax.all_gather(value_sum.astype(jnp.bfloat16), "tp", axis=1, tiled=True),
    )
    kv_count = key_all.shape[1] // HD
    kv_head = lax.axis_index("tp") * heads_dev // (HEADS // KVH)
    key_raw = lax.dynamic_index_in_dim(
        key_all.reshape(tok_rows, HD, kv_count), kv_head, 2, keepdims=False
    )
    key_rot = rotate(key_raw.astype(jnp.float32)[:, None, :], positions)[:, 0, :].astype(
        jnp.bfloat16
    )
    value_own = lax.dynamic_index_in_dim(
        value_all.reshape(tok_rows, HD, kv_count), kv_head, 2, keepdims=False
    )
    score_scale = HD ** (-0.5)
    first_doc = doc_ids[0]
    last_position = positions[tok_rows - 1]
    start_state = (
        jnp.full((heads_dev, tok_rows), neg_large, jnp.float32),
        jnp.zeros((heads_dev, tok_rows), jnp.float32),
        jnp.zeros((heads_dev, tok_rows, HD), jnp.float32),
    )
    key_rows = lax.all_gather(key_rot, "ctx", axis=0, tiled=True)
    value_rows = lax.all_gather(value_own, "ctx", axis=0, tiled=True)
    key_count = key_rows.shape[0]
    block_rows = math.gcd(key_count, 512)

    def one_block(block_index, state):
        key_start = block_index * block_rows
        key_block = lax.dynamic_slice_in_dim(key_rows, block_index * block_rows, block_rows, 0)
        value_block = lax.dynamic_slice_in_dim(value_rows, block_index * block_rows, block_rows, 0)
        key_positions = key_start + jnp.arange(block_rows, dtype=jnp.int32)
        key_docs = doc_of(key_positions, doc_starts)

        def update(inner):
            best_score, row_total, weighted = inner
            scores = (
                jnp.einsum("hqd,kd->hqk", query, key_block, preferred_element_type=jnp.float32)
                * score_scale
            )
            allowed = (key_positions[None, :] <= positions[:, None]) & (
                key_docs[None, :] == doc_ids[:, None]
            )
            scores = jnp.where(allowed[None], scores, neg_large)
            new_best = jnp.maximum(best_score, jnp.max(scores, axis=-1))
            factor = jnp.exp(best_score - new_best)
            expo = jnp.where(allowed[None], jnp.exp(scores - new_best[..., None]), 0.0)
            row_total = row_total * factor + jnp.sum(expo, axis=-1)
            weighted = weighted * factor[..., None] + jnp.einsum(
                "hqk,kd->hqd",
                expo.astype(jnp.bfloat16),
                value_block,
                preferred_element_type=jnp.float32,
            )
            return (new_best, row_total, weighted)

        needed = (key_start <= last_position) & (key_docs[block_rows - 1] >= first_doc)
        return lax.cond(needed, update, lambda unchanged: unchanged, state)

    best_score, row_total, weighted = lax.fori_loop(
        0, key_count // block_rows, one_block, start_state
    )
    attended = (weighted / row_total[..., None]).astype(jnp.bfloat16)
    attended = jnp.transpose(attended, (1, 0, 2)).reshape(tok_rows, heads_dev * HD)
    output_full = lax.all_gather(w_output, "ctx", axis=1, tiled=True)
    return lax.psum_scatter(
        jnp.dot(attended, output_full, preferred_element_type=jnp.float32).astype(jnp.bfloat16),
        "tp",
        scatter_dimension=0,
        tiled=True,
    )


def solution(mesh):
    placed = (P("ctx", None), P(), P("ctx", "tp"), P("ctx", "tp"), P("ctx", "tp"), P("tp", "ctx"))
    return jax.shard_map(
        on_device, mesh=mesh, in_specs=placed, out_specs=P(("ctx", "tp"), None), check_vma=False
    )
```

profile of v0, /device:TPU:6, one launch (start us, length us, event | category | flops | bytes accessed | tf_op | source)
XLA Modules:
  0.0 400.2 jit_solution(14418746316033721426)
XLA Ops:
  6.6 17.3 %all_gather.24 = bf16[8192,32]{0,1:T(8,128)(2,1)S(1)} all-gather(bf16[512,32]{0,1:T(8,128)(2,1)} %param.13), channel_id=1, replica_groups=mesh['ctx'=16,'tp'=16] {'ctx'}, dimensions={0}, use_global_device_ids=true | all-gather | bytes 557056 | tf_op jit(solution)/shard_map/all_gather | solution.py:50
  23.9 6.0 %convolution_convert_fusion.2 = bf16[512,32]{0,1:T(8,128)(2,1)S(1)} fusion(bf16[512,8192]{1,0:T(8,128)(2,1)} %param.10, bf16[8192,32]{0,1:T(8,128)(2,1)S(1)} %all_gather.24), kind=kOutput, calls=%fused_computation.30 | convolution fusion | flops 268451840 | bytes 8945664 | tf_op jit(solution)/shard_map/dot_general | solution.py:49
  29.9 50.0 %all_gather.25 = bf16[512,512]{0,1:T(8,128)(2,1)S(1)} all-gather(bf16[512,32]{0,1:T(8,128)(2,1)S(1)} %convolution_convert_fusion.2), channel_id=1, replica_groups=mesh['ctx'=16,'tp'=16] {'tp'}, dimensions={1}, use_global_device_ids=true | all-gather | bytes 557056 | tf_op jit(solution)/shard_map/all_gather | solution.py:61
  80.9 0.7 pad_maximum_fusion
  81.7 0.7 all-gather.7.cloned.1.call-update
  82.4 21.1 %all_gather.28 = bf16[8192,32]{0,1:T(8,128)(2,1)S(1)} all-gather(bf16[512,32]{0,1:T(8,128)(2,1)S(1)} %copy-done), channel_id=1, replica_groups=mesh['ctx'=16,'tp'=16] {'ctx'}, dimensions={0}, use_global_device_ids=true | all-gather | bytes 557056 | tf_op jit(solution)/shard_map/all_gather | solution.py:54
  103.6 6.0 %convolution_convert_fusion.1 = bf16[512,32]{0,1:T(8,128)(2,1)S(1)} fusion(bf16[512,8192]{1,0:T(8,128)(2,1)} %param.10, bf16[8192,32]{0,1:T(8,128)(2,1)S(1)} %all_gather.28), kind=kOutput, calls=%fused_computation.29 | convolution fusion | flops 268451840 | bytes 8945664 | tf_op jit(solution)/shard_map/dot_general | solution.py:52
  109.6 43.7 %all_gather.29 = bf16[512,512]{0,1:T(8,128)(2,1)S(1)} all-gather(bf16[512,32]{0,1:T(8,128)(2,1)S(1)} %convolution_convert_fusion.1), channel_id=1, replica_groups=mesh['ctx'=16,'tp'=16] {'tp'}, dimensions={1}, use_global_device_ids=true | all-gather | bytes 557056 | tf_op jit(solution)/shard_map/all_gather | solution.py:62
  153.7 0.8 copy.41
  155.5 0.6 slice.25
  156.8 1.8 multiply_cosine_fusion
  158.5 3.2 copy.35
  161.8 6.9 %fusion.31 = f32[512,256]{0,1:T(8,128)S(1)} fusion(bf16[512,8192]{1,0:T(8,128)(2,1)} %param.10, bf16[8192,256]{1,0:T(8,128)(2,1)} %all-gather.7.cloned.1.call-done), kind=kOutput, calls=%fused_computation.58 | convolution fusion | flops 2147483648 | bytes 13107200 | tf_op jit(solution)/shard_map/dot_general | solution.py:44
  169.2 1.2 subtract_convert_fusion
  170.5 24.6 %all-gather.13.cloned.1.call-done = bf16[8192,128,1]{1,0,2:T(8,128)(2,1)} async-done(((bf16[512,128,1]{1,0,2:T(8,128)(2,1)}), bf16[8192,128,1]{1,0,2:T(8,128)(2,1)}) %all-gather.13.cloned.1.call-update) | async-done | bytes 2097168 | tf_op jit(solution)/shard_map/all_gather | solution.py:84
  195.2 46.3 %while.18 = (s32[]{:T(128)}, f32[2,512]{1,0:T(2,128)S(1)}, f32[2,512]{1,0:T(2,128)S(1)}, f32[2,512,128]{2,1,0:T(8,128)S(1)}, s32[]{:T(128)}, /*index=5*/s32[8]{0...) while((s32[]{:T(128)}, f32[2,512]{1,0:T(2,128)S(1)}, ...), condition=%wide.region_8.9_spmd.clone, body=%wide.region_2.8_spmd.clone.sunk | while | flops 276315136 | bytes 9003425 | solution.py:120
  210.0 3.3 conditional.3
  210.9 0.6 fusion.4
  211.5 1.9 convolution_add_fusion
  215.8 3.4 conditional.3
  216.7 0.6 fusion.4
  217.3 1.9 convolution_add_fusion
  241.7 7.8 %convolution_convert_fusion = bf16[512,8192]{1,0:T(8,128)(2,1)} fusion(bf16[512,256]{0,1:T(8,128)(2,1)S(1)} %bitcast.54, bf16[256,8192]{1,0:T(8,128)(2,1)} %all-gather.9.cloned.1.call-done), kind=kOutput, calls=%fused_computation.28 | convolution fusion | flops 2151677952 | bytes 12845056 | tf_op jit(solution)/shard_map/dot_general | solution.py:127
  249.6 144.1 %reduce-scatter.2.cloned.1.call-done = bf16[32,8192]{1,0:T(8,128)(2,1)} async-done(((bf16[512,8192]{1,0:T(8,128)(2,1)}), bf16[32,8192]{1,0:T(8,128)(2,1)}) %reduce-scatter.2.cloned.1.call-update) | async-done | bytes 524304 | tf_op jit(solution)/shard_map/reduce_scatter | solution.py:126
  (128 shorter events, 16.4 us)
Async XLA Ops:
  6.5 152.0 %all-gather.11.cloned.1.call-start = ((), (), s32[]{:S(2)}) async-start(), calls=%async_computation.4 | async-start | bytes 2228224 | tf_op jit(solution)/shard_map/all_gather | solution.py:83
  29.8 52.6 %copy-start = (bf16[512,32]{0,1:T(8,128)(2,1)S(1)}, bf16[512,32]{0,1:T(8,128)(2,1)}, u32[]{:S(2)}) copy-start(bf16[512,32]{0,1:T(8,128)(2,1)} %param.14) | copy-start | bytes 98308
  81.6 80.2 %all-gather.7.cloned.1.call-start = ((), (), s32[]{:S(2)}) async-start(), calls=%async_computation.1 | async-start | bytes 4456448 | tf_op jit(solution)/shard_map/all_gather | solution.py:46
  82.4 112.8 %all-gather.13.cloned.1.call-start = ((), (), s32[]{:S(2)}) async-start(), calls=%async_computation.5 | async-start | bytes 2228224 | tf_op jit(solution)/shard_map/all_gather | solution.py:84
  109.6 45.8 %copy-start.1 = (s32[8]{0:T(128)S(1)}, s32[8]{0:T(128)}, u32[]{:S(2)}) copy-start(s32[8]{0:T(128)} %param.11) | copy-start | bytes 100
  154.5 87.2 %all-gather.9.cloned.1.call-start = ((), (), s32[]{:S(2)}) async-start(), calls=%async_computation.2 | async-start | bytes 4456448 | tf_op jit(solution)/shard_map/all_gather | solution.py:125
  155.1 238.5 %reduce-scatter.2.cloned.1.call-start = ((), (), s32[]{:S(2)}) async-start(), calls=%async_computation.3 | async-start | bytes 8912896 | tf_op jit(solution)/shard_map/reduce_scatter | solution.py:126
Sparse Core Ops, SparseCore 0:
  81.7 33.2 all-gather.10
  116.9 38.8 all-gather.6
  157.7 37.4 all-gather.12
  196.8 39.5 all-gather.8
  249.7 143.9 reduce-scatter.1
where the time goes:
time: 401 us; the launch traced here: 400 us
  waiting for transfers between devices  170 us (42%)
  blocking collectives  132 us (33%)
  matrix products  31.5 us (8%)
  loops' own time  29.3 us (7%)
  local copies, waits for them, and re-layouts  15.6 us (4%)
  between operations  13.3 us (3%)
  other arithmetic  7.85 us (2%)
    reduce_scatter x1, waiting for transfers between devices, on_device(): lax.psum_scatter(jnp.dot(attended, output_full, preferred_element_type=jn...  144 us
    all_gather x1, blocking collectives, on_device(): lax.all_gather(key_sum.astype(jnp.bfloat16), 'tp', axis=1, tiled=True)  50 us
    all_gather x1, blocking collectives, on_device(): lax.all_gather(value_sum.astype(jnp.bfloat16), 'tp', axis=1, tiled=True)  43.7 us
    another operation x1, loops' own time, on_device(): lax.fori_loop(0, key_count // block_rows, one_block, start_state)  29 us
    all_gather x1, waiting for transfers between devices, on_device(): value_rows = lax.all_gather(value_own, 'ctx', axis=0, tiled=True)  24.6 us
    all_gather x1, blocking collectives, on_device(): lax.all_gather(w_value, 'ctx', axis=0, tiled=True)  21.1 us
    all_gather x1, blocking collectives, on_device(): lax.all_gather(w_key, 'ctx', axis=0, tiled=True)  17.3 us
    slice x16, local copies, waits for them, and re-layouts, one_block(): key_docs[block_rows - 1] >= first_doc  8.91 us
  transfers between devices with their start and end apart: 5, of which 2 were waited for; matrix products, arithmetic and copies ran while one was open for 10% of the time, Pallas kernels for 0%

commit v1 on v0

v1 whole, which is shorter than its diff:
```python
import jax
import jax.numpy as jnp
from jax import lax
from jax.sharding import PartitionSpec as P

HD = 128
HEADS = 32
KVH = 4
DOC_MOST = 4096

rope_base = 500000.0


def rotate(field, positions):
    half_dim = field.shape[-1] // 2
    inverse_freq = rope_base ** (-2.0 * jnp.arange(half_dim, dtype=jnp.float32) / field.shape[-1])
    angles = positions.astype(jnp.float32)[:, None] * inverse_freq[None, :]
    cosine = jnp.cos(angles)[:, None, :]
    sine_part = jnp.sin(angles)[:, None, :]
    first_half = field[..., :half_dim]
    second_half = field[..., half_dim:]
    return jnp.concatenate(
        [
            first_half * cosine - second_half * sine_part,
            second_half * cosine + first_half * sine_part,
        ],
        axis=-1,
    )


def doc_of(positions, doc_starts):
    return jnp.sum((positions[:, None] >= doc_starts[None, :]).astype(jnp.int32), axis=1)


def on_device(tokens, doc_lengths, w_query, w_key, w_value, w_output):
    tok_rows = tokens.shape[0]
    n_tp = lax.axis_size("tp")
    ctx_index = lax.axis_index("ctx")
    tp_index = lax.axis_index("tp")
    first_row = ctx_index * tok_rows
    positions = first_row + jnp.arange(tok_rows, dtype=jnp.int32)
    doc_starts = jnp.cumsum(doc_lengths) - doc_lengths
    doc_ids = doc_of(positions, doc_starts)

    q_cols = w_query.shape[1]
    k_cols = w_key.shape[1]
    w_all = jnp.concatenate([w_query, w_key, w_value], axis=1)
    w_full = lax.all_gather(w_all, "ctx", axis=0, tiled=True)
    proj = jnp.dot(tokens, w_full, preferred_element_type=jnp.float32)
    query_sum = proj[:, :q_cols]
    kv_local = proj[:, q_cols:].astype(jnp.bfloat16)

    heads_dev = q_cols // HD
    query = rotate(query_sum.reshape(tok_rows, heads_dev, HD), positions).astype(jnp.bfloat16)

    kv_parts = lax.all_gather(kv_local, "tp", axis=0, tiled=False)
    dd = k_cols // KVH
    kv_head = tp_index * heads_dev // (HEADS // KVH)
    kv_parts = kv_parts.reshape(n_tp, tok_rows, 2, dd, KVH)
    kv_own = lax.dynamic_index_in_dim(kv_parts, kv_head, 4, keepdims=False)
    kv_own = jnp.transpose(kv_own, (1, 2, 0, 3)).reshape(tok_rows, 2, n_tp * dd)
    key_raw = kv_own[:, 0, :]
    value_own = kv_own[:, 1, :]
    key_rot = rotate(key_raw.astype(jnp.float32)[:, None, :], positions)[:, 0, :].astype(jnp.bfloat16)

    kv_rows_local = jnp.concatenate([key_rot, value_own], axis=1)
    kv_rows = lax.all_gather(kv_rows_local, "ctx", axis=0, tiled=True)
    seq = kv_rows.shape[0]

    window_blocks = min(seq // tok_rows, -(-(DOC_MOST - 1) // tok_rows) + 1)
    window = window_blocks * tok_rows
    start_block = jnp.clip(ctx_index - (window_blocks - 1), 0, seq // tok_rows - window_blocks)
    key_start = start_block * tok_rows
    kv_win = lax.dynamic_slice_in_dim(kv_rows, key_start, window, 0)
    key_win = kv_win[:, :HD]
    value_win = kv_win[:, HD:]
    key_positions = key_start + jnp.arange(window, dtype=jnp.int32)
    key_docs = doc_of(key_positions, doc_starts)

    score_scale = HD ** (-0.5)
    n_split = 2
    part_rows = tok_rows // n_split
    q_parts = jnp.transpose(query, (1, 0, 2)).reshape(heads_dev * n_split, part_rows, HD)
    pos_parts = jnp.tile(positions.reshape(n_split, part_rows), (heads_dev, 1))
    doc_parts = jnp.tile(doc_ids.reshape(n_split, part_rows), (heads_dev, 1))

    def one_part(args):
        q_part, pos_part, doc_part = args
        allowed = (key_positions[None, :] <= pos_part[:, None]) & (key_docs[None, :] == doc_part[:, None])
        scores = jnp.dot(q_part, key_win.T, preferred_element_type=jnp.float32) * score_scale
        masked = jnp.where(allowed, scores, -jnp.inf)
        row_max = jnp.max(masked, axis=-1, keepdims=True)
        expo = jnp.where(allowed, jnp.exp(masked - row_max), 0.0)
        row_total = jnp.sum(expo, axis=-1, keepdims=True)
        mixed = jnp.dot(expo.astype(jnp.bfloat16), value_win, preferred_element_type=jnp.float32)
        return (mixed / row_total).astype(jnp.bfloat16)

    attended = lax.map(one_part, (q_parts, pos_parts, doc_parts))
    attended = attended.reshape(heads_dev, tok_rows, HD)
    attended = jnp.transpose(attended, (1, 0, 2)).reshape(tok_rows, heads_dev * HD)

    output_full = lax.all_gather(w_output, "ctx", axis=1, tiled=True)
    return lax.psum_scatter(
        jnp.dot(attended, output_full, preferred_element_type=jnp.float32).astype(jnp.bfloat16),
        "tp",
        scatter_dimension=0,
        tiled=True,
    )


def solution(mesh):
    placed = (P("ctx", None), P(), P("ctx", "tp"), P("ctx", "tp"), P("ctx", "tp"), P("tp", "ctx"))
    return jax.shard_map(
        on_device, mesh=mesh, in_specs=placed, out_specs=P(("ctx", "tp"), None), check_vma=False
    )
```

time: 401 us -> 339 us (0.85)
  blocking collectives: 132 us -> 0 us
  waiting for transfers between devices: 170 us -> 272 us
  loops' own time: 29.3 us -> 0.08 us
  local copies, waits for them, and re-layouts: 15.6 us -> 9.47 us
    all_gather x4 -> x0, blocking collectives: 132 us -> none  [the longest x1 50 us: on_device(): lax.all_gather(key_sum.astype(jnp.bfloat16), 'tp', axis=1, tiled=True)]
    all_gather x3, waiting for transfers between devices: 24.6 us -> 136 us  [the longest x1 55.3 us: on_device(): kv_parts = lax.all_gather(kv_local, 'tp', axis=0, tiled=False)]
    another operation x17 -> x1, loops' own time: 29.3 us -> 0.08 us  [on_device(): attended = lax.map(one_part, (q_parts, pos_parts, doc_parts))]
    reduce_scatter x1, waiting for transfers between devices: 144 us -> 122 us  [on_device(): lax.psum_scatter(jnp.dot(attended, output_full, preferred_element_type=jn...]
    all_gather x1, waiting for transfers between devices: 0.02 us -> 14.1 us  [on_device(): output_full = lax.all_gather(w_output, 'ctx', axis=1, tiled=True)]
    slice x19 -> x3, local copies, waits for them, and re-layouts: 10.1 us -> 2.45 us  [the longest x1 1.78 us: on_device(): value_win = kv_win[:, HD:]]
    reduce_sum x2 -> x4, other arithmetic: 1.13 us -> 5.78 us  [one_part(): row_total = jnp.sum(expo, axis=-1, keepdims=True)]
    dot_general x7 -> x9, matrix products: 23.8 us -> 24.9 us  [the longest x4 8.79 us: one_part(): jnp.dot(q_part, key_win.T, preferred_element_type=jnp.float32) * score_scale]
  transfers between devices with their start and end apart: 5 -> 5, of which waited for: 2 -> 5; matrix products, arithmetic and copies ran while one was open for 10% -> 9% of each run, Pallas kernels for 0% -> 0%
where the time goes in v1:
time: 339 us
  waiting for transfers between devices  272 us (80%)
  matrix products  32.7 us (10%)
  between operations  13.3 us (4%)
  other arithmetic  10.6 us (3%)
  local copies, waits for them, and re-layouts  9.47 us (3%)
    reduce_scatter x1, waiting for transfers between devices, on_device(): lax.psum_scatter(jnp.dot(attended, output_full, preferred_element_type=jn...  122 us
    all_gather x1, waiting for transfers between devices, on_device(): kv_parts = lax.all_gather(kv_local, 'tp', axis=0, tiled=False)  55.3 us
    all_gather x1, waiting for transfers between devices, on_device(): w_full = lax.all_gather(w_all, 'ctx', axis=0, tiled=True)  47.7 us
    all_gather x1, waiting for transfers between devices, on_device(): kv_rows = lax.all_gather(kv_rows_local, 'ctx', axis=0, tiled=True)  32.8 us
    all_gather x1, waiting for transfers between devices, on_device(): output_full = lax.all_gather(w_output, 'ctx', axis=1, tiled=True)  14.1 us
    dot_general x4, matrix products, one_part(): jnp.dot(q_part, key_win.T, preferred_element_type=jnp.float32) * score_scale  8.79 us
    dot_general x4, matrix products, one_part(): jnp.dot(expo.astype(jnp.bfloat16), value_win, preferred_element_type=jnp....  8.27 us
    dot_general x1, matrix products, on_device(): proj = jnp.dot(tokens, w_full, preferred_element_type=jnp.float32)  7.84 us
  transfers between devices with their start and end apart: 5, of which 5 were waited for; matrix products, arithmetic and copies ran while one was open for 9% of the time, Pallas kernels for 0%

profile of v1, /device:TPU:6, one launch (start us, length us, event | category | flops | bytes accessed | tf_op | source)
XLA Modules:
  0.0 338.6 jit_solution(4860525413379743854)
XLA Ops:
  8.3 1.8 pad_maximum_fusion
  10.2 47.7 %all-gather.6.cloned.1.call-done = bf16[8192,320]{1,0:T(8,128)(2,1)} async-done(((bf16[512,320]{1,0:T(8,128)(2,1)}), bf16[8192,320]{1,0:T(8,128)(2,1)}) %all-gather.6.cloned.1.call-update) | async-done | bytes 5242896 | tf_op jit(solution)/shard_map/all_gather | solution.py:48
  57.9 7.8 %convolution_bitcast_fusion = f32[512,320]{0,1:T(8,128)S(1)} fusion(bf16[8192,320]{1,0:T(8,128)(2,1)} %all-gather.6.cloned.1.call-done, bf16[512,8192]{1,0:T(8,128)(2,1)} %param.8), kind=kOutput, calls=%fused_computation.20 | convolution fusion | flops 2684354560 | bytes 14286848 | tf_op jit(solution)/shard_map/dot_general | solution.py:49
  66.6 55.3 %all-gather.12.cloned.1.call-done = bf16[8192,64]{0,1:T(8,128)(2,1)} async-done(((bf16[512,64]{0,1:T(8,128)(2,1)}), bf16[8192,64]{0,1:T(8,128)(2,1)}) %all-gather.12.cloned.1.call-update) | async-done | bytes 1048592 | tf_op jit(solution)/shard_map/all_gather | solution.py:56
  121.9 1.6 copy.35
  128.3 32.8 %all-gather.8.cloned.1.call-done = bf16[8192,256]{0,1:T(8,128)(2,1)} async-done(((bf16[512,256]{0,1:T(8,128)(2,1)}), bf16[8192,256]{0,1:T(8,128)(2,1)}) %all-gather.8.cloned.1.call-update) | async-done | bytes 4194320 | tf_op jit(solution)/shard_map/all_gather | solution.py:67
  161.1 1.8 fusion.33
  164.3 23.0 %while.11 = (s32[]{:T(128)}, bf16[4,256,128]{2,1,0:T(8,128)(2,1)}, s32[4,256]{1,0:T(4,128)S(1)}, s32[4608]{0:T(1024)}, s32[4,256]{1,0:T(4,128)S(1)}, /*index=5*/...) while((s32[]{:T(128)}, bf16[4,256,128]{2,1,0:T(8,128)(2,1)}, ...), condition=%wide.region_6.7_spmd.clone, body=%wide.region_3.6_spmd.clone.sunk | while | flops 625283072 | bytes 16866456 | solution.py:98
  164.4 2.2 fusion.49
  166.6 1.4 fusion.50
  168.0 2.1 fusion.51
  170.1 2.2 fusion.49
  172.3 1.4 fusion.50
  173.8 2.1 fusion.51
  175.8 2.2 fusion.49
  178.0 1.4 fusion.50
  179.5 2.1 fusion.51
  181.6 2.2 fusion.49
  183.8 1.4 fusion.50
  185.2 2.1 fusion.51
  187.3 1.1 copy.32
  188.4 14.1 %all-gather.10.cloned.1.call-done = bf16[256,8192]{1,0:T(8,128)(2,1)} async-done(((bf16[256,512]{1,0:T(8,128)(2,1)}), bf16[256,8192]{1,0:T(8,128)(2,1)}) %all-gather.10.cloned.1.call-update) | async-done | bytes 4194320 | tf_op jit(solution)/shard_map/all_gather | solution.py:102
  202.5 7.8 %convolution_convert_fusion = bf16[512,8192]{1,0:T(8,128)(2,1)} fusion(bf16[512,256]{0,1:T(8,128)(2,1)S(1)} %bitcast.61, bf16[256,8192]{1,0:T(8,128)(2,1)} %all-gather.10.cloned.1.call-done), kind=kOutput, calls=%fused_computation.19 | convolution fusion | flops 2151677952 | bytes 12845056 | tf_op jit(solution)/shard_map/dot_general | solution.py:104
  210.3 121.8 %reduce-scatter.2.cloned.1.call-done = bf16[32,8192]{1,0:T(8,128)(2,1)} async-done(((bf16[512,8192]{1,0:T(8,128)(2,1)}), bf16[32,8192]{1,0:T(8,128)(2,1)}) %reduce-scatter.2.cloned.1.call-update) | async-done | bytes 524304 | tf_op jit(solution)/shard_map/reduce_scatter | solution.py:103
  (58 shorter events, 8.8 us)
Async XLA Ops:
  6.5 51.4 %all-gather.6.cloned.1.call-start = ((), (), s32[]{:S(2)}) async-start(), calls=%async_computation.1 | async-start | bytes 6684672 | tf_op jit(solution)/shard_map/all_gather | solution.py:48
  10.1 111.7 %all-gather.12.cloned.1.call-start = ((), (), s32[]{:S(2)}) async-start(), calls=%async_computation.5 | async-start | bytes 1114112 | tf_op jit(solution)/shard_map/all_gather | solution.py:56
  65.8 59.9 %copy-start.1 = (s32[8]{0:T(128)S(1)}, s32[8]{0:T(128)}, u32[]{:S(2)}) copy-start(s32[8]{0:T(128)} %param.9) | copy-start | bytes 100
  66.5 94.6 %all-gather.8.cloned.1.call-start = ((), (), s32[]{:S(2)}) async-start(), calls=%async_computation.2 | async-start | bytes 4456448 | tf_op jit(solution)/shard_map/all_gather | solution.py:67
  125.0 77.5 %all-gather.10.cloned.1.call-start = ((), (), s32[]{:S(2)}) async-start(), calls=%async_computation.3 | async-start | bytes 4456448 | tf_op jit(solution)/shard_map/all_gather | solution.py:102
  125.6 206.5 %reduce-scatter.2.cloned.1.call-start = ((), (), s32[]{:S(2)}) async-start(), calls=%async_computation.4 | async-start | bytes 8912896 | tf_op jit(solution)/shard_map/reduce_scatter | solution.py:103
  164.3 2.2 copy-start
  170.1 2.2 copy-start
  175.8 2.2 copy-start
  181.6 2.2 copy-start
Sparse Core Ops, SparseCore 0:
  10.3 47.6 all-gather.5
  66.6 55.2 all-gather.11
  125.1 35.8 all-gather.7
  162.7 39.7 all-gather.9
  210.4 121.5 reduce-scatter.1

commit v2 on v1

--- a/solution.py
+++ b/solution.py
@@ -53,29 +53,34 @@
     heads_dev = q_cols // HD
     query = rotate(query_sum.reshape(tok_rows, heads_dev, HD), positions).astype(jnp.bfloat16)
 
-    kv_parts = lax.all_gather(kv_local, "tp", axis=0, tiled=False)
     dd = k_cols // KVH
-    kv_head = tp_index * heads_dev // (HEADS // KVH)
-    kv_parts = kv_parts.reshape(n_tp, tok_rows, 2, dd, KVH)
-    kv_own = lax.dynamic_index_in_dim(kv_parts, kv_head, 4, keepdims=False)
-    kv_own = jnp.transpose(kv_own, (1, 2, 0, 3)).reshape(tok_rows, 2, n_tp * dd)
+    group = HEADS // KVH
+    kv_local = kv_local.reshape(tok_rows, 2, dd, KVH)
+    dest_heads = jnp.arange(n_tp, dtype=jnp.int32) * heads_dev // group
+    pieces = jnp.take(kv_local, dest_heads, axis=3)
+    pieces = jnp.transpose(pieces, (3, 0, 1, 2))
+    got = lax.all_to_all(pieces, "tp", 0, 0, tiled=False)
+    kv_own = jnp.transpose(got, (1, 2, 0, 3)).reshape(tok_rows, 2, n_tp * dd)
     key_raw = kv_own[:, 0, :]
     value_own = kv_own[:, 1, :]
     key_rot = rotate(key_raw.astype(jnp.float32)[:, None, :], positions)[:, 0, :].astype(jnp.bfloat16)
+    kv_rows_local = jnp.concatenate([key_rot, value_own], axis=1)
 
-    kv_rows_local = jnp.concatenate([key_rot, value_own], axis=1)
-    kv_rows = lax.all_gather(kv_rows_local, "ctx", axis=0, tiled=True)
-    seq = kv_rows.shape[0]
-
-    window_blocks = min(seq // tok_rows, -(-(DOC_MOST - 1) // tok_rows) + 1)
-    window = window_blocks * tok_rows
-    start_block = jnp.clip(ctx_index - (window_blocks - 1), 0, seq // tok_rows - window_blocks)
-    key_start = start_block * tok_rows
-    kv_win = lax.dynamic_slice_in_dim(kv_rows, key_start, window, 0)
+    n_ctx = lax.axis_size("ctx")
+    back = min(n_ctx - 1, -(-(DOC_MOST - 1) // tok_rows))
+    slots = []
+    for shift in range(back, 0, -1):
+        slots.append(
+            lax.ppermute(kv_rows_local, "ctx", [(i, i + shift) for i in range(n_ctx - shift)])
+        )
+    slots.append(kv_rows_local)
+    kv_win = jnp.concatenate(slots, axis=0)
+    window = kv_win.shape[0]
+    key_start = (ctx_index - back) * tok_rows
     key_win = kv_win[:, :HD]
     value_win = kv_win[:, HD:]
     key_positions = key_start + jnp.arange(window, dtype=jnp.int32)
-    key_docs = doc_of(key_positions, doc_starts)
+    key_docs = jnp.where(key_positions >= 0, doc_of(key_positions, doc_starts), -1)
 
     score_scale = HD ** (-0.5)
     n_split = 2

time: 339 us -> 310 us (0.914)
  waiting for transfers between devices: 272 us -> 214 us
  starting transfers between devices: 0.17 us -> 31 us
    all_gather x2 -> x0, waiting for transfers between devices: 88.1 us -> none  [the longest x1 55.3 us: on_device(): kv_parts = lax.all_gather(kv_local, 'tp', axis=0, tiled=False)]
    ppermute x0 -> x8, waiting for transfers between devices: none -> 27.8 us  [on_device(): lax.ppermute(kv_rows_local, 'ctx', [(i, i + shift) for i in range(n_ctx -...]
    ppermute x0 -> x8, starting transfers between devices: none -> 22 us  [on_device(): lax.ppermute(kv_rows_local, 'ctx', [(i, i + shift) for i in range(n_ctx -...]
    all_to_all x0 -> x1, waiting for transfers between devices: none -> 14.7 us  [on_device(): got = lax.all_to_all(pieces, 'tp', 0, 0, tiled=False)]
    all_gather x1, waiting for transfers between devices: 14.1 us -> 0.02 us  [on_device(): output_full = lax.all_gather(w_output, 'ctx', axis=1, tiled=True)]
    all_to_all x0 -> x1, starting transfers between devices: none -> 8.92 us  [on_device(): got = lax.all_to_all(pieces, 'tp', 0, 0, tiled=False)]
    reduce_scatter x1, waiting for transfers between devices: 122 us -> 126 us  [on_device(): lax.psum_scatter(jnp.dot(attended, output_full, preferred_element_type=jn...]
  transfers between devices with their start and end apart: 5 -> 12, of which waited for: 5 -> 7; matrix products, arithmetic and copies ran while one was open for 9% -> 13% of each run, Pallas kernels for 0% -> 0%
where the time goes in v2:
time: 310 us; the launch traced here: 309 us
  waiting for transfers between devices  214 us (69%)
  matrix products  32.8 us (11%)
  starting transfers between devices  31 us (10%)
  between operations  13.5 us (4%)
  other arithmetic  11.9 us (4%)
  local copies, waits for them, and re-layouts  6.19 us (2%)
    reduce_scatter x1, waiting for transfers between devices, on_device(): lax.psum_scatter(jnp.dot(attended, output_full, preferred_element_type=jn...  126 us
    all_gather x1, waiting for transfers between devices, on_device(): w_full = lax.all_gather(w_all, 'ctx', axis=0, tiled=True)  45.2 us
    ppermute x8, waiting for transfers between devices, on_device(): lax.ppermute(kv_rows_local, 'ctx', [(i, i + shift) for i in range(n_ctx -...  27.8 us
    ppermute x8, starting transfers between devices, on_device(): lax.ppermute(kv_rows_local, 'ctx', [(i, i + shift) for i in range(n_ctx -...  22 us
    all_to_all x1, waiting for transfers between devices, on_device(): got = lax.all_to_all(pieces, 'tp', 0, 0, tiled=False)  14.7 us
    all_to_all x1, starting transfers between devices, on_device(): got = lax.all_to_all(pieces, 'tp', 0, 0, tiled=False)  8.92 us
    dot_general x4, matrix products, one_part(): jnp.dot(q_part, key_win.T, preferred_element_type=jnp.float32) * score_scale  8.79 us
    dot_general x4, matrix products, one_part(): jnp.dot(expo.astype(jnp.bfloat16), value_win, preferred_element_type=jnp....  8.37 us
  transfers between devices with their start and end apart: 12, of which 7 were waited for; matrix products, arithmetic and copies ran while one was open for 13% of the time, Pallas kernels for 0%

profile of v2, /device:TPU:6, one launch (start us, length us, event | category | flops | bytes accessed | tf_op | source)
XLA Modules:
  0.0 309.5 jit_solution(6007037738465411206)
XLA Ops:
  12.7 45.2 %all-gather.3.cloned.1.call-done = bf16[8192,320]{1,0:T(8,128)(2,1)} async-done(((bf16[512,320]{1,0:T(8,128)(2,1)}), bf16[8192,320]{1,0:T(8,128)(2,1)}) %all-gather.3.cloned.1.call-update) | async-done | bytes 5242896 | tf_op jit(solution)/shard_map/all_gather | solution.py:48
  57.9 7.8 %convolution_bitcast_fusion = f32[512,320]{0,1:T(8,128)S(1)} fusion(bf16[8192,320]{1,0:T(8,128)(2,1)} %all-gather.3.cloned.1.call-done, bf16[512,8192]{1,0:T(8,128)(2,1)} %param.8), kind=kOutput, calls=%fused_computation.21 | convolution fusion | flops 2684354560 | bytes 14286848 | tf_op jit(solution)/shard_map/dot_general | solution.py:49
  67.2 8.9 %all-to-all-start = ((bf16[16,512,2,8]{1,3,2,0:T(8,128)(2,1)}), bf16[16,512,2,8]{1,3,2,0:T(8,128)(2,1)S(1)}, u32[]{:S(2)}, u32[]{:S(2)}) async-start(bf16[16,512,2,8]{1,3,2,0:T(8,128)(2,1)} %broadcast_select_fusion), calls=%async_computation | async-start | bytes 524288 | tf_op jit(solution)/shard_map/all_to_all | solution.py:62
  77.4 14.7 %all-to-all-done = bf16[16,512,2,8]{1,3,2,0:T(8,128)(2,1)S(1)} async-done(((bf16[16,512,2,8]{1,3,2,0:T(8,128)(2,1)}), bf16[16,512,2,8]{1,3,2,0:T(8,128)(2,1)S(1)}, u32[]{:S(2)}, u32[]{:S(2)}) %all-to-all-start) | async-done | bytes 262176 | tf_op jit(solution)/shard_map/all_to_all | solution.py:62
  96.1 1.9 collective-permute-start.2
  98.9 2.0 collective-permute-start.7
  101.0 3.8 %collective-permute-start.6 = (bf16[512,256]{0,1:T(8,128)(2,1)S(1)}, bf16[512,256]{0,1:T(8,128)(2,1)S(1)}, u32[]{:S(2)}, u32[]{:S(2)}) collective-permute-start(bf16[512,256]{0,1:T(8,128)(2,1)S(1)} %pad_maximum_fusion.1), channel_id=1, source_target_pairs={{0,32},{16,48},{32,64},{48,80},{64,96},{80,112},{96,128},{112,144}... | collective-permute-start | bytes 786440 | tf_op jit(solution)/shard_map/ppermute | solution.py:74
  104.8 4.7 %collective-permute-done = bf16[512,256]{0,1:T(8,128)(2,1)S(1)} collective-permute-done((bf16[512,256]{0,1:T(8,128)(2,1)S(1)}, bf16[512,256]{0,1:T(8,128)(2,1)S(1)}, u32[]{:S(2)}, u32[]{:S(2)}) %collective-permute-start) | collective-permute-done | bytes 262176 | tf_op jit(solution)/shard_map/ppermute | solution.py:74
  111.5 7.1 %collective-permute-start.4 = (bf16[512,256]{0,1:T(8,128)(2,1)S(1)}, bf16[512,256]{0,1:T(8,128)(2,1)S(1)}, u32[]{:S(2)}, u32[]{:S(2)}) collective-permute-start(bf16[512,256]{0,1:T(8,128)(2,1)S(1)} %pad_maximum_fusion.1), channel_id=1, source_target_pairs={{0,64},{16,80},{32,96},{48,112},{64,128},{80,144},{96,160},{112,17... | collective-permute-start | bytes 786440 | tf_op jit(solution)/shard_map/ppermute | solution.py:74
  118.6 2.1 collective-permute-start.5
  120.7 11.8 %collective-permute-done.3 = bf16[512,256]{0,1:T(8,128)(2,1)S(1)} collective-permute-done((bf16[512,256]{0,1:T(8,128)(2,1)S(1)}, bf16[512,256]{0,1:T(8,128)(2,1)S(1)}, u32[]{:S(2)}, u32[]{:S(2)}) %collective-permute-start.3) | collective-permute-done | bytes 262176 | tf_op jit(solution)/shard_map/ppermute | solution.py:74
  132.6 5.6 %collective-permute-done.4 = bf16[512,256]{0,1:T(8,128)(2,1)S(1)} collective-permute-done((bf16[512,256]{0,1:T(8,128)(2,1)S(1)}, bf16[512,256]{0,1:T(8,128)(2,1)S(1)}, u32[]{:S(2)}, u32[]{:S(2)}) %collective-permute-start.4) | collective-permute-done | bytes 262176 | tf_op jit(solution)/shard_map/ppermute | solution.py:74
  138.2 5.6 %collective-permute-done.5 = bf16[512,256]{0,1:T(8,128)(2,1)S(1)} collective-permute-done((bf16[512,256]{0,1:T(8,128)(2,1)S(1)}, bf16[512,256]{0,1:T(8,128)(2,1)S(1)}, u32[]{:S(2)}, u32[]{:S(2)}) %collective-permute-start.5) | collective-permute-done | bytes 262176 | tf_op jit(solution)/shard_map/ppermute | solution.py:74
  145.6 23.0 %while.11 = (s32[]{:T(128)}, bf16[4,256,128]{2,1,0:T(8,128)(2,1)}, s32[4,256]{1,0:T(4,128)S(1)}, s32[4608]{0:T(1024)}, s32[4,256]{1,0:T(4,128)S(1)}, /*index=5*/...) while((s32[]{:T(128)}, bf16[4,256,128]{2,1,0:T(8,128)(2,1)}, ...), condition=%wide.region_6.7_spmd.clone, body=%wide.region_3.6_spmd.clone.sunk | while | flops 625283072 | bytes 16866456 | solution.py:103
  145.6 2.2 fusion.51
  149.2 2.1 fusion.53
  151.3 2.2 fusion.51
  155.0 2.1 fusion.53
  157.1 2.2 fusion.51
  160.7 2.1 fusion.53
  162.8 2.2 fusion.51
  166.4 2.1 fusion.53
  169.6 7.8 %convolution_convert_fusion = bf16[512,8192]{1,0:T(8,128)(2,1)} fusion(bf16[512,256]{0,1:T(8,128)(2,1)S(1)} %bitcast.56, bf16[256,8192]{1,0:T(8,128)(2,1)} %all-gather.5.cloned.1.call-done), kind=kOutput, calls=%fused_computation.20 | convolution fusion | flops 2151677952 | bytes 12845056 | tf_op jit(solution)/shard_map/dot_general | solution.py:109
  177.5 125.5 %reduce-scatter.2.cloned.1.call-done = bf16[32,8192]{1,0:T(8,128)(2,1)} async-done(((bf16[512,8192]{1,0:T(8,128)(2,1)}), bf16[32,8192]{1,0:T(8,128)(2,1)}) %reduce-scatter.2.cloned.1.call-update) | async-done | bytes 524304 | tf_op jit(solution)/shard_map/reduce_scatter | solution.py:108
  (86 shorter events, 24.0 us)
Async XLA Ops:
  6.5 51.4 %all-gather.3.cloned.1.call-start = ((), (), s32[]{:S(2)}) async-start(), calls=%async_computation.2 | async-start | bytes 6684672 | tf_op jit(solution)/shard_map/all_gather | solution.py:48
  10.1 159.5 %all-gather.5.cloned.1.call-start = ((), (), s32[]{:S(2)}) async-start(), calls=%async_computation.3 | async-start | bytes 4456448 | tf_op jit(solution)/shard_map/all_gather | solution.py:107
  65.8 11.6 %copy-start = (f32[512,320]{0,1:T(8,128)}, f32[512,320]{0,1:T(8,128)S(1)}, u32[]{:S(2)}) copy-start(f32[512,320]{0,1:T(8,128)S(1)} %convolution_bitcast_fusion) | copy-start | bytes 1966084
  67.2 25.0 %all-to-all-start = ((bf16[16,512,2,8]{1,3,2,0:T(8,128)(2,1)}), bf16[16,512,2,8]{1,3,2,0:T(8,128)(2,1)S(1)}, u32[]{:S(2)}, u32[]{:S(2)}) async-start(bf16[16,512,2,8]{1,3,2,0:T(8,128)(2,1)} %broadcast_select_fusion), calls=%async_computation | async-start | bytes 524288 | tf_op jit(solution)/shard_map/all_to_all | solution.py:62
  76.1 226.8 %reduce-scatter.2.cloned.1.call-start = ((), (), s32[]{:S(2)}) async-start(), calls=%async_computation.4 | async-start | bytes 8912896 | tf_op jit(solution)/shard_map/reduce_scatter | solution.py:108
  77.4 18.6 %slice-start = ((f32[512,320]{0,1:T(8,128)}), f32[512,256]{0,1:T(8,128)S(1)}, s32[]{:S(2)}) async-start(f32[512,320]{0,1:T(8,128)} %copy-done), calls=%async_computation.5 | async-start | bytes 1048576 | tf_op jit(solution)/shard_map/slice | solution.py:50
  92.8 18.6 %collective-permute-start.1 = (bf16[512,256]{0,1:T(8,128)(2,1)S(1)}, bf16[512,256]{0,1:T(8,128)(2,1)S(1)}, u32[]{:S(2)}, u32[]{:S(2)}) collective-permute-start(bf16[512,256]{0,1:T(8,128)(2,1)S(1)} %pad_maximum_fusion.1), channel_id=1, source_target_pairs={{0,112},{16,128},{32,144},{48,160},{64,176},{80,192},{96,208},{112... | collective-permute-start | bytes 786440 | tf_op jit(solution)/shard_map/ppermute | solution.py:74
  94.2 15.4 %collective-permute-start = (bf16[512,256]{0,1:T(8,128)(2,1)S(1)}, bf16[512,256]{0,1:T(8,128)(2,1)S(1)}, u32[]{:S(2)}, u32[]{:S(2)}) collective-permute-start(bf16[512,256]{0,1:T(8,128)(2,1)S(1)} %pad_maximum_fusion.1), channel_id=1, source_target_pairs={{0,128},{16,144},{32,160},{48,176},{64,192},{80,208},{96,224},{112... | collective-permute-start | bytes 786440 | tf_op jit(solution)/shard_map/ppermute | solution.py:74
  96.1 22.4 %collective-permute-start.2 = (bf16[512,256]{0,1:T(8,128)(2,1)S(1)}, bf16[512,256]{0,1:T(8,128)(2,1)S(1)}, u32[]{:S(2)}, u32[]{:S(2)}) collective-permute-start(bf16[512,256]{0,1:T(8,128)(2,1)S(1)} %pad_maximum_fusion.1), channel_id=1, source_target_pairs={{0,96},{16,112},{32,128},{48,144},{64,160},{80,176},{96,192},{112,... | collective-permute-start | bytes 786440 | tf_op jit(solution)/shard_map/ppermute | solution.py:74
  98.9 44.9 %collective-permute-start.7 = (bf16[512,256]{0,1:T(8,128)(2,1)S(1)}, bf16[512,256]{0,1:T(8,128)(2,1)S(1)}, u32[]{:S(2)}, u32[]{:S(2)}) collective-permute-start(bf16[512,256]{0,1:T(8,128)(2,1)S(1)} %pad_maximum_fusion.1), channel_id=1, source_target_pairs={{0,16},{16,32},{32,48},{48,64},{64,80},{80,96},{96,112},{112,128},... | collective-permute-start | bytes 786440 | tf_op jit(solution)/shard_map/ppermute | solution.py:74
  101.0 42.9 %collective-permute-start.6 = (bf16[512,256]{0,1:T(8,128)(2,1)S(1)}, bf16[512,256]{0,1:T(8,128)(2,1)S(1)}, u32[]{:S(2)}, u32[]{:S(2)}) collective-permute-start(bf16[512,256]{0,1:T(8,128)(2,1)S(1)} %pad_maximum_fusion.1), channel_id=1, source_target_pairs={{0,32},{16,48},{32,64},{48,80},{64,96},{80,112},{96,128},{112,144}... | collective-permute-start | bytes 786440 | tf_op jit(solution)/shard_map/ppermute | solution.py:74
  109.5 23.0 %collective-permute-start.3 = (bf16[512,256]{0,1:T(8,128)(2,1)S(1)}, bf16[512,256]{0,1:T(8,128)(2,1)S(1)}, u32[]{:S(2)}, u32[]{:S(2)}) collective-permute-start(bf16[512,256]{0,1:T(8,128)(2,1)S(1)} %pad_maximum_fusion.1), channel_id=1, source_target_pairs={{0,80},{16,96},{32,112},{48,128},{64,144},{80,160},{96,176},{112,1... | collective-permute-start | bytes 786440 | tf_op jit(solution)/shard_map/ppermute | solution.py:74
  111.5 26.7 %collective-permute-start.4 = (bf16[512,256]{0,1:T(8,128)(2,1)S(1)}, bf16[512,256]{0,1:T(8,128)(2,1)S(1)}, u32[]{:S(2)}, u32[]{:S(2)}) collective-permute-start(bf16[512,256]{0,1:T(8,128)(2,1)S(1)} %pad_maximum_fusion.1), channel_id=1, source_target_pairs={{0,64},{16,80},{32,96},{48,112},{64,128},{80,144},{96,160},{112,17... | collective-permute-start | bytes 786440 | tf_op jit(solution)/shard_map/ppermute | solution.py:74
  118.6 25.2 %collective-permute-start.5 = (bf16[512,256]{0,1:T(8,128)(2,1)S(1)}, bf16[512,256]{0,1:T(8,128)(2,1)S(1)}, u32[]{:S(2)}, u32[]{:S(2)}) collective-permute-start(bf16[512,256]{0,1:T(8,128)(2,1)S(1)} %pad_maximum_fusion.1), channel_id=1, source_target_pairs={{0,48},{16,64},{32,80},{48,96},{64,112},{80,128},{96,144},{112,160... | collective-permute-start | bytes 786440 | tf_op jit(solution)/shard_map/ppermute | solution.py:74
  145.6 2.2 copy-start.1
  151.3 2.2 copy-start.1
  157.1 2.2 copy-start.1
  162.8 2.2 copy-start.1
Sparse Core Ops, SparseCore 0:
  10.3 47.6 all-gather.2
  59.7 45.4 all-gather.4
  177.6 125.3 reduce-scatter.1

commit v3 on v2

--- a/solution.py
+++ b/solution.py
@@ -104,13 +104,20 @@
     attended = attended.reshape(heads_dev, tok_rows, HD)
     attended = jnp.transpose(attended, (1, 0, 2)).reshape(tok_rows, heads_dev * HD)
 
-    output_full = lax.all_gather(w_output, "ctx", axis=1, tiled=True)
-    return lax.psum_scatter(
-        jnp.dot(attended, output_full, preferred_element_type=jnp.float32).astype(jnp.bfloat16),
-        "tp",
-        scatter_dimension=0,
-        tiled=True,
+    n_ctx_all = lax.axis_size("ctx")
+    w_moved = lax.ppermute(
+        w_output,
+        ("ctx", "tp"),
+        [(c * n_tp + t, t * n_tp + c) for c in range(n_ctx_all) for t in range(n_tp)],
     )
+    w_chunk = lax.all_gather(w_moved, "ctx", axis=0, tiled=True)
+    attended_all = lax.all_gather(attended, "tp", axis=1, tiled=True)
+    out_chunk = jnp.dot(attended_all, w_chunk, preferred_element_type=jnp.float32).astype(jnp.bfloat16)
+    chunk = out_chunk.shape[1]
+    out_rows = tok_rows // n_tp
+    sent = out_chunk.reshape(n_tp, out_rows, chunk)
+    got_rows = lax.all_to_all(sent, "tp", 0, 0, tiled=False)
+    return jnp.transpose(got_rows, (1, 0, 2)).reshape(out_rows, n_tp * chunk)
 
 
 def solution(mesh):

time: 310 us -> 299 us (0.965)
  waiting for transfers between devices: 214 us -> 175 us
  blocking collectives: 0 us -> 25.5 us
    reduce_scatter x1 -> x0, waiting for transfers between devices: 126 us -> none  [on_device(): lax.psum_scatter(jnp.dot(attended, output_full, preferred_element_type=jn...]
    all_gather x1 -> x2, waiting for transfers between devices: 0.02 us -> 74.6 us  [the longest x1 74.5 us: on_device(): attended_all = lax.all_gather(attended, 'tp', axis=1, tiled=True)]
    all_to_all x0 -> x1, blocking collectives: none -> 25.5 us  [on_device(): got_rows = lax.all_to_all(sent, 'tp', 0, 0, tiled=False)]
    ppermute x8, waiting for transfers between devices: 27.8 us -> 45.8 us  [on_device(): lax.ppermute(kv_rows_local, 'ctx', [(i, i + shift) for i in range(n_ctx -...]
    ppermute x0 -> x1, starting transfers between devices: none -> 7.73 us  [on_device(): lax.ppermute(w_output, ('ctx', 'tp'), [(c * n_tp + t, t * n_tp + c) for c...]
    ppermute x8, starting transfers between devices: 22 us -> 14.6 us  [on_device(): lax.ppermute(kv_rows_local, 'ctx', [(i, i + shift) for i in range(n_ctx -...]
    all_to_all x1, waiting for transfers between devices: 14.7 us -> 11.3 us  [on_device(): got = lax.all_to_all(pieces, 'tp', 0, 0, tiled=False)]
  transfers between devices with their start and end apart: 12 -> 13, of which waited for: 7 -> 10; matrix products, arithmetic and copies ran while one was open for 13% -> 14% of each run, Pallas kernels for 0% -> 0%
where the time goes in v3:
time: 299 us; the launch traced here: 298 us
  waiting for transfers between devices  175 us (59%)
  starting transfers between devices  32.1 us (11%)
  matrix products  30.8 us (10%)
  blocking collectives  25.5 us (9%)
  between operations  13.5 us (5%)
  other arithmetic  11.9 us (4%)
  local copies, waits for them, and re-layouts  8.45 us (3%)
    all_gather x1, waiting for transfers between devices, on_device(): attended_all = lax.all_gather(attended, 'tp', axis=1, tiled=True)  74.5 us
    ppermute x8, waiting for transfers between devices, on_device(): lax.ppermute(kv_rows_local, 'ctx', [(i, i + shift) for i in range(n_ctx -...  45.8 us
    all_gather x1, waiting for transfers between devices, on_device(): w_full = lax.all_gather(w_all, 'ctx', axis=0, tiled=True)  43.5 us
    all_to_all x1, blocking collectives, on_device(): got_rows = lax.all_to_all(sent, 'tp', 0, 0, tiled=False)  25.5 us
    ppermute x8, starting transfers between devices, on_device(): lax.ppermute(kv_rows_local, 'ctx', [(i, i + shift) for i in range(n_ctx -...  14.6 us
    all_to_all x1, waiting for transfers between devices, on_device(): got = lax.all_to_all(pieces, 'tp', 0, 0, tiled=False)  11.3 us
    all_to_all x1, starting transfers between devices, on_device(): got = lax.all_to_all(pieces, 'tp', 0, 0, tiled=False)  9.73 us
    dot_general x4, matrix products, one_part(): jnp.dot(q_part, key_win.T, preferred_element_type=jnp.float32) * score_scale  8.8 us
  transfers between devices with their start and end apart: 13, of which 10 were waited for; matrix products, arithmetic and copies ran while one was open for 14% of the time, Pallas kernels for 0%

profile of v3, /device:TPU:6, one launch (start us, length us, event | category | flops | bytes accessed | tf_op | source)
XLA Modules:
  0.0 297.7 jit_solution(6567654846643146191)
XLA Ops:
  10.1 7.7 %collective-permute-start.8 = (bf16[256,512]{1,0:T(8,128)(2,1)}, bf16[256,512]{1,0:T(8,128)(2,1)S(1)}, u32[]{:S(2)}, u32[]{:S(2)}) collective-permute-start(bf16[256,512]{1,0:T(8,128)(2,1)} %param.13), channel_id=1, source_target_pairs={{0,0},{1,16},{2,32},{3,48},{4,64},{5,80},{6,96},{7,112},{8,128},{9... | collective-permute-start | bytes 786440 | tf_op jit(solution)/shard_map/ppermute | solution.py:108
  20.2 43.5 %all-gather.4.cloned.1.call-done = bf16[8192,320]{1,0:T(8,128)(2,1)} async-done(((bf16[512,320]{1,0:T(8,128)(2,1)}), bf16[8192,320]{1,0:T(8,128)(2,1)}) %all-gather.4.cloned.1.call-update) | async-done | bytes 5242896 | tf_op jit(solution)/shard_map/all_gather | solution.py:48
  63.6 7.8 %convolution_bitcast_fusion = f32[512,320]{0,1:T(8,128)S(1)} fusion(bf16[8192,320]{1,0:T(8,128)(2,1)} %all-gather.4.cloned.1.call-done, bf16[512,8192]{1,0:T(8,128)(2,1)} %param.8), kind=kOutput, calls=%fused_computation.21 | convolution fusion | flops 2684354560 | bytes 14286848 | tf_op jit(solution)/shard_map/dot_general | solution.py:49
  72.9 9.7 %all-to-all-start = ((bf16[16,512,2,8]{1,3,2,0:T(8,128)(2,1)}), bf16[16,512,2,8]{1,3,2,0:T(8,128)(2,1)S(1)}, u32[]{:S(2)}, u32[]{:S(2)}) async-start(bf16[16,512,2,8]{1,3,2,0:T(8,128)(2,1)} %broadcast_select_fusion), calls=%async_computation | async-start | bytes 524288 | tf_op jit(solution)/shard_map/all_to_all | solution.py:62
  84.2 11.3 %all-to-all-done = bf16[16,512,2,8]{1,3,2,0:T(8,128)(2,1)S(1)} async-done(((bf16[16,512,2,8]{1,3,2,0:T(8,128)(2,1)}), bf16[16,512,2,8]{1,3,2,0:T(8,128)(2,1)S(1)}, u32[]{:S(2)}, u32[]{:S(2)}) %all-to-all-start) | async-done | bytes 262176 | tf_op jit(solution)/shard_map/all_to_all | solution.py:62
  106.1 3.5 %collective-permute-done = bf16[512,256]{0,1:T(8,128)(2,1)S(1)} collective-permute-done((bf16[512,256]{0,1:T(8,128)(2,1)S(1)}, bf16[512,256]{0,1:T(8,128)(2,1)S(1)}, u32[]{:S(2)}, u32[]{:S(2)}) %collective-permute-start) | collective-permute-done | bytes 262176 | tf_op jit(solution)/shard_map/ppermute | solution.py:74
  111.6 9.3 %collective-permute-done.1 = bf16[512,256]{0,1:T(8,128)(2,1)S(1)} collective-permute-done((bf16[512,256]{0,1:T(8,128)(2,1)S(1)}, bf16[512,256]{0,1:T(8,128)(2,1)S(1)}, u32[]{:S(2)}, u32[]{:S(2)}) %collective-permute-start.1) | collective-permute-done | bytes 262176 | tf_op jit(solution)/shard_map/ppermute | solution.py:74
  122.9 9.2 %collective-permute-done.2 = bf16[512,256]{0,1:T(8,128)(2,1)S(1)} collective-permute-done((bf16[512,256]{0,1:T(8,128)(2,1)S(1)}, bf16[512,256]{0,1:T(8,128)(2,1)S(1)}, u32[]{:S(2)}, u32[]{:S(2)}) %collective-permute-start.2) | collective-permute-done | bytes 262176 | tf_op jit(solution)/shard_map/ppermute | solution.py:74
  134.0 6.3 %collective-permute-done.3 = bf16[512,256]{0,1:T(8,128)(2,1)S(1)} collective-permute-done((bf16[512,256]{0,1:T(8,128)(2,1)S(1)}, bf16[512,256]{0,1:T(8,128)(2,1)S(1)}, u32[]{:S(2)}, u32[]{:S(2)}) %collective-permute-start.3) | collective-permute-done | bytes 262176 | tf_op jit(solution)/shard_map/ppermute | solution.py:74
  140.3 6.3 %collective-permute-done.4 = bf16[512,256]{0,1:T(8,128)(2,1)S(1)} collective-permute-done((bf16[512,256]{0,1:T(8,128)(2,1)S(1)}, bf16[512,256]{0,1:T(8,128)(2,1)S(1)}, u32[]{:S(2)}, u32[]{:S(2)}) %collective-permute-start.4) | collective-permute-done | bytes 262176 | tf_op jit(solution)/shard_map/ppermute | solution.py:74
  146.6 5.6 %collective-permute-done.5 = bf16[512,256]{0,1:T(8,128)(2,1)S(1)} collective-permute-done((bf16[512,256]{0,1:T(8,128)(2,1)S(1)}, bf16[512,256]{0,1:T(8,128)(2,1)S(1)}, u32[]{:S(2)}, u32[]{:S(2)}) %collective-permute-start.5) | collective-permute-done | bytes 262176 | tf_op jit(solution)/shard_map/ppermute | solution.py:74
  152.3 5.6 %collective-permute-done.6 = bf16[512,256]{0,1:T(8,128)(2,1)S(1)} collective-permute-done((bf16[512,256]{0,1:T(8,128)(2,1)S(1)}, bf16[512,256]{0,1:T(8,128)(2,1)S(1)}, u32[]{:S(2)}, u32[]{:S(2)}) %collective-permute-start.6) | collective-permute-done | bytes 262176 | tf_op jit(solution)/shard_map/ppermute | solution.py:74
  159.6 23.0 %while.11 = (s32[]{:T(128)}, bf16[4,256,128]{2,1,0:T(8,128)(2,1)}, s32[4,256]{1,0:T(4,128)S(1)}, s32[4608]{0:T(1024)}, s32[4,256]{1,0:T(4,128)S(1)}, /*index=5*/...) while((s32[]{:T(128)}, bf16[4,256,128]{2,1,0:T(8,128)(2,1)}, ...), condition=%wide.region_6.7_spmd.clone, body=%wide.region_3.6_spmd.clone.sunk | while | flops 625283072 | bytes 16867464 | solution.py:103
  159.6 2.2 fusion.51
  163.2 2.1 fusion.53
  165.4 2.2 fusion.51
  169.0 2.1 fusion.53
  171.1 2.2 fusion.51
  174.7 2.1 fusion.53
  176.8 2.2 fusion.51
  180.5 2.1 fusion.53
  184.4 74.5 %all-gather.6.cloned.1.call-done = bf16[512,4096]{0,1:T(8,128)(2,1)} async-done(((bf16[512,256]{0,1:T(8,128)(2,1)}), bf16[512,4096]{0,1:T(8,128)(2,1)}) %all-gather.6.cloned.1.call-update) | async-done | bytes 4194320 | tf_op jit(solution)/shard_map/all_gather | solution.py:114
  258.9 5.8 %convolution_convert_fusion = bf16[512,512]{1,0:T(8,128)(2,1)S(1)} fusion(bf16[512,4096]{0,1:T(8,128)(2,1)} %all-gather.6.cloned.1.call-done, bf16[4096,512]{1,0:T(8,128)(2,1)} %all-gather.8.cloned.1.call-done), kind=kOutput, calls=%fused_computation.20 | convolution fusion | flops 2147745792 | bytes 8912896 | tf_op jit(solution)/shard_map/dot_general | solution.py:115
  264.8 25.5 %all_to_all.10 = bf16[16,32,512]{2,1,0:T(8,128)(2,1)S(1)} all-to-all(bf16[16,32,512]{2,1,0:T(8,128)(2,1)S(1)} %bitcast.62), channel_id=1, replica_groups=mesh['ctx'=16,'tp'=16] {'tp'}, dimensions={0} | all-to-all | bytes 1048576 | tf_op jit(solution)/shard_map/all_to_all | solution.py:119
  (92 shorter events, 35.1 us)
Async XLA Ops:
  6.5 57.1 %all-gather.4.cloned.1.call-start = ((), (), s32[]{:S(2)}) async-start(), calls=%async_computation.2 | async-start | bytes 6684672 | tf_op jit(solution)/shard_map/all_gather | solution.py:48
  10.1 73.3 %collective-permute-start.8 = (bf16[256,512]{1,0:T(8,128)(2,1)}, bf16[256,512]{1,0:T(8,128)(2,1)S(1)}, u32[]{:S(2)}, u32[]{:S(2)}) collective-permute-start(bf16[256,512]{1,0:T(8,128)(2,1)} %param.13), channel_id=1, source_target_pairs={{0,0},{1,16},{2,32},{3,48},{4,64},{5,80},{6,96},{7,112},{8,128},{9... | collective-permute-start | bytes 786440 | tf_op jit(solution)/shard_map/ppermute | solution.py:108
  71.5 12.7 %copy-start = (f32[512,320]{0,1:T(8,128)}, f32[512,320]{0,1:T(8,128)S(1)}, u32[]{:S(2)}) copy-start(f32[512,320]{0,1:T(8,128)S(1)} %convolution_bitcast_fusion) | copy-start | bytes 1966084
  72.9 22.6 %all-to-all-start = ((bf16[16,512,2,8]{1,3,2,0:T(8,128)(2,1)}), bf16[16,512,2,8]{1,3,2,0:T(8,128)(2,1)S(1)}, u32[]{:S(2)}, u32[]{:S(2)}) async-start(bf16[16,512,2,8]{1,3,2,0:T(8,128)(2,1)} %broadcast_select_fusion), calls=%async_computation | async-start | bytes 524288 | tf_op jit(solution)/shard_map/all_to_all | solution.py:62
  82.7 101.7 %all-gather.8.cloned.1.call-start = ((), (), s32[]{:S(2)}) async-start(), calls=%async_computation.4 | async-start | bytes 4456448 | tf_op jit(solution)/shard_map/all_gather | solution.py:113
  83.4 0.7 copy-start.2
  84.2 174.8 %all-gather.6.cloned.1.call-start = ((), (), s32[]{:S(2)}) async-start(), calls=%async_computation.3 | async-start | bytes 4456448 | tf_op jit(solution)/shard_map/all_gather | solution.py:114
  84.2 15.1 %slice-start = ((f32[512,320]{0,1:T(8,128)}), f32[512,256]{0,1:T(8,128)S(1)}, s32[]{:S(2)}) async-start(f32[512,320]{0,1:T(8,128)} %copy-done), calls=%async_computation.5 | async-start | bytes 1048576 | tf_op jit(solution)/shard_map/slice | solution.py:50
  96.2 13.4 %collective-permute-start = (bf16[512,256]{0,1:T(8,128)(2,1)S(1)}, bf16[512,256]{0,1:T(8,128)(2,1)S(1)}, u32[]{:S(2)}, u32[]{:S(2)}) collective-permute-start(bf16[512,256]{0,1:T(8,128)(2,1)S(1)} %pad_maximum_fusion.1), channel_id=1, source_target_pairs={{0,128},{16,144},{32,160},{48,176},{64,192},{80,208},{96,224},{112... | collective-permute-start | bytes 786440 | tf_op jit(solution)/shard_map/ppermute | solution.py:74
  98.1 22.8 %collective-permute-start.1 = (bf16[512,256]{0,1:T(8,128)(2,1)S(1)}, bf16[512,256]{0,1:T(8,128)(2,1)S(1)}, u32[]{:S(2)}, u32[]{:S(2)}) collective-permute-start(bf16[512,256]{0,1:T(8,128)(2,1)S(1)} %pad_maximum_fusion.1), channel_id=1, source_target_pairs={{0,112},{16,128},{32,144},{48,160},{64,176},{80,192},{96,208},{112... | collective-permute-start | bytes 786440 | tf_op jit(solution)/shard_map/ppermute | solution.py:74
  99.5 32.6 %collective-permute-start.2 = (bf16[512,256]{0,1:T(8,128)(2,1)S(1)}, bf16[512,256]{0,1:T(8,128)(2,1)S(1)}, u32[]{:S(2)}, u32[]{:S(2)}) collective-permute-start(bf16[512,256]{0,1:T(8,128)(2,1)S(1)} %pad_maximum_fusion.1), channel_id=1, source_target_pairs={{0,96},{16,112},{32,128},{48,144},{64,160},{80,176},{96,192},{112,... | collective-permute-start | bytes 786440 | tf_op jit(solution)/shard_map/ppermute | solution.py:74
  102.3 38.0 %collective-permute-start.3 = (bf16[512,256]{0,1:T(8,128)(2,1)S(1)}, bf16[512,256]{0,1:T(8,128)(2,1)S(1)}, u32[]{:S(2)}, u32[]{:S(2)}) collective-permute-start(bf16[512,256]{0,1:T(8,128)(2,1)S(1)} %pad_maximum_fusion.1), channel_id=1, source_target_pairs={{0,80},{16,96},{32,112},{48,128},{64,144},{80,160},{96,176},{112,1... | collective-permute-start | bytes 786440 | tf_op jit(solution)/shard_map/ppermute | solution.py:74
  104.2 42.4 %collective-permute-start.4 = (bf16[512,256]{0,1:T(8,128)(2,1)S(1)}, bf16[512,256]{0,1:T(8,128)(2,1)S(1)}, u32[]{:S(2)}, u32[]{:S(2)}) collective-permute-start(bf16[512,256]{0,1:T(8,128)(2,1)S(1)} %pad_maximum_fusion.1), channel_id=1, source_target_pairs={{0,64},{16,80},{32,96},{48,112},{64,128},{80,144},{96,160},{112,17... | collective-permute-start | bytes 786440 | tf_op jit(solution)/shard_map/ppermute | solution.py:74
  109.7 42.6 %collective-permute-start.5 = (bf16[512,256]{0,1:T(8,128)(2,1)S(1)}, bf16[512,256]{0,1:T(8,128)(2,1)S(1)}, u32[]{:S(2)}, u32[]{:S(2)}) collective-permute-start(bf16[512,256]{0,1:T(8,128)(2,1)S(1)} %pad_maximum_fusion.1), channel_id=1, source_target_pairs={{0,48},{16,64},{32,80},{48,96},{64,112},{80,128},{96,144},{112,160... | collective-permute-start | bytes 786440 | tf_op jit(solution)/shard_map/ppermute | solution.py:74
  120.9 36.9 %collective-permute-start.6 = (bf16[512,256]{0,1:T(8,128)(2,1)S(1)}, bf16[512,256]{0,1:T(8,128)(2,1)S(1)}, u32[]{:S(2)}, u32[]{:S(2)}) collective-permute-start(bf16[512,256]{0,1:T(8,128)(2,1)S(1)} %pad_maximum_fusion.1), channel_id=1, source_target_pairs={{0,32},{16,48},{32,64},{48,80},{64,96},{80,112},{96,128},{112,144}... | collective-permute-start | bytes 786440 | tf_op jit(solution)/shard_map/ppermute | solution.py:74
  132.1 25.8 %collective-permute-start.7 = (bf16[512,256]{0,1:T(8,128)(2,1)S(1)}, bf16[512,256]{0,1:T(8,128)(2,1)S(1)}, u32[]{:S(2)}, u32[]{:S(2)}) collective-permute-start(bf16[512,256]{0,1:T(8,128)(2,1)S(1)} %pad_maximum_fusion.1), channel_id=1, source_target_pairs={{0,16},{16,32},{32,48},{48,64},{64,80},{80,96},{96,112},{112,128},... | collective-permute-start | bytes 786440 | tf_op jit(solution)/shard_map/ppermute | solution.py:74
  159.6 2.2 copy-start.1
  165.3 2.2 copy-start.1
  171.1 2.2 copy-start.1
  176.8 2.2 copy-start.1
Sparse Core Ops, SparseCore 0:
  10.3 53.3 all-gather.3
  85.3 61.8 all-gather.7
  184.5 74.3 all-gather.5

commit v4 on v3

--- a/solution.py
+++ b/solution.py
@@ -44,11 +44,11 @@
 
     q_cols = w_query.shape[1]
     k_cols = w_key.shape[1]
-    w_all = jnp.concatenate([w_query, w_key, w_value], axis=1)
-    w_full = lax.all_gather(w_all, "ctx", axis=0, tiled=True)
-    proj = jnp.dot(tokens, w_full, preferred_element_type=jnp.float32)
-    query_sum = proj[:, :q_cols]
-    kv_local = proj[:, q_cols:].astype(jnp.bfloat16)
+    w_kv = jnp.concatenate([w_key, w_value], axis=1)
+    w_kv_full = lax.all_gather(w_kv, "ctx", axis=0, tiled=True)
+    kv_local = jnp.dot(tokens, w_kv_full, preferred_element_type=jnp.float32).astype(jnp.bfloat16)
+    w_q_full = lax.all_gather(w_query, "ctx", axis=0, tiled=True)
+    query_sum = jnp.dot(tokens, w_q_full, preferred_element_type=jnp.float32)
 
     heads_dev = q_cols // HD
     query = rotate(query_sum.reshape(tok_rows, heads_dev, HD), positions).astype(jnp.bfloat16)

time: 299 us -> 285 us (0.953)
  waiting for transfers between devices: 175 us -> 164 us
  local copies, waits for them, and re-layouts: 8.45 us -> 5.06 us
    ppermute x8, waiting for transfers between devices: 45.8 us -> 32.1 us  [on_device(): lax.ppermute(kv_rows_local, 'ctx', [(i, i + shift) for i in range(n_ctx -...]
    all_gather x1 -> x2, waiting for transfers between devices: 43.5 us -> 33.7 us  [the longest x1 33.6 us: on_device(): w_kv_full = lax.all_gather(w_kv, 'ctx', axis=0, tiled=True)]
    all_gather x1, waiting for transfers between devices: 74.5 us -> 82.9 us  [on_device(): attended_all = lax.all_gather(attended, 'tp', axis=1, tiled=True)]
    dot_general x1 -> x2, matrix products: 7.84 us -> 13.5 us  [the longest x1 7.14 us: on_device(): query_sum = jnp.dot(tokens, w_q_full, preferred_element_type=jnp.float32)]
    all_to_all x1, waiting for transfers between devices: 11.3 us -> 14.9 us  [on_device(): got = lax.all_to_all(pieces, 'tp', 0, 0, tiled=False)]
    dot_general x4, matrix products: 8.8 us -> 5.42 us  [one_part(): jnp.dot(q_part, key_win.T, preferred_element_type=jnp.float32) * score_scale]
  transfers between devices with their start and end apart: 13 -> 14, of which waited for: 10 -> 10; matrix products, arithmetic and copies ran while one was open for 14% -> 14% of each run, Pallas kernels for 0% -> 0%
where the time goes in v4:
time: 285 us; the launch traced here: 284 us
  waiting for transfers between devices  164 us (58%)
  starting transfers between devices  32.5 us (11%)
  matrix products  30.6 us (11%)
  blocking collectives  25.6 us (9%)
  between operations  13.6 us (5%)
  other arithmetic  12.4 us (4%)
  local copies, waits for them, and re-layouts  5.06 us (2%)
    all_gather x1, waiting for transfers between devices, on_device(): attended_all = lax.all_gather(attended, 'tp', axis=1, tiled=True)  82.9 us
    all_gather x1, waiting for transfers between devices, on_device(): w_kv_full = lax.all_gather(w_kv, 'ctx', axis=0, tiled=True)  33.6 us
    ppermute x8, waiting for transfers between devices, on_device(): lax.ppermute(kv_rows_local, 'ctx', [(i, i + shift) for i in range(n_ctx -...  32.1 us
    all_to_all x1, blocking collectives, on_device(): got_rows = lax.all_to_all(sent, 'tp', 0, 0, tiled=False)  25.6 us
    ppermute x8, starting transfers between devices, on_device(): lax.ppermute(kv_rows_local, 'ctx', [(i, i + shift) for i in range(n_ctx -...  17.1 us
    all_to_all x1, waiting for transfers between devices, on_device(): got = lax.all_to_all(pieces, 'tp', 0, 0, tiled=False)  14.9 us
    ppermute x1, starting transfers between devices, on_device(): lax.ppermute(w_output, ('ctx', 'tp'), [(c * n_tp + t, t * n_tp + c) for c...  7.73 us
    all_to_all x1, starting transfers between devices, on_device(): got = lax.all_to_all(pieces, 'tp', 0, 0, tiled=False)  7.63 us
  transfers between devices with their start and end apart: 14, of which 10 were waited for; matrix products, arithmetic and copies ran while one was open for 14% of the time, Pallas kernels for 0%

profile of v4, /device:TPU:6, one launch (start us, length us, event | category | flops | bytes accessed | tf_op | source)
XLA Modules:
  0.0 284.2 jit_solution(3714294898143145552)
XLA Ops:
  8.7 7.7 %collective-permute-start.8 = (bf16[256,512]{1,0:T(8,128)(2,1)}, bf16[256,512]{1,0:T(8,128)(2,1)S(1)}, u32[]{:S(2)}, u32[]{:S(2)}) collective-permute-start(bf16[256,512]{1,0:T(8,128)(2,1)} %param.13), channel_id=1, source_target_pairs={{0,0},{1,16},{2,32},{3,48},{4,64},{5,80},{6,96},{7,112},{8,128},{9... | collective-permute-start | bytes 786440 | tf_op jit(solution)/shard_map/ppermute | solution.py:108
  18.0 33.6 %all-gather.7.cloned.1.call-done = bf16[8192,64]{0,1:T(8,128)(2,1)} async-done(((bf16[512,64]{0,1:T(8,128)(2,1)}), bf16[8192,64]{0,1:T(8,128)(2,1)}) %all-gather.7.cloned.1.call-update) | async-done | bytes 1048592 | tf_op jit(solution)/shard_map/all_gather | solution.py:48
  51.7 6.4 %fusion.23 = bf16[512,64]{0,1:T(8,128)(2,1)S(1)} fusion(bf16[8192,64]{0,1:T(8,128)(2,1)} %all-gather.7.cloned.1.call-done, bf16[512,8192]{1,0:T(8,128)(2,1)} %param.8), kind=kOutput, calls=%fused_computation.22 | convolution fusion | flops 536903680 | bytes 9502720 | tf_op jit(solution)/shard_map/dot_general | solution.py:49
  59.5 7.6 %all-to-all-start = ((bf16[16,512,2,8]{1,3,2,0:T(8,128)(2,1)}), bf16[16,512,2,8]{1,3,2,0:T(8,128)(2,1)S(1)}, u32[]{:S(2)}, u32[]{:S(2)}) async-start(bf16[16,512,2,8]{1,3,2,0:T(8,128)(2,1)} %broadcast_select_fusion), calls=%async_computation | async-start | bytes 524288 | tf_op jit(solution)/shard_map/all_to_all | solution.py:62
  68.6 14.9 %all-to-all-done = bf16[16,512,2,8]{1,3,2,0:T(8,128)(2,1)S(1)} async-done(((bf16[16,512,2,8]{1,3,2,0:T(8,128)(2,1)}), bf16[16,512,2,8]{1,3,2,0:T(8,128)(2,1)S(1)}, u32[]{:S(2)}, u32[]{:S(2)}) %all-to-all-start) | async-done | bytes 262176 | tf_op jit(solution)/shard_map/all_to_all | solution.py:62
  84.1 2.9 %collective-permute-start = (bf16[512,256]{0,1:T(8,128)(2,1)S(1)}, bf16[512,256]{0,1:T(8,128)(2,1)S(1)}, u32[]{:S(2)}, u32[]{:S(2)}) collective-permute-start(bf16[512,256]{0,1:T(8,128)(2,1)S(1)} %pad_maximum_fusion), channel_id=1, source_target_pairs={{0,128},{16,144},{32,160},{48,176},{64,192},{80,208},{96,224},{112... | collective-permute-start | bytes 786440 | tf_op jit(solution)/shard_map/ppermute | solution.py:74
  89.1 1.9 collective-permute-start.2
  91.9 1.9 collective-permute-start.3
  93.8 2.0 collective-permute-start.4
  95.8 2.8 collective-permute-done
  98.5 3.1 %collective-permute-start.5 = (bf16[512,256]{0,1:T(8,128)(2,1)S(1)}, bf16[512,256]{0,1:T(8,128)(2,1)S(1)}, u32[]{:S(2)}, u32[]{:S(2)}) collective-permute-start(bf16[512,256]{0,1:T(8,128)(2,1)S(1)} %pad_maximum_fusion), channel_id=1, source_target_pairs={{0,48},{16,64},{32,80},{48,96},{64,112},{80,128},{96,144},{112,160... | collective-permute-start | bytes 786440 | tf_op jit(solution)/shard_map/ppermute | solution.py:74
  101.6 2.9 %collective-permute-done.1 = bf16[512,256]{0,1:T(8,128)(2,1)S(1)} collective-permute-done((bf16[512,256]{0,1:T(8,128)(2,1)S(1)}, bf16[512,256]{0,1:T(8,128)(2,1)S(1)}, u32[]{:S(2)}, u32[]{:S(2)}) %collective-permute-start.1) | collective-permute-done | bytes 262176 | tf_op jit(solution)/shard_map/ppermute | solution.py:74
  104.5 1.9 collective-permute-start.6
  106.5 6.1 %collective-permute-done.2 = bf16[512,256]{0,1:T(8,128)(2,1)S(1)} collective-permute-done((bf16[512,256]{0,1:T(8,128)(2,1)S(1)}, bf16[512,256]{0,1:T(8,128)(2,1)S(1)}, u32[]{:S(2)}, u32[]{:S(2)}) %collective-permute-start.2) | collective-permute-done | bytes 262176 | tf_op jit(solution)/shard_map/ppermute | solution.py:74
  112.6 2.1 collective-permute-start.7
  115.8 5.6 %collective-permute-done.4 = bf16[512,256]{0,1:T(8,128)(2,1)S(1)} collective-permute-done((bf16[512,256]{0,1:T(8,128)(2,1)S(1)}, bf16[512,256]{0,1:T(8,128)(2,1)S(1)}, u32[]{:S(2)}, u32[]{:S(2)}) %collective-permute-start.4) | collective-permute-done | bytes 262176 | tf_op jit(solution)/shard_map/ppermute | solution.py:74
  121.4 5.6 %collective-permute-done.5 = bf16[512,256]{0,1:T(8,128)(2,1)S(1)} collective-permute-done((bf16[512,256]{0,1:T(8,128)(2,1)S(1)}, bf16[512,256]{0,1:T(8,128)(2,1)S(1)}, u32[]{:S(2)}, u32[]{:S(2)}) %collective-permute-start.5) | collective-permute-done | bytes 262176 | tf_op jit(solution)/shard_map/ppermute | solution.py:74
  127.0 8.1 %collective-permute-done.6 = bf16[512,256]{0,1:T(8,128)(2,1)S(1)} collective-permute-done((bf16[512,256]{0,1:T(8,128)(2,1)S(1)}, bf16[512,256]{0,1:T(8,128)(2,1)S(1)}, u32[]{:S(2)}, u32[]{:S(2)}) %collective-permute-start.6) | collective-permute-done | bytes 262176 | tf_op jit(solution)/shard_map/ppermute | solution.py:74
  136.9 7.1 %fusion.36 = f32[512,256]{0,1:T(8,128)S(1)} fusion(bf16[512,8192]{1,0:T(8,128)(2,1)} %param.8, bf16[8192,256]{1,0:T(8,128)(2,1)} %all-gather.5.cloned.1.call-done), kind=kOutput, calls=%fused_computation.78 | convolution fusion | flops 2147483648 | bytes 13107200 | tf_op jit(solution)/shard_map/dot_general | solution.py:51
  144.4 17.3 %while.11 = (s32[]{:T(128)}, bf16[4,256,128]{2,1,0:T(8,128)(2,1)S(1)}, s32[4,256]{1,0:T(4,128)S(1)}, s32[4608]{0:T(1024)S(1)}, s32[4,256]{1,0:T(4,128)S(1)}, /*i...) while((s32[]{:T(128)}, ...), condition=%wide.region_6.7_spmd.clone, body=%wide.region_3.6_spmd.clone.sunk | while | flops 625283072 | bytes 16798836 | solution.py:103
  147.3 1.5 fusion.57
  162.6 82.9 %all-gather.9.cloned.1.call-done = bf16[512,4096]{0,1:T(8,128)(2,1)} async-done(((bf16[512,256]{0,1:T(8,128)(2,1)}), bf16[512,4096]{0,1:T(8,128)(2,1)}) %all-gather.9.cloned.1.call-update) | async-done | bytes 4194320 | tf_op jit(solution)/shard_map/all_gather | solution.py:114
  245.4 5.8 %convolution_convert_fusion = bf16[512,512]{1,0:T(8,128)(2,1)S(1)} fusion(bf16[512,4096]{0,1:T(8,128)(2,1)} %all-gather.9.cloned.1.call-done, bf16[4096,512]{1,0:T(8,128)(2,1)} %all-gather.11.cloned.1.call-done), kind=kOutput, calls=%fused_computation.20 | convolution fusion | flops 2147745792 | bytes 8912896 | tf_op jit(solution)/shard_map/dot_general | solution.py:115
  251.3 25.6 %all_to_all.10 = bf16[16,32,512]{2,1,0:T(8,128)(2,1)S(1)} all-to-all(bf16[16,32,512]{2,1,0:T(8,128)(2,1)S(1)} %bitcast.64), channel_id=1, replica_groups=mesh['ctx'=16,'tp'=16] {'tp'}, dimensions={0} | all-to-all | bytes 1048576 | tf_op jit(solution)/shard_map/all_to_all | solution.py:119
  (89 shorter events, 30.6 us)
Async XLA Ops:
  6.5 45.1 %all-gather.7.cloned.1.call-start = ((), (), s32[]{:S(2)}) async-start(), calls=%async_computation.3 | async-start | bytes 1114112 | tf_op jit(solution)/shard_map/all_gather | solution.py:48
  8.0 128.9 %all-gather.5.cloned.1.call-start = ((), (), s32[]{:S(2)}) async-start(), calls=%async_computation.2 | async-start | bytes 4456448 | tf_op jit(solution)/shard_map/all_gather | solution.py:50
  8.7 82.3 %collective-permute-start.8 = (bf16[256,512]{1,0:T(8,128)(2,1)}, bf16[256,512]{1,0:T(8,128)(2,1)S(1)}, u32[]{:S(2)}, u32[]{:S(2)}) collective-permute-start(bf16[256,512]{1,0:T(8,128)(2,1)} %param.13), channel_id=1, source_target_pairs={{0,0},{1,16},{2,32},{3,48},{4,64},{5,80},{6,96},{7,112},{8,128},{9... | collective-permute-start | bytes 786440 | tf_op jit(solution)/shard_map/ppermute | solution.py:108
  59.5 24.0 %all-to-all-start = ((bf16[16,512,2,8]{1,3,2,0:T(8,128)(2,1)}), bf16[16,512,2,8]{1,3,2,0:T(8,128)(2,1)S(1)}, u32[]{:S(2)}, u32[]{:S(2)}) async-start(bf16[16,512,2,8]{1,3,2,0:T(8,128)(2,1)} %broadcast_select_fusion), calls=%async_computation | async-start | bytes 524288 | tf_op jit(solution)/shard_map/all_to_all | solution.py:62
  67.1 95.5 %all-gather.11.cloned.1.call-start = ((), (), s32[]{:S(2)}) async-start(), calls=%async_computation.5 | async-start | bytes 4456448 | tf_op jit(solution)/shard_map/all_gather | solution.py:113
  84.1 14.4 %collective-permute-start = (bf16[512,256]{0,1:T(8,128)(2,1)S(1)}, bf16[512,256]{0,1:T(8,128)(2,1)S(1)}, u32[]{:S(2)}, u32[]{:S(2)}) collective-permute-start(bf16[512,256]{0,1:T(8,128)(2,1)S(1)} %pad_maximum_fusion), channel_id=1, source_target_pairs={{0,128},{16,144},{32,160},{48,176},{64,192},{80,208},{96,224},{112... | collective-permute-start | bytes 786440 | tf_op jit(solution)/shard_map/ppermute | solution.py:74
  87.7 16.8 %collective-permute-start.1 = (bf16[512,256]{0,1:T(8,128)(2,1)S(1)}, bf16[512,256]{0,1:T(8,128)(2,1)S(1)}, u32[]{:S(2)}, u32[]{:S(2)}) collective-permute-start(bf16[512,256]{0,1:T(8,128)(2,1)S(1)} %pad_maximum_fusion), channel_id=1, source_target_pairs={{0,112},{16,128},{32,144},{48,160},{64,176},{80,192},{96,208},{112... | collective-permute-start | bytes 786440 | tf_op jit(solution)/shard_map/ppermute | solution.py:74
  89.1 23.5 %collective-permute-start.2 = (bf16[512,256]{0,1:T(8,128)(2,1)S(1)}, bf16[512,256]{0,1:T(8,128)(2,1)S(1)}, u32[]{:S(2)}, u32[]{:S(2)}) collective-permute-start(bf16[512,256]{0,1:T(8,128)(2,1)S(1)} %pad_maximum_fusion), channel_id=1, source_target_pairs={{0,96},{16,112},{32,128},{48,144},{64,160},{80,176},{96,192},{112,... | collective-permute-start | bytes 786440 | tf_op jit(solution)/shard_map/ppermute | solution.py:74
  91.1 0.7 copy-start.3
  91.8 153.6 %all-gather.9.cloned.1.call-start = ((), (), s32[]{:S(2)}) async-start(), calls=%async_computation.4 | async-start | bytes 4456448 | tf_op jit(solution)/shard_map/all_gather | solution.py:114
  91.9 23.9 %collective-permute-start.3 = (bf16[512,256]{0,1:T(8,128)(2,1)S(1)}, bf16[512,256]{0,1:T(8,128)(2,1)S(1)}, u32[]{:S(2)}, u32[]{:S(2)}) collective-permute-start(bf16[512,256]{0,1:T(8,128)(2,1)S(1)} %pad_maximum_fusion), channel_id=1, source_target_pairs={{0,80},{16,96},{32,112},{48,128},{64,144},{80,160},{96,176},{112,1... | collective-permute-start | bytes 786440 | tf_op jit(solution)/shard_map/ppermute | solution.py:74
  93.8 27.6 %collective-permute-start.4 = (bf16[512,256]{0,1:T(8,128)(2,1)S(1)}, bf16[512,256]{0,1:T(8,128)(2,1)S(1)}, u32[]{:S(2)}, u32[]{:S(2)}) collective-permute-start(bf16[512,256]{0,1:T(8,128)(2,1)S(1)} %pad_maximum_fusion), channel_id=1, source_target_pairs={{0,64},{16,80},{32,96},{48,112},{64,128},{80,144},{96,160},{112,17... | collective-permute-start | bytes 786440 | tf_op jit(solution)/shard_map/ppermute | solution.py:74
  98.5 28.4 %collective-permute-start.5 = (bf16[512,256]{0,1:T(8,128)(2,1)S(1)}, bf16[512,256]{0,1:T(8,128)(2,1)S(1)}, u32[]{:S(2)}, u32[]{:S(2)}) collective-permute-start(bf16[512,256]{0,1:T(8,128)(2,1)S(1)} %pad_maximum_fusion), channel_id=1, source_target_pairs={{0,48},{16,64},{32,80},{48,96},{64,112},{80,128},{96,144},{112,160... | collective-permute-start | bytes 786440 | tf_op jit(solution)/shard_map/ppermute | solution.py:74
  104.5 30.6 %collective-permute-start.6 = (bf16[512,256]{0,1:T(8,128)(2,1)S(1)}, bf16[512,256]{0,1:T(8,128)(2,1)S(1)}, u32[]{:S(2)}, u32[]{:S(2)}) collective-permute-start(bf16[512,256]{0,1:T(8,128)(2,1)S(1)} %pad_maximum_fusion), channel_id=1, source_target_pairs={{0,32},{16,48},{32,64},{48,80},{64,96},{80,112},{96,128},{112,144}... | collective-permute-start | bytes 786440 | tf_op jit(solution)/shard_map/ppermute | solution.py:74
  112.6 22.6 %collective-permute-start.7 = (bf16[512,256]{0,1:T(8,128)(2,1)S(1)}, bf16[512,256]{0,1:T(8,128)(2,1)S(1)}, u32[]{:S(2)}, u32[]{:S(2)}) collective-permute-start(bf16[512,256]{0,1:T(8,128)(2,1)S(1)} %pad_maximum_fusion), channel_id=1, source_target_pairs={{0,16},{16,32},{32,48},{48,64},{64,80},{80,96},{96,112},{112,128},... | collective-permute-start | bytes 786440 | tf_op jit(solution)/shard_map/ppermute | solution.py:74
  136.8 7.2 %copy-start.1 = (f32[512,64]{0,1:T(8,128)S(1)}, f32[512,64]{0,1:T(8,128)}, u32[]{:S(2)}) copy-start(f32[512,64]{0,1:T(8,128)} %get-tuple-element.131) | copy-start | bytes 393220
  136.8 7.2 %copy-start.2 = (f32[512,64]{0,1:T(8,128)S(1)}, f32[512,64]{0,1:T(8,128)}, u32[]{:S(2)}) copy-start(f32[512,64]{0,1:T(8,128)} %get-tuple-element.132) | copy-start | bytes 393220
  136.9 7.5 %copy-start = (s32[4608]{0:T(1024)S(1)}, s32[4608]{0:T(1024)}, u32[]{:S(2)}) copy-start(s32[4608]{0:T(1024)} %compare_select_fusion) | copy-start | bytes 55300
  136.9 7.5 %copy-start.4 = (bf16[4,256,128]{2,1,0:T(8,128)(2,1)S(1)}, bf16[4,256,128]{2,1,0:T(8,128)(2,1)}, u32[]{:S(2)}) copy-start(bf16[4,256,128]{2,1,0:T(8,128)(2,1)} %custom-call.3) | copy-start | bytes 786436
Sparse Core Ops, SparseCore 0:
  9.1 42.4 all-gather.6
  53.5 47.7 all-gather.4
  103.2 56.4 all-gather.10
  162.7 82.7 all-gather.8

commit v5 on v4

--- a/solution.py
+++ b/solution.py
@@ -111,7 +111,9 @@
         [(c * n_tp + t, t * n_tp + c) for c in range(n_ctx_all) for t in range(n_tp)],
     )
     w_chunk = lax.all_gather(w_moved, "ctx", axis=0, tiled=True)
-    attended_all = lax.all_gather(attended, "tp", axis=1, tiled=True)
+    copies = jnp.broadcast_to(attended[None], (n_tp,) + attended.shape)
+    from_peers = lax.all_to_all(copies, "tp", 0, 0, tiled=False)
+    attended_all = jnp.transpose(from_peers, (1, 0, 2)).reshape(tok_rows, n_tp * attended.shape[1])
     out_chunk = jnp.dot(attended_all, w_chunk, preferred_element_type=jnp.float32).astype(jnp.bfloat16)
     chunk = out_chunk.shape[1]
     out_rows = tok_rows // n_tp

time: 285 us -> 295 us (1.035)
  starting transfers between devices: 32.5 us -> 41.4 us
    all_gather x1 -> x0, waiting for transfers between devices: 82.9 us -> none  [on_device(): attended_all = lax.all_gather(attended, 'tp', axis=1, tiled=True)]
    all_to_all x0 -> x1, waiting for transfers between devices: none -> 82.4 us  [on_device(): from_peers = lax.all_to_all(copies, 'tp', 0, 0, tiled=False)]
    all_to_all x0 -> x1, starting transfers between devices: none -> 8.89 us  [on_device(): from_peers = lax.all_to_all(copies, 'tp', 0, 0, tiled=False)]
where the time goes in v5:
time: 295 us; the launch traced here: 293 us
  waiting for transfers between devices  164 us (56%)
  starting transfers between devices  41.4 us (14%)
  matrix products  30.6 us (10%)
  blocking collectives  24.7 us (8%)
  between operations  13.6 us (5%)
  other arithmetic  12.4 us (4%)
  local copies, waits for them, and re-layouts  6.75 us (2%)
    all_to_all x1, waiting for transfers between devices, on_device(): from_peers = lax.all_to_all(copies, 'tp', 0, 0, tiled=False)  82.4 us
    all_gather x1, waiting for transfers between devices, on_device(): w_kv_full = lax.all_gather(w_kv, 'ctx', axis=0, tiled=True)  33.6 us
    ppermute x8, waiting for transfers between devices, on_device(): lax.ppermute(kv_rows_local, 'ctx', [(i, i + shift) for i in range(n_ctx -...  32.2 us
    all_to_all x1, blocking collectives, on_device(): got_rows = lax.all_to_all(sent, 'tp', 0, 0, tiled=False)  24.7 us
    ppermute x8, starting transfers between devices, on_device(): lax.ppermute(kv_rows_local, 'ctx', [(i, i + shift) for i in range(n_ctx -...  17.1 us
    all_to_all x1, waiting for transfers between devices, on_device(): got = lax.all_to_all(pieces, 'tp', 0, 0, tiled=False)  14.9 us
    all_to_all x1, starting transfers between devices, on_device(): from_peers = lax.all_to_all(copies, 'tp', 0, 0, tiled=False)  8.89 us
    ppermute x1, starting transfers between devices, on_device(): lax.ppermute(w_output, ('ctx', 'tp'), [(c * n_tp + t, t * n_tp + c) for c...  7.73 us
  transfers between devices with their start and end apart: 14, of which 10 were waited for; matrix products, arithmetic and copies ran while one was open for 14% of the time, Pallas kernels for 0%

profile of v5, /device:TPU:6, one launch (start us, length us, event | category | flops | bytes accessed | tf_op | source)
XLA Modules:
  0.0 293.4 jit_solution(110066974156185982)
XLA Ops:
  8.7 7.7 %collective-permute-start.8 = (bf16[256,512]{1,0:T(8,128)(2,1)}, bf16[256,512]{1,0:T(8,128)(2,1)S(1)}, u32[]{:S(2)}, u32[]{:S(2)}) collective-permute-start(bf16[256,512]{1,0:T(8,128)(2,1)} %param.13), channel_id=1, source_target_pairs={{0,0},{1,16},{2,32},{3,48},{4,64},{5,80},{6,96},{7,112},{8,128},{9... | collective-permute-start | bytes 786440 | tf_op jit(solution)/shard_map/ppermute | solution.py:108
  18.0 33.6 %all-gather.6.cloned.1.call-done = bf16[8192,64]{0,1:T(8,128)(2,1)} async-done(((bf16[512,64]{0,1:T(8,128)(2,1)}), bf16[8192,64]{0,1:T(8,128)(2,1)}) %all-gather.6.cloned.1.call-update) | async-done | bytes 1048592 | tf_op jit(solution)/shard_map/all_gather | solution.py:48
  51.7 6.4 %fusion.23 = bf16[512,64]{0,1:T(8,128)(2,1)S(1)} fusion(bf16[8192,64]{0,1:T(8,128)(2,1)} %all-gather.6.cloned.1.call-done, bf16[512,8192]{1,0:T(8,128)(2,1)} %param.8), kind=kOutput, calls=%fused_computation.22 | convolution fusion | flops 536903680 | bytes 9502720 | tf_op jit(solution)/shard_map/dot_general | solution.py:49
  59.5 7.6 %all-to-all-start = ((bf16[16,512,2,8]{1,3,2,0:T(8,128)(2,1)}), bf16[16,512,2,8]{1,3,2,0:T(8,128)(2,1)S(1)}, u32[]{:S(2)}, u32[]{:S(2)}) async-start(bf16[16,512,2,8]{1,3,2,0:T(8,128)(2,1)} %broadcast_select_fusion), calls=%async_computation | async-start | bytes 524288 | tf_op jit(solution)/shard_map/all_to_all | solution.py:62
  68.5 14.9 %all-to-all-done = bf16[16,512,2,8]{1,3,2,0:T(8,128)(2,1)S(1)} async-done(((bf16[16,512,2,8]{1,3,2,0:T(8,128)(2,1)}), bf16[16,512,2,8]{1,3,2,0:T(8,128)(2,1)S(1)}, u32[]{:S(2)}, u32[]{:S(2)}) %all-to-all-start) | async-done | bytes 262176 | tf_op jit(solution)/shard_map/all_to_all | solution.py:62
  84.1 2.9 collective-permute-start
  89.0 1.9 collective-permute-start.2
  91.8 1.9 collective-permute-start.3
  93.7 2.0 collective-permute-start.4
  95.7 2.8 collective-permute-done
  98.5 3.1 %collective-permute-start.5 = (bf16[512,256]{0,1:T(8,128)(2,1)S(1)}, bf16[512,256]{0,1:T(8,128)(2,1)S(1)}, u32[]{:S(2)}, u32[]{:S(2)}) collective-permute-start(bf16[512,256]{0,1:T(8,128)(2,1)S(1)} %pad_maximum_fusion), channel_id=1, source_target_pairs={{0,48},{16,64},{32,80},{48,96},{64,112},{80,128},{96,144},{112,160... | collective-permute-start | bytes 786440 | tf_op jit(solution)/shard_map/ppermute | solution.py:74
  101.6 2.9 collective-permute-done.1
  106.5 6.1 %collective-permute-done.2 = bf16[512,256]{0,1:T(8,128)(2,1)S(1)} collective-permute-done((bf16[512,256]{0,1:T(8,128)(2,1)S(1)}, bf16[512,256]{0,1:T(8,128)(2,1)S(1)}, u32[]{:S(2)}, u32[]{:S(2)}) %collective-permute-start.2) | collective-permute-done | bytes 262176 | tf_op jit(solution)/shard_map/ppermute | solution.py:74
  112.5 2.1 collective-permute-start.7
  115.8 5.6 %collective-permute-done.4 = bf16[512,256]{0,1:T(8,128)(2,1)S(1)} collective-permute-done((bf16[512,256]{0,1:T(8,128)(2,1)S(1)}, bf16[512,256]{0,1:T(8,128)(2,1)S(1)}, u32[]{:S(2)}, u32[]{:S(2)}) %collective-permute-start.4) | collective-permute-done | bytes 262176 | tf_op jit(solution)/shard_map/ppermute | solution.py:74
  121.4 5.6 %collective-permute-done.5 = bf16[512,256]{0,1:T(8,128)(2,1)S(1)} collective-permute-done((bf16[512,256]{0,1:T(8,128)(2,1)S(1)}, bf16[512,256]{0,1:T(8,128)(2,1)S(1)}, u32[]{:S(2)}, u32[]{:S(2)}) %collective-permute-start.5) | collective-permute-done | bytes 262176 | tf_op jit(solution)/shard_map/ppermute | solution.py:74
  127.0 8.1 %collective-permute-done.6 = bf16[512,256]{0,1:T(8,128)(2,1)S(1)} collective-permute-done((bf16[512,256]{0,1:T(8,128)(2,1)S(1)}, bf16[512,256]{0,1:T(8,128)(2,1)S(1)}, u32[]{:S(2)}, u32[]{:S(2)}) %collective-permute-start.6) | collective-permute-done | bytes 262176 | tf_op jit(solution)/shard_map/ppermute | solution.py:74
  136.9 7.1 %fusion.36 = f32[512,256]{0,1:T(8,128)S(1)} fusion(bf16[512,8192]{1,0:T(8,128)(2,1)} %param.8, bf16[8192,256]{1,0:T(8,128)(2,1)} %all-gather.4.cloned.1.call-done), kind=kOutput, calls=%fused_computation.78 | convolution fusion | flops 2147483648 | bytes 13107200 | tf_op jit(solution)/shard_map/dot_general | solution.py:51
  144.4 17.3 %while.11 = (s32[]{:T(128)}, bf16[4,256,128]{2,1,0:T(8,128)(2,1)S(1)}, s32[4,256]{1,0:T(4,128)S(1)}, s32[4608]{0:T(1024)S(1)}, s32[4,256]{1,0:T(4,128)S(1)}, /*i...) while((s32[]{:T(128)}, ...), condition=%wide.region_6.7_spmd.clone, body=%wide.region_3.6_spmd.clone.sunk | while | flops 625283072 | bytes 16798836 | solution.py:103
  161.8 2.4 broadcast_in_dim.59
  164.2 8.9 %all-to-all-start.1 = ((bf16[16,512,256]{1,2,0:T(8,128)(2,1)}), bf16[16,512,256]{1,2,0:T(8,128)(2,1)}, u32[]{:S(2)}, u32[]{:S(2)}) async-start(bf16[16,512,256]{1,2,0:T(8,128)(2,1)} %broadcast_in_dim.59), calls=%async_computation.1 | async-start | bytes 8388608 | tf_op jit(solution)/shard_map/all_to_all | solution.py:115
  173.1 82.4 %all-to-all-done.1 = bf16[16,512,256]{1,2,0:T(8,128)(2,1)} async-done(((bf16[16,512,256]{1,2,0:T(8,128)(2,1)}), bf16[16,512,256]{1,2,0:T(8,128)(2,1)}, u32[]{:S(2)}, u32[]{:S(2)}) %all-to-all-start.1) | async-done | bytes 4194336 | tf_op jit(solution)/shard_map/all_to_all | solution.py:115
  255.5 5.8 %convolution_convert_fusion = bf16[512,512]{1,0:T(8,128)(2,1)S(1)} fusion(bf16[512,4096]{0,1:T(8,128)(2,1)} %bitcast.15, bf16[4096,512]{1,0:T(8,128)(2,1)} %all-gather.8.cloned.1.call-done), kind=kOutput, calls=%fused_computation.20 | convolution fusion | flops 2147745792 | bytes 8912896 | tf_op jit(solution)/shard_map/dot_general | solution.py:117
  261.3 24.7 %all_to_all.15 = bf16[16,32,512]{2,1,0:T(8,128)(2,1)S(1)} all-to-all(bf16[16,32,512]{2,1,0:T(8,128)(2,1)S(1)} %bitcast.67), channel_id=1, replica_groups=mesh['ctx'=16,'tp'=16] {'tp'}, dimensions={0} | all-to-all | bytes 1048576 | tf_op jit(solution)/shard_map/all_to_all | solution.py:121
  (89 shorter events, 33.2 us)
Async XLA Ops:
  6.5 45.1 %all-gather.6.cloned.1.call-start = ((), (), s32[]{:S(2)}) async-start(), calls=%async_computation.4 | async-start | bytes 1114112 | tf_op jit(solution)/shard_map/all_gather | solution.py:48
  8.0 128.9 %all-gather.4.cloned.1.call-start = ((), (), s32[]{:S(2)}) async-start(), calls=%async_computation.3 | async-start | bytes 4456448 | tf_op jit(solution)/shard_map/all_gather | solution.py:50
  8.7 82.3 %collective-permute-start.8 = (bf16[256,512]{1,0:T(8,128)(2,1)}, bf16[256,512]{1,0:T(8,128)(2,1)S(1)}, u32[]{:S(2)}, u32[]{:S(2)}) collective-permute-start(bf16[256,512]{1,0:T(8,128)(2,1)} %param.13), channel_id=1, source_target_pairs={{0,0},{1,16},{2,32},{3,48},{4,64},{5,80},{6,96},{7,112},{8,128},{9... | collective-permute-start | bytes 786440 | tf_op jit(solution)/shard_map/ppermute | solution.py:108
  59.5 24.0 %all-to-all-start = ((bf16[16,512,2,8]{1,3,2,0:T(8,128)(2,1)}), bf16[16,512,2,8]{1,3,2,0:T(8,128)(2,1)S(1)}, u32[]{:S(2)}, u32[]{:S(2)}) async-start(bf16[16,512,2,8]{1,3,2,0:T(8,128)(2,1)} %broadcast_select_fusion), calls=%async_computation | async-start | bytes 524288 | tf_op jit(solution)/shard_map/all_to_all | solution.py:62
  67.1 106.0 %all-gather.8.cloned.1.call-start = ((), (), s32[]{:S(2)}) async-start(), calls=%async_computation.5 | async-start | bytes 4456448 | tf_op jit(solution)/shard_map/all_gather | solution.py:113
  84.1 14.4 %collective-permute-start = (bf16[512,256]{0,1:T(8,128)(2,1)S(1)}, bf16[512,256]{0,1:T(8,128)(2,1)S(1)}, u32[]{:S(2)}, u32[]{:S(2)}) collective-permute-start(bf16[512,256]{0,1:T(8,128)(2,1)S(1)} %pad_maximum_fusion), channel_id=1, source_target_pairs={{0,128},{16,144},{32,160},{48,176},{64,192},{80,208},{96,224},{112... | collective-permute-start | bytes 786440 | tf_op jit(solution)/shard_map/ppermute | solution.py:74
  87.7 16.9 %collective-permute-start.1 = (bf16[512,256]{0,1:T(8,128)(2,1)S(1)}, bf16[512,256]{0,1:T(8,128)(2,1)S(1)}, u32[]{:S(2)}, u32[]{:S(2)}) collective-permute-start(bf16[512,256]{0,1:T(8,128)(2,1)S(1)} %pad_maximum_fusion), channel_id=1, source_target_pairs={{0,112},{16,128},{32,144},{48,160},{64,176},{80,192},{96,208},{112... | collective-permute-start | bytes 786440 | tf_op jit(solution)/shard_map/ppermute | solution.py:74
  89.0 23.5 %collective-permute-start.2 = (bf16[512,256]{0,1:T(8,128)(2,1)S(1)}, bf16[512,256]{0,1:T(8,128)(2,1)S(1)}, u32[]{:S(2)}, u32[]{:S(2)}) collective-permute-start(bf16[512,256]{0,1:T(8,128)(2,1)S(1)} %pad_maximum_fusion), channel_id=1, source_target_pairs={{0,96},{16,112},{32,128},{48,144},{64,160},{80,176},{96,192},{112,... | collective-permute-start | bytes 786440 | tf_op jit(solution)/shard_map/ppermute | solution.py:74
  91.1 0.7 copy-start.3
  91.8 23.9 %collective-permute-start.3 = (bf16[512,256]{0,1:T(8,128)(2,1)S(1)}, bf16[512,256]{0,1:T(8,128)(2,1)S(1)}, u32[]{:S(2)}, u32[]{:S(2)}) collective-permute-start(bf16[512,256]{0,1:T(8,128)(2,1)S(1)} %pad_maximum_fusion), channel_id=1, source_target_pairs={{0,80},{16,96},{32,112},{48,128},{64,144},{80,160},{96,176},{112,1... | collective-permute-start | bytes 786440 | tf_op jit(solution)/shard_map/ppermute | solution.py:74
  93.7 27.6 %collective-permute-start.4 = (bf16[512,256]{0,1:T(8,128)(2,1)S(1)}, bf16[512,256]{0,1:T(8,128)(2,1)S(1)}, u32[]{:S(2)}, u32[]{:S(2)}) collective-permute-start(bf16[512,256]{0,1:T(8,128)(2,1)S(1)} %pad_maximum_fusion), channel_id=1, source_target_pairs={{0,64},{16,80},{32,96},{48,112},{64,128},{80,144},{96,160},{112,17... | collective-permute-start | bytes 786440 | tf_op jit(solution)/shard_map/ppermute | solution.py:74
  98.5 28.4 %collective-permute-start.5 = (bf16[512,256]{0,1:T(8,128)(2,1)S(1)}, bf16[512,256]{0,1:T(8,128)(2,1)S(1)}, u32[]{:S(2)}, u32[]{:S(2)}) collective-permute-start(bf16[512,256]{0,1:T(8,128)(2,1)S(1)} %pad_maximum_fusion), channel_id=1, source_target_pairs={{0,48},{16,64},{32,80},{48,96},{64,112},{80,128},{96,144},{112,160... | collective-permute-start | bytes 786440 | tf_op jit(solution)/shard_map/ppermute | solution.py:74
  104.5 30.6 %collective-permute-start.6 = (bf16[512,256]{0,1:T(8,128)(2,1)S(1)}, bf16[512,256]{0,1:T(8,128)(2,1)S(1)}, u32[]{:S(2)}, u32[]{:S(2)}) collective-permute-start(bf16[512,256]{0,1:T(8,128)(2,1)S(1)} %pad_maximum_fusion), channel_id=1, source_target_pairs={{0,32},{16,48},{32,64},{48,80},{64,96},{80,112},{96,128},{112,144}... | collective-permute-start | bytes 786440 | tf_op jit(solution)/shard_map/ppermute | solution.py:74
  112.5 22.6 %collective-permute-start.7 = (bf16[512,256]{0,1:T(8,128)(2,1)S(1)}, bf16[512,256]{0,1:T(8,128)(2,1)S(1)}, u32[]{:S(2)}, u32[]{:S(2)}) collective-permute-start(bf16[512,256]{0,1:T(8,128)(2,1)S(1)} %pad_maximum_fusion), channel_id=1, source_target_pairs={{0,16},{16,32},{32,48},{48,64},{64,80},{80,96},{96,112},{112,128},... | collective-permute-start | bytes 786440 | tf_op jit(solution)/shard_map/ppermute | solution.py:74
  136.8 7.2 %copy-start.1 = (f32[512,64]{0,1:T(8,128)S(1)}, f32[512,64]{0,1:T(8,128)}, u32[]{:S(2)}) copy-start(f32[512,64]{0,1:T(8,128)} %get-tuple-element.131) | copy-start | bytes 393220
  136.8 7.2 %copy-start.2 = (f32[512,64]{0,1:T(8,128)S(1)}, f32[512,64]{0,1:T(8,128)}, u32[]{:S(2)}) copy-start(f32[512,64]{0,1:T(8,128)} %get-tuple-element.132) | copy-start | bytes 393220
  136.9 7.5 %copy-start = (s32[4608]{0:T(1024)S(1)}, s32[4608]{0:T(1024)}, u32[]{:S(2)}) copy-start(s32[4608]{0:T(1024)} %compare_select_fusion) | copy-start | bytes 55300
  136.9 7.5 %copy-start.4 = (bf16[4,256,128]{2,1,0:T(8,128)(2,1)S(1)}, bf16[4,256,128]{2,1,0:T(8,128)(2,1)}, u32[]{:S(2)}) copy-start(bf16[4,256,128]{2,1,0:T(8,128)(2,1)} %custom-call.3) | copy-start | bytes 786436
  164.2 91.3 %all-to-all-start.1 = ((bf16[16,512,256]{1,2,0:T(8,128)(2,1)}), bf16[16,512,256]{1,2,0:T(8,128)(2,1)}, u32[]{:S(2)}, u32[]{:S(2)}) async-start(bf16[16,512,256]{1,2,0:T(8,128)(2,1)} %broadcast_in_dim.59), calls=%async_computation.1 | async-start | bytes 8388608 | tf_op jit(solution)/shard_map/all_to_all | solution.py:115
Sparse Core Ops, SparseCore 0:
  9.1 42.4 all-gather.5
  53.5 47.7 all-gather.3
  103.2 56.8 all-gather.7

commit v6 on v4

--- a/solution.py
+++ b/solution.py
@@ -47,7 +47,17 @@
     w_kv = jnp.concatenate([w_key, w_value], axis=1)
     w_kv_full = lax.all_gather(w_kv, "ctx", axis=0, tiled=True)
     kv_local = jnp.dot(tokens, w_kv_full, preferred_element_type=jnp.float32).astype(jnp.bfloat16)
-    w_q_full = lax.all_gather(w_query, "ctx", axis=0, tiled=True)
+    n_ctx_all = lax.axis_size("ctx")
+    w_moved = lax.ppermute(
+        w_output,
+        ("ctx", "tp"),
+        [(c * n_tp + t, t * n_tp + c) for c in range(n_ctx_all) for t in range(n_tp)],
+    )
+    o_rows, o_cols = w_moved.shape
+    w_q_o = jnp.concatenate([w_query, w_moved.reshape(tok_rows, o_rows * o_cols // tok_rows)], axis=1)
+    w_q_o_full = lax.all_gather(w_q_o, "ctx", axis=0, tiled=False)
+    w_q_full = w_q_o_full[:, :, :q_cols].reshape(n_ctx_all * tok_rows, q_cols)
+    w_chunk = w_q_o_full[:, :, q_cols:].reshape(n_ctx_all * o_rows, o_cols)
     query_sum = jnp.dot(tokens, w_q_full, preferred_element_type=jnp.float32)
 
     heads_dev = q_cols // HD
@@ -104,13 +114,6 @@
     attended = attended.reshape(heads_dev, tok_rows, HD)
     attended = jnp.transpose(attended, (1, 0, 2)).reshape(tok_rows, heads_dev * HD)
 
-    n_ctx_all = lax.axis_size("ctx")
-    w_moved = lax.ppermute(
-        w_output,
-        ("ctx", "tp"),
-        [(c * n_tp + t, t * n_tp + c) for c in range(n_ctx_all) for t in range(n_tp)],
-    )
-    w_chunk = lax.all_gather(w_moved, "ctx", axis=0, tiled=True)
     attended_all = lax.all_gather(attended, "tp", axis=1, tiled=True)
     out_chunk = jnp.dot(attended_all, w_chunk, preferred_element_type=jnp.float32).astype(jnp.bfloat16)
     chunk = out_chunk.shape[1]

time: 285 us -> 301 us (1.056)
  local copies, waits for them, and re-layouts: 5.06 us -> 16.8 us
  waiting for transfers between devices: 164 us -> 168 us
    all_gather x1, waiting for transfers between devices: 33.6 us -> 15 us  [on_device(): w_kv_full = lax.all_gather(w_kv, 'ctx', axis=0, tiled=True)]
    ppermute x8, waiting for transfers between devices: 32.1 us -> 49.3 us  [on_device(): lax.ppermute(kv_rows_local, 'ctx', [(i, i + shift) for i in range(n_ctx -...]
    ppermute x1, waiting for transfers between devices: 0.01 us -> 16.8 us  [on_device(): lax.ppermute(w_output, ('ctx', 'tp'), [(c * n_tp + t, t * n_tp + c) for c...]
    all_gather x1, waiting for transfers between devices: 82.9 us -> 72.2 us  [on_device(): attended_all = lax.all_gather(attended, 'tp', axis=1, tiled=True)]
    reshape x0 -> x2, local copies, waits for them, and re-layouts: none -> 7.25 us  [the longest x1 7.16 us: on_device(): w_chunk = w_q_o_full[:, :, q_cols:].reshape(n_ctx_all * o_rows, o_cols)]
    slice x0 -> x1, local copies, waits for them, and re-layouts: none -> 5.22 us  [on_device(): w_chunk = w_q_o_full[:, :, q_cols:].reshape(n_ctx_all * o_rows, o_cols)]
  transfers between devices with their start and end apart: 14 -> 13, of which waited for: 10 -> 11; matrix products, arithmetic and copies ran while one was open for 14% -> 8% of each run, Pallas kernels for 0% -> 0%
where the time goes in v6:
time: 301 us
  waiting for transfers between devices  168 us (56%)
  starting transfers between devices  32.9 us (11%)
  matrix products  29.3 us (10%)
  blocking collectives  25.5 us (8%)
  local copies, waits for them, and re-layouts  16.8 us (6%)
  other arithmetic  14.2 us (5%)
  between operations  13.5 us (4%)
    all_gather x1, waiting for transfers between devices, on_device(): attended_all = lax.all_gather(attended, 'tp', axis=1, tiled=True)  72.2 us
    ppermute x8, waiting for transfers between devices, on_device(): lax.ppermute(kv_rows_local, 'ctx', [(i, i + shift) for i in range(n_ctx -...  49.3 us
    all_to_all x1, blocking collectives, on_device(): got_rows = lax.all_to_all(sent, 'tp', 0, 0, tiled=False)  25.5 us
    ppermute x8, starting transfers between devices, on_device(): lax.ppermute(kv_rows_local, 'ctx', [(i, i + shift) for i in range(n_ctx -...  17.4 us
    ppermute x1, waiting for transfers between devices, on_device(): lax.ppermute(w_output, ('ctx', 'tp'), [(c * n_tp + t, t * n_tp + c) for c...  16.8 us
    all_gather x1, waiting for transfers between devices, on_device(): w_kv_full = lax.all_gather(w_kv, 'ctx', axis=0, tiled=True)  15 us
    all_to_all x1, waiting for transfers between devices, on_device(): got = lax.all_to_all(pieces, 'tp', 0, 0, tiled=False)  14.9 us
    ppermute x1, starting transfers between devices, on_device(): lax.ppermute(w_output, ('ctx', 'tp'), [(c * n_tp + t, t * n_tp + c) for c...  7.73 us
  transfers between devices with their start and end apart: 13, of which 11 were waited for; matrix products, arithmetic and copies ran while one was open for 8% of the time, Pallas kernels for 0%

profile of v6, /device:TPU:6, one launch (start us, length us, event | category | flops | bytes accessed | tf_op | source)
XLA Modules:
  0.0 300.6 jit_solution(11714272904759222937)
XLA Ops:
  8.0 7.7 %collective-permute-start = (bf16[256,512]{1,0:T(8,128)(2,1)}, bf16[256,512]{1,0:T(8,128)(2,1)S(1)}, u32[]{:S(2)}, u32[]{:S(2)}) collective-permute-start(bf16[256,512]{1,0:T(8,128)(2,1)} %param.13), channel_id=1, source_target_pairs={{0,0},{1,16},{2,32},{3,48},{4,64},{5,80},{6,96},{7,112},{8,128},{9... | collective-permute-start | bytes 786440 | tf_op jit(solution)/shard_map/ppermute | solution.py:51
  15.7 16.8 %collective-permute-done = bf16[256,512]{1,0:T(8,128)(2,1)S(1)} collective-permute-done((bf16[256,512]{1,0:T(8,128)(2,1)}, bf16[256,512]{1,0:T(8,128)(2,1)S(1)}, u32[]{:S(2)}, u32[]{:S(2)}) %collective-permute-start) | collective-permute-done | bytes 262176 | tf_op jit(solution)/shard_map/ppermute | solution.py:51
  36.0 15.0 %all-gather.5.cloned.1.call-done = bf16[8192,64]{0,1:T(8,128)(2,1)} async-done(((bf16[512,64]{0,1:T(8,128)(2,1)}), bf16[8192,64]{0,1:T(8,128)(2,1)}) %all-gather.5.cloned.1.call-update) | async-done | bytes 1048592 | tf_op jit(solution)/shard_map/all_gather | solution.py:48
  50.9 6.4 %fusion.23 = bf16[512,64]{0,1:T(8,128)(2,1)S(1)} fusion(bf16[8192,64]{0,1:T(8,128)(2,1)} %all-gather.5.cloned.1.call-done, bf16[512,8192]{1,0:T(8,128)(2,1)} %param.8), kind=kOutput, calls=%fused_computation.22 | convolution fusion | flops 536903680 | bytes 9502720 | tf_op jit(solution)/shard_map/dot_general | solution.py:49
  58.7 7.7 %all-to-all-start = ((bf16[16,512,2,8]{1,3,2,0:T(8,128)(2,1)}), bf16[16,512,2,8]{1,3,2,0:T(8,128)(2,1)S(1)}, u32[]{:S(2)}, u32[]{:S(2)}) async-start(bf16[16,512,2,8]{1,3,2,0:T(8,128)(2,1)} %broadcast_select_fusion), calls=%async_computation | async-start | bytes 524288 | tf_op jit(solution)/shard_map/all_to_all | solution.py:72
  67.9 14.9 %all-to-all-done = bf16[16,512,2,8]{1,3,2,0:T(8,128)(2,1)S(1)} async-done(((bf16[16,512,2,8]{1,3,2,0:T(8,128)(2,1)}), bf16[16,512,2,8]{1,3,2,0:T(8,128)(2,1)S(1)}, u32[]{:S(2)}, u32[]{:S(2)}) %all-to-all-start) | async-done | bytes 262176 | tf_op jit(solution)/shard_map/all_to_all | solution.py:72
  83.4 2.9 collective-permute-start.1
  92.3 2.1 collective-permute-start.5
  94.3 4.3 %collective-permute-done.1 = bf16[512,256]{0,1:T(8,128)(2,1)S(1)} collective-permute-done((bf16[512,256]{0,1:T(8,128)(2,1)S(1)}, bf16[512,256]{0,1:T(8,128)(2,1)S(1)}, u32[]{:S(2)}, u32[]{:S(2)}) %collective-permute-start.1) | collective-permute-done | bytes 262176 | tf_op jit(solution)/shard_map/ppermute | solution.py:84
  98.6 3.3 %collective-permute-start.6 = (bf16[512,256]{0,1:T(8,128)(2,1)S(1)}, bf16[512,256]{0,1:T(8,128)(2,1)S(1)}, u32[]{:S(2)}, u32[]{:S(2)}) collective-permute-start(bf16[512,256]{0,1:T(8,128)(2,1)S(1)} %pad_maximum_fusion.1), channel_id=1, source_target_pairs={{0,48},{16,64},{32,80},{48,96},{64,112},{80,128},{96,144},{112,160... | collective-permute-start | bytes 786440 | tf_op jit(solution)/shard_map/ppermute | solution.py:84
  101.9 7.9 %collective-permute-done.2 = bf16[512,256]{0,1:T(8,128)(2,1)S(1)} collective-permute-done((bf16[512,256]{0,1:T(8,128)(2,1)S(1)}, bf16[512,256]{0,1:T(8,128)(2,1)S(1)}, u32[]{:S(2)}, u32[]{:S(2)}) %collective-permute-start.2) | collective-permute-done | bytes 262176 | tf_op jit(solution)/shard_map/ppermute | solution.py:84
  111.8 9.3 %collective-permute-done.3 = bf16[512,256]{0,1:T(8,128)(2,1)S(1)} collective-permute-done((bf16[512,256]{0,1:T(8,128)(2,1)S(1)}, bf16[512,256]{0,1:T(8,128)(2,1)S(1)}, u32[]{:S(2)}, u32[]{:S(2)}) %collective-permute-start.3) | collective-permute-done | bytes 262176 | tf_op jit(solution)/shard_map/ppermute | solution.py:84
  121.1 2.1 collective-permute-start.8
  123.2 9.1 %collective-permute-done.4 = bf16[512,256]{0,1:T(8,128)(2,1)S(1)} collective-permute-done((bf16[512,256]{0,1:T(8,128)(2,1)S(1)}, bf16[512,256]{0,1:T(8,128)(2,1)S(1)}, u32[]{:S(2)}, u32[]{:S(2)}) %collective-permute-start.4) | collective-permute-done | bytes 262176 | tf_op jit(solution)/shard_map/ppermute | solution.py:84
  132.3 7.6 %collective-permute-done.5 = bf16[512,256]{0,1:T(8,128)(2,1)S(1)} collective-permute-done((bf16[512,256]{0,1:T(8,128)(2,1)S(1)}, bf16[512,256]{0,1:T(8,128)(2,1)S(1)}, u32[]{:S(2)}, u32[]{:S(2)}) %collective-permute-start.5) | collective-permute-done | bytes 262176 | tf_op jit(solution)/shard_map/ppermute | solution.py:84
  139.9 5.6 %collective-permute-done.6 = bf16[512,256]{0,1:T(8,128)(2,1)S(1)} collective-permute-done((bf16[512,256]{0,1:T(8,128)(2,1)S(1)}, bf16[512,256]{0,1:T(8,128)(2,1)S(1)}, u32[]{:S(2)}, u32[]{:S(2)}) %collective-permute-start.6) | collective-permute-done | bytes 262176 | tf_op jit(solution)/shard_map/ppermute | solution.py:84
  145.5 5.6 %collective-permute-done.7 = bf16[512,256]{0,1:T(8,128)(2,1)S(1)} collective-permute-done((bf16[512,256]{0,1:T(8,128)(2,1)S(1)}, bf16[512,256]{0,1:T(8,128)(2,1)S(1)}, u32[]{:S(2)}, u32[]{:S(2)}) %collective-permute-start.7) | collective-permute-done | bytes 262176 | tf_op jit(solution)/shard_map/ppermute | solution.py:84
  152.9 5.2 %fusion.35 = (bf16[16,512,256]{2,1,0:T(8,128)(2,1)}, bf16[16,512,256]{2,1,0:T(8,128)(2,1)S(1)}) fusion(bf16[16,512,512]{2,1,0:T(8,128)(2,1)} %bitcast.65), kind=kLoop, calls=%fused_computation.78 | loop fusion | bytes 16777216 | tf_op jit(solution)/shard_map/slice | solution.py:60
  158.1 5.8 %fusion.37 = f32[256,512]{1,0:T(8,128)S(1)} fusion(bf16[8192,256]{1,0:T(8,128)(2,1)S(1)} %bitcast.66, bf16[512,8192]{1,0:T(8,128)(2,1)} %param.8), kind=kOutput, calls=%fused_computation.80 | convolution fusion | flops 2147483648 | bytes 13107200 | tf_op jit(solution)/shard_map/dot_general | solution.py:61
  164.3 17.3 %while.11 = (s32[]{:T(128)}, bf16[4,256,128]{2,1,0:T(8,128)(2,1)S(1)}, s32[4,256]{1,0:T(4,128)S(1)}, s32[4608]{0:T(1024)S(1)}, s32[4,256]{1,0:T(4,128)S(1)}, /*i...) while((s32[]{:T(128)}, ...), condition=%wide.region_6.7_spmd.clone, body=%wide.region_3.6_spmd.clone.sunk | while | flops 625283072 | bytes 16798844 | solution.py:113
  182.5 7.2 %reshape.269 = bf16[4096,512]{1,0:T(8,128)(2,1)} reshape(bf16[16,512,256]{2,1,0:T(8,128)(2,1)} %get-tuple-element.123) | data formatting | bytes 8388608 | tf_op jit(solution)/shard_map/reshape | solution.py:60
  189.6 72.2 %all-gather.7.cloned.1.call-done = bf16[512,4096]{0,1:T(8,128)(2,1)} async-done(((bf16[512,256]{0,1:T(8,128)(2,1)}), bf16[512,4096]{0,1:T(8,128)(2,1)}) %all-gather.7.cloned.1.call-update) | async-done | bytes 4194320 | tf_op jit(solution)/shard_map/all_gather | solution.py:117
  261.8 5.8 %convolution_convert_fusion = bf16[512,512]{1,0:T(8,128)(2,1)S(1)} fusion(bf16[512,4096]{0,1:T(8,128)(2,1)} %all-gather.7.cloned.1.call-done, bf16[4096,512]{1,0:T(8,128)(2,1)} %reshape.269), kind=kOutput, calls=%fused_computation.20 | convolution fusion | flops 2147745792 | bytes 8912896 | tf_op jit(solution)/shard_map/dot_general | solution.py:118
  267.6 25.5 %all_to_all.10 = bf16[16,32,512]{2,1,0:T(8,128)(2,1)S(1)} all-to-all(bf16[16,32,512]{2,1,0:T(8,128)(2,1)S(1)} %bitcast.70), channel_id=1, replica_groups=mesh['ctx'=16,'tp'=16] {'tp'}, dimensions={0} | all-to-all | bytes 1048576 | tf_op jit(solution)/shard_map/all_to_all | solution.py:122
  (88 shorter events, 37.1 us)
Async XLA Ops:
  6.5 44.4 %all-gather.5.cloned.1.call-start = ((), (), s32[]{:S(2)}) async-start(), calls=%async_computation.2 | async-start | bytes 1114112 | tf_op jit(solution)/shard_map/all_gather | solution.py:48
  8.0 144.9 %all-gather.9.cloned.1.call-start = ((), (), s32[]{:S(2)}) async-start(), calls=%async_computation.4 | async-start | bytes 8912896 | tf_op jit(solution)/shard_map/all_gather | solution.py:58
  8.0 24.5 %collective-permute-start = (bf16[256,512]{1,0:T(8,128)(2,1)}, bf16[256,512]{1,0:T(8,128)(2,1)S(1)}, u32[]{:S(2)}, u32[]{:S(2)}) collective-permute-start(bf16[256,512]{1,0:T(8,128)(2,1)} %param.13), channel_id=1, source_target_pairs={{0,0},{1,16},{2,32},{3,48},{4,64},{5,80},{6,96},{7,112},{8,128},{9... | collective-permute-start | bytes 786440 | tf_op jit(solution)/shard_map/ppermute | solution.py:51
  58.7 24.0 %all-to-all-start = ((bf16[16,512,2,8]{1,3,2,0:T(8,128)(2,1)}), bf16[16,512,2,8]{1,3,2,0:T(8,128)(2,1)S(1)}, u32[]{:S(2)}, u32[]{:S(2)}) async-start(bf16[16,512,2,8]{1,3,2,0:T(8,128)(2,1)} %broadcast_select_fusion), calls=%async_computation | async-start | bytes 524288 | tf_op jit(solution)/shard_map/all_to_all | solution.py:72
  66.4 195.4 %all-gather.7.cloned.1.call-start = ((), (), s32[]{:S(2)}) async-start(), calls=%async_computation.3 | async-start | bytes 4456448 | tf_op jit(solution)/shard_map/all_gather | solution.py:117
  83.4 15.2 %collective-permute-start.1 = (bf16[512,256]{0,1:T(8,128)(2,1)S(1)}, bf16[512,256]{0,1:T(8,128)(2,1)S(1)}, u32[]{:S(2)}, u32[]{:S(2)}) collective-permute-start(bf16[512,256]{0,1:T(8,128)(2,1)S(1)} %pad_maximum_fusion.1), channel_id=1, source_target_pairs={{0,128},{16,144},{32,160},{48,176},{64,192},{80,208},{96,224},{112... | collective-permute-start | bytes 786440 | tf_op jit(solution)/shard_map/ppermute | solution.py:84
  86.9 22.9 %collective-permute-start.2 = (bf16[512,256]{0,1:T(8,128)(2,1)S(1)}, bf16[512,256]{0,1:T(8,128)(2,1)S(1)}, u32[]{:S(2)}, u32[]{:S(2)}) collective-permute-start(bf16[512,256]{0,1:T(8,128)(2,1)S(1)} %pad_maximum_fusion.1), channel_id=1, source_target_pairs={{0,112},{16,128},{32,144},{48,160},{64,176},{80,192},{96,208},{112... | collective-permute-start | bytes 786440 | tf_op jit(solution)/shard_map/ppermute | solution.py:84
  88.3 32.8 %collective-permute-start.3 = (bf16[512,256]{0,1:T(8,128)(2,1)S(1)}, bf16[512,256]{0,1:T(8,128)(2,1)S(1)}, u32[]{:S(2)}, u32[]{:S(2)}) collective-permute-start(bf16[512,256]{0,1:T(8,128)(2,1)S(1)} %pad_maximum_fusion.1), channel_id=1, source_target_pairs={{0,96},{16,112},{32,128},{48,144},{64,160},{80,176},{96,192},{112,... | collective-permute-start | bytes 786440 | tf_op jit(solution)/shard_map/ppermute | solution.py:84
  90.3 42.0 %collective-permute-start.4 = (bf16[512,256]{0,1:T(8,128)(2,1)S(1)}, bf16[512,256]{0,1:T(8,128)(2,1)S(1)}, u32[]{:S(2)}, u32[]{:S(2)}) collective-permute-start(bf16[512,256]{0,1:T(8,128)(2,1)S(1)} %pad_maximum_fusion.1), channel_id=1, source_target_pairs={{0,80},{16,96},{32,112},{48,128},{64,144},{80,160},{96,176},{112,1... | collective-permute-start | bytes 786440 | tf_op jit(solution)/shard_map/ppermute | solution.py:84
  92.3 47.7 %collective-permute-start.5 = (bf16[512,256]{0,1:T(8,128)(2,1)S(1)}, bf16[512,256]{0,1:T(8,128)(2,1)S(1)}, u32[]{:S(2)}, u32[]{:S(2)}) collective-permute-start(bf16[512,256]{0,1:T(8,128)(2,1)S(1)} %pad_maximum_fusion.1), channel_id=1, source_target_pairs={{0,64},{16,80},{32,96},{48,112},{64,128},{80,144},{96,160},{112,17... | collective-permute-start | bytes 786440 | tf_op jit(solution)/shard_map/ppermute | solution.py:84
  98.6 46.9 %collective-permute-start.6 = (bf16[512,256]{0,1:T(8,128)(2,1)S(1)}, bf16[512,256]{0,1:T(8,128)(2,1)S(1)}, u32[]{:S(2)}, u32[]{:S(2)}) collective-permute-start(bf16[512,256]{0,1:T(8,128)(2,1)S(1)} %pad_maximum_fusion.1), channel_id=1, source_target_pairs={{0,48},{16,64},{32,80},{48,96},{64,112},{80,128},{96,144},{112,160... | collective-permute-start | bytes 786440 | tf_op jit(solution)/shard_map/ppermute | solution.py:84
  109.8 41.3 %collective-permute-start.7 = (bf16[512,256]{0,1:T(8,128)(2,1)S(1)}, bf16[512,256]{0,1:T(8,128)(2,1)S(1)}, u32[]{:S(2)}, u32[]{:S(2)}) collective-permute-start(bf16[512,256]{0,1:T(8,128)(2,1)S(1)} %pad_maximum_fusion.1), channel_id=1, source_target_pairs={{0,32},{16,48},{32,64},{48,80},{64,96},{80,112},{96,128},{112,144}... | collective-permute-start | bytes 786440 | tf_op jit(solution)/shard_map/ppermute | solution.py:84
  121.1 30.1 %collective-permute-start.8 = (bf16[512,256]{0,1:T(8,128)(2,1)S(1)}, bf16[512,256]{0,1:T(8,128)(2,1)S(1)}, u32[]{:S(2)}, u32[]{:S(2)}) collective-permute-start(bf16[512,256]{0,1:T(8,128)(2,1)S(1)} %pad_maximum_fusion.1), channel_id=1, source_target_pairs={{0,16},{16,32},{32,48},{48,64},{64,80},{80,96},{96,112},{112,128},... | collective-permute-start | bytes 786440 | tf_op jit(solution)/shard_map/ppermute | solution.py:84
  158.1 5.8 %copy-start.1 = (f32[512,64]{0,1:T(8,128)S(1)}, f32[512,64]{0,1:T(8,128)}, u32[]{:S(2)}) copy-start(f32[512,64]{0,1:T(8,128)} %get-tuple-element.133) | copy-start | bytes 393220
  158.1 5.9 %copy-start.2 = (f32[512,64]{0,1:T(8,128)S(1)}, f32[512,64]{0,1:T(8,128)}, u32[]{:S(2)}) copy-start(f32[512,64]{0,1:T(8,128)} %get-tuple-element.134) | copy-start | bytes 393220
  158.1 6.2 %copy-start = (s32[4608]{0:T(1024)S(1)}, s32[4608]{0:T(1024)}, u32[]{:S(2)}) copy-start(s32[4608]{0:T(1024)} %compare_select_fusion) | copy-start | bytes 55300
  158.1 6.2 %copy-start.3 = (bf16[4,256,128]{2,1,0:T(8,128)(2,1)S(1)}, bf16[4,256,128]{2,1,0:T(8,128)(2,1)}, u32[]{:S(2)}) copy-start(bf16[4,256,128]{2,1,0:T(8,128)(2,1)} %custom-call.3) | copy-start | bytes 786436
Sparse Core Ops, SparseCore 0:
  9.1 41.7 all-gather.4
  52.8 83.9 all-gather.8
  182.6 79.2 all-gather.6

commit v7 on v4

--- a/solution.py
+++ b/solution.py
@@ -45,7 +45,13 @@
     q_cols = w_query.shape[1]
     k_cols = w_key.shape[1]
     w_kv = jnp.concatenate([w_key, w_value], axis=1)
-    w_kv_full = lax.all_gather(w_kv, "ctx", axis=0, tiled=True)
+    n_ctx_all = lax.axis_size("ctx")
+    ring = [w_kv]
+    for shift in range(1, n_ctx_all):
+        ring.append(lax.ppermute(w_kv, "ctx", [(i, (i + shift) % n_ctx_all) for i in range(n_ctx_all)]))
+    ring = jnp.stack(ring)
+    sources = (ctx_index - jnp.arange(n_ctx_all, dtype=jnp.int32)) % n_ctx_all
+    w_kv_full = jnp.take(ring, sources, axis=0).reshape(n_ctx_all * tok_rows, w_kv.shape[1])
     kv_local = jnp.dot(tokens, w_kv_full, preferred_element_type=jnp.float32).astype(jnp.bfloat16)
     w_q_full = lax.all_gather(w_query, "ctx", axis=0, tiled=True)
     query_sum = jnp.dot(tokens, w_q_full, preferred_element_type=jnp.float32)
@@ -104,7 +110,6 @@
     attended = attended.reshape(heads_dev, tok_rows, HD)
     attended = jnp.transpose(attended, (1, 0, 2)).reshape(tok_rows, heads_dev * HD)
 
-    n_ctx_all = lax.axis_size("ctx")
     w_moved = lax.ppermute(
         w_output,
         ("ctx", "tp"),

time: 285 us -> 284 us (level)
  waiting for transfers between devices: 164 us -> 134 us
  starting transfers between devices: 32.5 us -> 60.7 us
    all_gather x1 -> x0, waiting for transfers between devices: 33.6 us -> none  [on_device(): w_kv_full = lax.all_gather(w_kv, 'ctx', axis=0, tiled=True)]
    ppermute x0 -> x15, starting transfers between devices: none -> 20.1 us  [on_device(): lax.ppermute(w_kv, 'ctx', [(i, (i + shift) % n_ctx_all) for i in range(n_...]
    ppermute x8, waiting for transfers between devices: 32.1 us -> 44.5 us  [on_device(): lax.ppermute(kv_rows_local, 'ctx', [(i, i + shift) for i in range(n_ctx -...]
    all_gather x1, waiting for transfers between devices: 82.9 us -> 74.1 us  [on_device(): attended_all = lax.all_gather(attended, 'tp', axis=1, tiled=True)]
    all_to_all x1, starting transfers between devices: 7.63 us -> 15.2 us  [on_device(): got = lax.all_to_all(pieces, 'tp', 0, 0, tiled=False)]
    all_to_all x1, waiting for transfers between devices: 14.9 us -> 11.6 us  [on_device(): got = lax.all_to_all(pieces, 'tp', 0, 0, tiled=False)]
    ppermute x0 -> x15, waiting for transfers between devices: none -> 3.04 us  [on_device(): lax.ppermute(w_kv, 'ctx', [(i, (i + shift) % n_ctx_all) for i in range(n_...]
  transfers between devices with their start and end apart: 14 -> 28, of which waited for: 10 -> 10; matrix products, arithmetic and copies ran while one was open for 14% -> 15% of each run, Pallas kernels for 0% -> 0%
where the time goes in v7:
time: 284 us; the launch traced here: 283 us
  waiting for transfers between devices  134 us (47%)
  starting transfers between devices  60.7 us (21%)
  matrix products  30.3 us (11%)
  blocking collectives  25.6 us (9%)
  between operations  13.7 us (5%)
  other arithmetic  11.1 us (4%)
  local copies, waits for them, and re-layouts  7.47 us (3%)
    all_gather x1, waiting for transfers between devices, on_device(): attended_all = lax.all_gather(attended, 'tp', axis=1, tiled=True)  74.1 us
    ppermute x8, waiting for transfers between devices, on_device(): lax.ppermute(kv_rows_local, 'ctx', [(i, i + shift) for i in range(n_ctx -...  44.5 us
    all_to_all x1, blocking collectives, on_device(): got_rows = lax.all_to_all(sent, 'tp', 0, 0, tiled=False)  25.6 us
    ppermute x15, starting transfers between devices, on_device(): lax.ppermute(w_kv, 'ctx', [(i, (i + shift) % n_ctx_all) for i in range(n_...  20.1 us
    all_to_all x1, starting transfers between devices, on_device(): got = lax.all_to_all(pieces, 'tp', 0, 0, tiled=False)  15.2 us
    ppermute x8, starting transfers between devices, on_device(): lax.ppermute(kv_rows_local, 'ctx', [(i, i + shift) for i in range(n_ctx -...  15 us
    all_to_all x1, waiting for transfers between devices, on_device(): got = lax.all_to_all(pieces, 'tp', 0, 0, tiled=False)  11.6 us
    ppermute x1, starting transfers between devices, on_device(): lax.ppermute(w_output, ('ctx', 'tp'), [(c * n_tp + t, t * n_tp + c) for c...  10.3 us
  transfers between devices with their start and end apart: 28, of which 10 were waited for; matrix products, arithmetic and copies ran while one was open for 15% of the time, Pallas kernels for 0%

profile of v7, /device:TPU:6, one launch (start us, length us, event | category | flops | bytes accessed | tf_op | source)
XLA Modules:
  0.0 282.9 jit_solution(1578596560247495090)
XLA Ops:
  10.6 2.4 collective-permute-start.2
  13.0 2.4 collective-permute-start.3
  21.6 2.7 collective-permute-start.9
  27.5 2.1 collective-permute-start.12
  31.9 10.3 %collective-permute-start.23 = (bf16[256,512]{1,0:T(8,128)(2,1)}, bf16[256,512]{1,0:T(8,128)(2,1)S(1)}, u32[]{:S(2)}, u32[]{:S(2)}) collective-permute-start(bf16[256,512]{1,0:T(8,128)(2,1)} %param.13), channel_id=1, source_target_pairs={{0,0},{1,16},{2,32},{3,48},{4,64},{5,80},{6,96},{7,112},{8,128},{9... | collective-permute-start | bytes 786440 | tf_op jit(solution)/shard_map/ppermute | solution.py:113
  44.8 6.2 %fusion.23 = bf16[512,64]{0,1:T(8,128)(2,1)S(1)} fusion(bf16[512,8192]{1,0:T(8,128)(2,1)} %param.8, bf16[8192,64]{0,1:T(8,128)(2,1)S(1)} %bitcast.100, pred[8192]{0:T(1024)(128)(4,1)S(1)} %bitcast.113), kind=kOutput, calls=%fused_computation.23 | convolution fusion | flops 537427968 | bytes 9510912 | tf_op jit(solution)/shard_map/dot_general | solution.py:55
  52.4 15.2 %all-to-all-start = ((bf16[16,512,2,8]{1,3,2,0:T(8,128)(2,1)}), bf16[16,512,2,8]{1,3,2,0:T(8,128)(2,1)S(1)}, u32[]{:S(2)}, u32[]{:S(2)}) async-start(bf16[16,512,2,8]{1,3,2,0:T(8,128)(2,1)} %broadcast_select_fusion), calls=%async_computation | async-start | bytes 524288 | tf_op jit(solution)/shard_map/all_to_all | solution.py:68
  69.0 11.6 %all-to-all-done = bf16[16,512,2,8]{1,3,2,0:T(8,128)(2,1)S(1)} async-done(((bf16[16,512,2,8]{1,3,2,0:T(8,128)(2,1)}), bf16[16,512,2,8]{1,3,2,0:T(8,128)(2,1)S(1)}, u32[]{:S(2)}, u32[]{:S(2)}) %all-to-all-start) | async-done | bytes 262176 | tf_op jit(solution)/shard_map/all_to_all | solution.py:68
  84.7 1.9 collective-permute-start.17
  87.5 1.9 collective-permute-start.18
  89.4 2.7 collective-permute-start.19
  92.1 2.0 collective-permute-start.20
  94.9 2.0 collective-permute-start.21
  97.0 9.4 %collective-permute-done.17 = bf16[512,256]{0,1:T(8,128)(2,1)S(1)} collective-permute-done((bf16[512,256]{0,1:T(8,128)(2,1)S(1)}, bf16[512,256]{0,1:T(8,128)(2,1)S(1)}, u32[]{:S(2)}, u32[]{:S(2)}) %collective-permute-start.17) | collective-permute-done | bytes 262176 | tf_op jit(solution)/shard_map/ppermute | solution.py:80
  106.4 1.9 collective-permute-start.22
  108.3 5.3 %collective-permute-done.18 = bf16[512,256]{0,1:T(8,128)(2,1)S(1)} collective-permute-done((bf16[512,256]{0,1:T(8,128)(2,1)S(1)}, bf16[512,256]{0,1:T(8,128)(2,1)S(1)}, u32[]{:S(2)}, u32[]{:S(2)}) %collective-permute-start.18) | collective-permute-done | bytes 262176 | tf_op jit(solution)/shard_map/ppermute | solution.py:80
  113.6 11.2 %collective-permute-done.19 = bf16[512,256]{0,1:T(8,128)(2,1)S(1)} collective-permute-done((bf16[512,256]{0,1:T(8,128)(2,1)S(1)}, bf16[512,256]{0,1:T(8,128)(2,1)S(1)}, u32[]{:S(2)}, u32[]{:S(2)}) %collective-permute-start.19) | collective-permute-done | bytes 262176 | tf_op jit(solution)/shard_map/ppermute | solution.py:80
  124.8 11.4 %collective-permute-done.20 = bf16[512,256]{0,1:T(8,128)(2,1)S(1)} collective-permute-done((bf16[512,256]{0,1:T(8,128)(2,1)S(1)}, bf16[512,256]{0,1:T(8,128)(2,1)S(1)}, u32[]{:S(2)}, u32[]{:S(2)}) %collective-permute-start.20) | collective-permute-done | bytes 262176 | tf_op jit(solution)/shard_map/ppermute | solution.py:80
  136.2 6.4 %collective-permute-done.21 = bf16[512,256]{0,1:T(8,128)(2,1)S(1)} collective-permute-done((bf16[512,256]{0,1:T(8,128)(2,1)S(1)}, bf16[512,256]{0,1:T(8,128)(2,1)S(1)}, u32[]{:S(2)}, u32[]{:S(2)}) %collective-permute-start.21) | collective-permute-done | bytes 262176 | tf_op jit(solution)/shard_map/ppermute | solution.py:80
  144.5 7.0 %fusion.43 = f32[512,256]{0,1:T(8,128)S(1)} fusion(bf16[512,8192]{1,0:T(8,128)(2,1)} %param.8, bf16[8192,256]{1,0:T(8,128)(2,1)} %all-gather.4.cloned.1.call-done), kind=kOutput, calls=%fused_computation.114 | convolution fusion | flops 2147483648 | bytes 13107200 | tf_op jit(solution)/shard_map/dot_general | solution.py:57
  151.9 17.3 %while.11 = (s32[]{:T(128)}, bf16[4,256,128]{2,1,0:T(8,128)(2,1)S(1)}, s32[4,256]{1,0:T(4,128)S(1)}, s32[4608]{0:T(1024)S(1)}, s32[4,256]{1,0:T(4,128)S(1)}, /*i...) while((s32[]{:T(128)}, ...), condition=%wide.region_6.7_spmd.clone, body=%wide.region_3.6_spmd.clone.sunk | while | flops 625283072 | bytes 16798836 | solution.py:109
  170.0 74.1 %all-gather.6.cloned.1.call-done = bf16[512,4096]{0,1:T(8,128)(2,1)} async-done(((bf16[512,256]{0,1:T(8,128)(2,1)}), bf16[512,4096]{0,1:T(8,128)(2,1)}) %all-gather.6.cloned.1.call-update) | async-done | bytes 4194320 | tf_op jit(solution)/shard_map/all_gather | solution.py:119
  244.2 5.8 %convolution_convert_fusion = bf16[512,512]{1,0:T(8,128)(2,1)S(1)} fusion(bf16[512,4096]{0,1:T(8,128)(2,1)} %all-gather.6.cloned.1.call-done, bf16[4096,512]{1,0:T(8,128)(2,1)} %all-gather.8.cloned.1.call-done), kind=kOutput, calls=%fused_computation.21 | convolution fusion | flops 2147745792 | bytes 8912896 | tf_op jit(solution)/shard_map/dot_general | solution.py:120
  250.0 25.6 %all_to_all.10 = bf16[16,32,512]{2,1,0:T(8,128)(2,1)S(1)} all-to-all(bf16[16,32,512]{2,1,0:T(8,128)(2,1)S(1)} %bitcast.104), channel_id=1, replica_groups=mesh['ctx'=16,'tp'=16] {'tp'}, dimensions={0} | all-to-all | bytes 1048576 | tf_op jit(solution)/shard_map/all_to_all | solution.py:124
  (140 shorter events, 47.6 us)
Async XLA Ops:
  6.5 137.9 %all-gather.4.cloned.1.call-start = ((), (), s32[]{:S(2)}) async-start(), calls=%async_computation.2 | async-start | bytes 4456448 | tf_op jit(solution)/shard_map/all_gather | solution.py:56
  8.8 8.5 %collective-permute-start = (bf16[512,64]{0,1:T(8,128)(2,1)S(1)}, bf16[512,64]{0,1:T(8,128)(2,1)S(1)}, u32[]{:S(2)}, u32[]{:S(2)}) collective-permute-start(bf16[512,64]{0,1:T(8,128)(2,1)S(1)} %constant_dynamic-update-slice_fusion), channel_id=1, source_target_pairs={{0,16},{16,32},{32,48},{48,64},{64,80},{80,96},{96,112},{112,128},... | collective-permute-start | bytes 196616 | tf_op jit(solution)/shard_map/ppermute | solution.py:51
  8.8 9.8 %collective-permute-start.1 = (bf16[512,64]{0,1:T(8,128)(2,1)S(1)}, bf16[512,64]{0,1:T(8,128)(2,1)S(1)}, u32[]{:S(2)}, u32[]{:S(2)}) collective-permute-start(bf16[512,64]{0,1:T(8,128)(2,1)S(1)} %constant_dynamic-update-slice_fusion), channel_id=1, source_target_pairs={{0,32},{16,48},{32,64},{48,80},{64,96},{80,112},{96,128},{112,144}... | collective-permute-start | bytes 196616 | tf_op jit(solution)/shard_map/ppermute | solution.py:51
  10.6 9.3 %collective-permute-start.2 = (bf16[512,64]{0,1:T(8,128)(2,1)S(1)}, bf16[512,64]{0,1:T(8,128)(2,1)S(1)}, u32[]{:S(2)}, u32[]{:S(2)}) collective-permute-start(bf16[512,64]{0,1:T(8,128)(2,1)S(1)} %constant_dynamic-update-slice_fusion), channel_id=1, source_target_pairs={{0,48},{16,64},{32,80},{48,96},{64,112},{80,128},{96,144},{112,160... | collective-permute-start | bytes 196616 | tf_op jit(solution)/shard_map/ppermute | solution.py:51
  13.0 8.4 %collective-permute-start.3 = (bf16[512,64]{0,1:T(8,128)(2,1)S(1)}, bf16[512,64]{0,1:T(8,128)(2,1)S(1)}, u32[]{:S(2)}, u32[]{:S(2)}) collective-permute-start(bf16[512,64]{0,1:T(8,128)(2,1)S(1)} %constant_dynamic-update-slice_fusion), channel_id=1, source_target_pairs={{0,64},{16,80},{32,96},{48,112},{64,128},{80,144},{96,160},{112,17... | collective-permute-start | bytes 196616 | tf_op jit(solution)/shard_map/ppermute | solution.py:51
  21.5 8.2 %collective-permute-start.8 = (bf16[512,64]{0,1:T(8,128)(2,1)S(1)}, bf16[512,64]{0,1:T(8,128)(2,1)S(1)}, u32[]{:S(2)}, u32[]{:S(2)}) collective-permute-start(bf16[512,64]{0,1:T(8,128)(2,1)S(1)} %constant_dynamic-update-slice_fusion), channel_id=1, source_target_pairs={{0,144},{16,160},{32,176},{48,192},{64,208},{80,224},{96,240},{112... | collective-permute-start | bytes 196616 | tf_op jit(solution)/shard_map/ppermute | solution.py:51
  21.6 8.4 %collective-permute-start.9 = (bf16[512,64]{0,1:T(8,128)(2,1)S(1)}, bf16[512,64]{0,1:T(8,128)(2,1)S(1)}, u32[]{:S(2)}, u32[]{:S(2)}) collective-permute-start(bf16[512,64]{0,1:T(8,128)(2,1)S(1)} %constant_dynamic-update-slice_fusion), channel_id=1, source_target_pairs={{0,160},{16,176},{32,192},{48,208},{64,224},{80,240},{96,0},{112,1... | collective-permute-start | bytes 196616 | tf_op jit(solution)/shard_map/ppermute | solution.py:51
  24.3 7.6 %collective-permute-start.10 = (bf16[512,64]{0,1:T(8,128)(2,1)S(1)}, bf16[512,64]{0,1:T(8,128)(2,1)S(1)}, u32[]{:S(2)}, u32[]{:S(2)}) collective-permute-start(bf16[512,64]{0,1:T(8,128)(2,1)S(1)} %constant_dynamic-update-slice_fusion), channel_id=1, source_target_pairs={{0,176},{16,192},{32,208},{48,224},{64,240},{80,0},{96,16},{112,32... | collective-permute-start | bytes 196616 | tf_op jit(solution)/shard_map/ppermute | solution.py:51
  25.8 16.4 %collective-permute-start.11 = (bf16[512,64]{0,1:T(8,128)(2,1)S(1)}, bf16[512,64]{0,1:T(8,128)(2,1)S(1)}, u32[]{:S(2)}, u32[]{:S(2)}) collective-permute-start(bf16[512,64]{0,1:T(8,128)(2,1)S(1)} %constant_dynamic-update-slice_fusion), channel_id=1, source_target_pairs={{0,192},{16,208},{32,224},{48,240},{64,0},{80,16},{96,32},{112,48}... | collective-permute-start | bytes 196616 | tf_op jit(solution)/shard_map/ppermute | solution.py:51
  27.5 14.8 %collective-permute-start.12 = (bf16[512,64]{0,1:T(8,128)(2,1)S(1)}, bf16[512,64]{0,1:T(8,128)(2,1)S(1)}, u32[]{:S(2)}, u32[]{:S(2)}) collective-permute-start(bf16[512,64]{0,1:T(8,128)(2,1)S(1)} %constant_dynamic-update-slice_fusion), channel_id=1, source_target_pairs={{0,208},{16,224},{32,240},{48,0},{64,16},{80,32},{96,48},{112,64},... | collective-permute-start | bytes 196616 | tf_op jit(solution)/shard_map/ppermute | solution.py:51
  29.6 14.4 %collective-permute-start.13 = (bf16[512,64]{0,1:T(8,128)(2,1)S(1)}, bf16[512,64]{0,1:T(8,128)(2,1)S(1)}, u32[]{:S(2)}, u32[]{:S(2)}) collective-permute-start(bf16[512,64]{0,1:T(8,128)(2,1)S(1)} %constant_dynamic-update-slice_fusion), channel_id=1, source_target_pairs={{0,224},{16,240},{32,0},{48,16},{64,32},{80,48},{96,64},{112,80},{... | collective-permute-start | bytes 196616 | tf_op jit(solution)/shard_map/ppermute | solution.py:51
  30.0 14.1 %collective-permute-start.14 = (bf16[512,64]{0,1:T(8,128)(2,1)S(1)}, bf16[512,64]{0,1:T(8,128)(2,1)S(1)}, u32[]{:S(2)}, u32[]{:S(2)}) collective-permute-start(bf16[512,64]{0,1:T(8,128)(2,1)S(1)} %constant_dynamic-update-slice_fusion), channel_id=1, source_target_pairs={{0,240},{16,0},{32,16},{48,32},{64,48},{80,64},{96,80},{112,96},{1... | collective-permute-start | bytes 196616 | tf_op jit(solution)/shard_map/ppermute | solution.py:51
  31.9 54.7 %collective-permute-start.23 = (bf16[256,512]{1,0:T(8,128)(2,1)}, bf16[256,512]{1,0:T(8,128)(2,1)S(1)}, u32[]{:S(2)}, u32[]{:S(2)}) collective-permute-start(bf16[256,512]{1,0:T(8,128)(2,1)} %param.13), channel_id=1, source_target_pairs={{0,0},{1,16},{2,32},{3,48},{4,64},{5,80},{6,96},{7,112},{8,128},{9... | collective-permute-start | bytes 786440 | tf_op jit(solution)/shard_map/ppermute | solution.py:113
  52.4 28.3 %all-to-all-start = ((bf16[16,512,2,8]{1,3,2,0:T(8,128)(2,1)}), bf16[16,512,2,8]{1,3,2,0:T(8,128)(2,1)S(1)}, u32[]{:S(2)}, u32[]{:S(2)}) async-start(bf16[16,512,2,8]{1,3,2,0:T(8,128)(2,1)} %broadcast_select_fusion), calls=%async_computation | async-start | bytes 524288 | tf_op jit(solution)/shard_map/all_to_all | solution.py:68
  67.6 102.5 %all-gather.8.cloned.1.call-start = ((), (), s32[]{:S(2)}) async-start(), calls=%async_computation.4 | async-start | bytes 4456448 | tf_op jit(solution)/shard_map/all_gather | solution.py:118
  81.3 10.8 %collective-permute-start.15 = (bf16[512,256]{0,1:T(8,128)(2,1)S(1)}, bf16[512,256]{0,1:T(8,128)(2,1)S(1)}, u32[]{:S(2)}, u32[]{:S(2)}) collective-permute-start(bf16[512,256]{0,1:T(8,128)(2,1)S(1)} %pad_maximum_fusion), channel_id=1, source_target_pairs={{0,128},{16,144},{32,160},{48,176},{64,192},{80,208},{96,224},{112... | collective-permute-start | bytes 786440 | tf_op jit(solution)/shard_map/ppermute | solution.py:80
  83.3 11.7 %collective-permute-start.16 = (bf16[512,256]{0,1:T(8,128)(2,1)S(1)}, bf16[512,256]{0,1:T(8,128)(2,1)S(1)}, u32[]{:S(2)}, u32[]{:S(2)}) collective-permute-start(bf16[512,256]{0,1:T(8,128)(2,1)S(1)} %pad_maximum_fusion), channel_id=1, source_target_pairs={{0,112},{16,128},{32,144},{48,160},{64,176},{80,192},{96,208},{112... | collective-permute-start | bytes 786440 | tf_op jit(solution)/shard_map/ppermute | solution.py:80
  84.7 21.7 %collective-permute-start.17 = (bf16[512,256]{0,1:T(8,128)(2,1)S(1)}, bf16[512,256]{0,1:T(8,128)(2,1)S(1)}, u32[]{:S(2)}, u32[]{:S(2)}) collective-permute-start(bf16[512,256]{0,1:T(8,128)(2,1)S(1)} %pad_maximum_fusion), channel_id=1, source_target_pairs={{0,96},{16,112},{32,128},{48,144},{64,160},{80,176},{96,192},{112,... | collective-permute-start | bytes 786440 | tf_op jit(solution)/shard_map/ppermute | solution.py:80
  87.4 156.7 %all-gather.6.cloned.1.call-start = ((), (), s32[]{:S(2)}) async-start(), calls=%async_computation.3 | async-start | bytes 4456448 | tf_op jit(solution)/shard_map/all_gather | solution.py:119
  87.5 26.1 %collective-permute-start.18 = (bf16[512,256]{0,1:T(8,128)(2,1)S(1)}, bf16[512,256]{0,1:T(8,128)(2,1)S(1)}, u32[]{:S(2)}, u32[]{:S(2)}) collective-permute-start(bf16[512,256]{0,1:T(8,128)(2,1)S(1)} %pad_maximum_fusion), channel_id=1, source_target_pairs={{0,80},{16,96},{32,112},{48,128},{64,144},{80,160},{96,176},{112,1... | collective-permute-start | bytes 786440 | tf_op jit(solution)/shard_map/ppermute | solution.py:80
  89.4 35.4 %collective-permute-start.19 = (bf16[512,256]{0,1:T(8,128)(2,1)S(1)}, bf16[512,256]{0,1:T(8,128)(2,1)S(1)}, u32[]{:S(2)}, u32[]{:S(2)}) collective-permute-start(bf16[512,256]{0,1:T(8,128)(2,1)S(1)} %pad_maximum_fusion), channel_id=1, source_target_pairs={{0,64},{16,80},{32,96},{48,112},{64,128},{80,144},{96,160},{112,17... | collective-permute-start | bytes 786440 | tf_op jit(solution)/shard_map/ppermute | solution.py:80
  92.1 44.1 %collective-permute-start.20 = (bf16[512,256]{0,1:T(8,128)(2,1)S(1)}, bf16[512,256]{0,1:T(8,128)(2,1)S(1)}, u32[]{:S(2)}, u32[]{:S(2)}) collective-permute-start(bf16[512,256]{0,1:T(8,128)(2,1)S(1)} %pad_maximum_fusion), channel_id=1, source_target_pairs={{0,48},{16,64},{32,80},{48,96},{64,112},{80,128},{96,144},{112,160... | collective-permute-start | bytes 786440 | tf_op jit(solution)/shard_map/ppermute | solution.py:80
  94.9 47.8 %collective-permute-start.21 = (bf16[512,256]{0,1:T(8,128)(2,1)S(1)}, bf16[512,256]{0,1:T(8,128)(2,1)S(1)}, u32[]{:S(2)}, u32[]{:S(2)}) collective-permute-start(bf16[512,256]{0,1:T(8,128)(2,1)S(1)} %pad_maximum_fusion), channel_id=1, source_target_pairs={{0,32},{16,48},{32,64},{48,80},{64,96},{80,112},{96,128},{112,144}... | collective-permute-start | bytes 786440 | tf_op jit(solution)/shard_map/ppermute | solution.py:80
  106.4 36.3 %collective-permute-start.22 = (bf16[512,256]{0,1:T(8,128)(2,1)S(1)}, bf16[512,256]{0,1:T(8,128)(2,1)S(1)}, u32[]{:S(2)}, u32[]{:S(2)}) collective-permute-start(bf16[512,256]{0,1:T(8,128)(2,1)S(1)} %pad_maximum_fusion), channel_id=1, source_target_pairs={{0,16},{16,32},{32,48},{48,64},{64,80},{80,96},{96,112},{112,128},... | collective-permute-start | bytes 786440 | tf_op jit(solution)/shard_map/ppermute | solution.py:80
  (9 other events, 57.8 us)
Sparse Core Ops, SparseCore 0:
  9.2 57.2 all-gather.3
  87.5 52.1 all-gather.7
  170.1 73.9 all-gather.5

commit v8 on v7

--- a/solution.py
+++ b/solution.py
@@ -71,6 +71,7 @@
     value_own = kv_own[:, 1, :]
     key_rot = rotate(key_raw.astype(jnp.float32)[:, None, :], positions)[:, 0, :].astype(jnp.bfloat16)
     kv_rows_local = jnp.concatenate([key_rot, value_own], axis=1)
+    kv_rows_local, query = lax.optimization_barrier((kv_rows_local, query))
 
     n_ctx = lax.axis_size("ctx")
     back = min(n_ctx - 1, -(-(DOC_MOST - 1) // tok_rows))

time: 284 us -> 290 us (1.021)
  matrix products: 30.3 us -> 36 us
    dot_general x4, matrix products: 5.41 us -> 8.8 us  [one_part(): jnp.dot(q_part, key_win.T, preferred_element_type=jnp.float32) * score_scale]
  transfers between devices with their start and end apart: 28 -> 28, of which waited for: 10 -> 9; matrix products, arithmetic and copies ran while one was open for 15% -> 17% of each run, Pallas kernels for 0% -> 0%
where the time goes in v8:
time: 290 us; the launch traced here: 289 us
  waiting for transfers between devices  133 us (46%)
  starting transfers between devices  61.7 us (21%)
  matrix products  36 us (12%)
  blocking collectives  25.8 us (9%)
  between operations  13.6 us (5%)
  other arithmetic  10.2 us (4%)
  local copies, waits for them, and re-layouts  9.11 us (3%)
    all_gather x1, waiting for transfers between devices, on_device(): attended_all = lax.all_gather(attended, 'tp', axis=1, tiled=True)  74.1 us
    ppermute x8, waiting for transfers between devices, on_device(): lax.ppermute(kv_rows_local, 'ctx', [(i, i + shift) for i in range(n_ctx -...  42.6 us
    all_to_all x1, blocking collectives, on_device(): got_rows = lax.all_to_all(sent, 'tp', 0, 0, tiled=False)  25.8 us
    ppermute x15, starting transfers between devices, on_device(): lax.ppermute(w_kv, 'ctx', [(i, (i + shift) % n_ctx_all) for i in range(n_...  20.1 us
    ppermute x8, starting transfers between devices, on_device(): lax.ppermute(kv_rows_local, 'ctx', [(i, i + shift) for i in range(n_ctx -...  16 us
    all_to_all x1, starting transfers between devices, on_device(): got = lax.all_to_all(pieces, 'tp', 0, 0, tiled=False)  15.2 us
    all_to_all x1, waiting for transfers between devices, on_device(): got = lax.all_to_all(pieces, 'tp', 0, 0, tiled=False)  12.4 us
    ppermute x1, starting transfers between devices, on_device(): lax.ppermute(w_output, ('ctx', 'tp'), [(c * n_tp + t, t * n_tp + c) for c...  10.3 us
  transfers between devices with their start and end apart: 28, of which 9 were waited for; matrix products, arithmetic and copies ran while one was open for 17% of the time, Pallas kernels for 0%

profile of v8, /device:TPU:6, one launch (start us, length us, event | category | flops | bytes accessed | tf_op | source)
XLA Modules:
  0.0 289.4 jit_solution(6151530702643819809)
XLA Ops:
  10.6 2.4 collective-permute-start.2
  13.0 2.4 collective-permute-start.3
  21.6 2.7 collective-permute-start.9
  31.9 10.3 %collective-permute-start.23 = (bf16[256,512]{1,0:T(8,128)(2,1)}, bf16[256,512]{1,0:T(8,128)(2,1)S(1)}, u32[]{:S(2)}, u32[]{:S(2)}) collective-permute-start(bf16[256,512]{1,0:T(8,128)(2,1)} %param.13), channel_id=1, source_target_pairs={{0,0},{1,16},{2,32},{3,48},{4,64},{5,80},{6,96},{7,112},{8,128},{9... | collective-permute-start | bytes 786440 | tf_op jit(solution)/shard_map/ppermute | solution.py:114
  44.8 6.2 %fusion.23 = bf16[512,64]{0,1:T(8,128)(2,1)S(1)} fusion(bf16[512,8192]{1,0:T(8,128)(2,1)} %param.8, bf16[8192,64]{0,1:T(8,128)(2,1)S(1)} %bitcast.99, pred[8192]{0:T(1024)(128)(4,1)S(1)} %bitcast.113), kind=kOutput, calls=%fused_computation.23 | convolution fusion | flops 537427968 | bytes 9510912 | tf_op jit(solution)/shard_map/dot_general | solution.py:55
  52.4 15.2 %all-to-all-start = ((bf16[16,512,2,8]{1,3,2,0:T(8,128)(2,1)}), bf16[16,512,2,8]{1,3,2,0:T(8,128)(2,1)S(1)}, u32[]{:S(2)}, u32[]{:S(2)}) async-start(bf16[16,512,2,8]{1,3,2,0:T(8,128)(2,1)} %broadcast_select_fusion), calls=%async_computation | async-start | bytes 524288 | tf_op jit(solution)/shard_map/all_to_all | solution.py:68
  68.3 12.4 %all-to-all-done = bf16[16,512,2,8]{1,3,2,0:T(8,128)(2,1)S(1)} async-done(((bf16[16,512,2,8]{1,3,2,0:T(8,128)(2,1)}), bf16[16,512,2,8]{1,3,2,0:T(8,128)(2,1)S(1)}, u32[]{:S(2)}, u32[]{:S(2)}) %all-to-all-start) | async-done | bytes 262176 | tf_op jit(solution)/shard_map/all_to_all | solution.py:68
  81.4 6.9 %fusion.43 = f32[512,256]{0,1:T(8,128)S(1)} fusion(bf16[512,8192]{1,0:T(8,128)(2,1)} %param.8, bf16[8192,256]{1,0:T(8,128)(2,1)} %all-gather.4.cloned.1.call-done), kind=kOutput, calls=%fused_computation.114 | convolution fusion | flops 2147483648 | bytes 13107200 | tf_op jit(solution)/shard_map/dot_general | solution.py:57
  96.5 2.7 collective-permute-start.19
  102.1 2.8 collective-permute-start.21
  104.9 8.6 %collective-permute-done.17 = bf16[512,256]{0,1:T(8,128)(2,1)S(1)} collective-permute-done((bf16[512,256]{0,1:T(8,128)(2,1)S(1)}, bf16[512,256]{0,1:T(8,128)(2,1)S(1)}, u32[]{:S(2)}, u32[]{:S(2)}) %collective-permute-start.17) | collective-permute-done | bytes 262176 | tf_op jit(solution)/shard_map/ppermute | solution.py:81
  113.5 2.1 collective-permute-start.22
  115.7 5.0 %collective-permute-done.18 = bf16[512,256]{0,1:T(8,128)(2,1)S(1)} collective-permute-done((bf16[512,256]{0,1:T(8,128)(2,1)S(1)}, bf16[512,256]{0,1:T(8,128)(2,1)S(1)}, u32[]{:S(2)}, u32[]{:S(2)}) %collective-permute-start.18) | collective-permute-done | bytes 262176 | tf_op jit(solution)/shard_map/ppermute | solution.py:81
  120.7 11.3 %collective-permute-done.19 = bf16[512,256]{0,1:T(8,128)(2,1)S(1)} collective-permute-done((bf16[512,256]{0,1:T(8,128)(2,1)S(1)}, bf16[512,256]{0,1:T(8,128)(2,1)S(1)}, u32[]{:S(2)}, u32[]{:S(2)}) %collective-permute-start.19) | collective-permute-done | bytes 262176 | tf_op jit(solution)/shard_map/ppermute | solution.py:81
  132.0 11.2 %collective-permute-done.20 = bf16[512,256]{0,1:T(8,128)(2,1)S(1)} collective-permute-done((bf16[512,256]{0,1:T(8,128)(2,1)S(1)}, bf16[512,256]{0,1:T(8,128)(2,1)S(1)}, u32[]{:S(2)}, u32[]{:S(2)}) %collective-permute-start.20) | collective-permute-done | bytes 262176 | tf_op jit(solution)/shard_map/ppermute | solution.py:81
  143.3 6.5 %collective-permute-done.21 = bf16[512,256]{0,1:T(8,128)(2,1)S(1)} collective-permute-done((bf16[512,256]{0,1:T(8,128)(2,1)S(1)}, bf16[512,256]{0,1:T(8,128)(2,1)S(1)}, u32[]{:S(2)}, u32[]{:S(2)}) %collective-permute-start.21) | collective-permute-done | bytes 262176 | tf_op jit(solution)/shard_map/ppermute | solution.py:81
  151.5 22.9 %while.11 = (s32[]{:T(128)}, bf16[4,256,128]{2,1,0:T(8,128)(2,1)}, s32[4,256]{1,0:T(4,128)S(1)}, s32[4608]{0:T(1024)}, s32[4,256]{1,0:T(4,128)S(1)}, /*index=5*/...) while((s32[]{:T(128)}, bf16[4,256,128]{2,1,0:T(8,128)(2,1)}, ...), condition=%wide.region_6.7_spmd.clone, body=%wide.region_3.6_spmd.clone.sunk | while | flops 625283072 | bytes 16867464 | solution.py:110
  151.6 2.2 fusion.61
  157.3 2.2 fusion.61
  163.0 2.2 fusion.61
  168.7 2.2 fusion.61
  176.3 74.1 %all-gather.6.cloned.1.call-done = bf16[512,4096]{0,1:T(8,128)(2,1)} async-done(((bf16[512,256]{0,1:T(8,128)(2,1)}), bf16[512,4096]{0,1:T(8,128)(2,1)}) %all-gather.6.cloned.1.call-update) | async-done | bytes 4194320 | tf_op jit(solution)/shard_map/all_gather | solution.py:120
  250.4 5.8 %convolution_convert_fusion = bf16[512,512]{1,0:T(8,128)(2,1)S(1)} fusion(bf16[512,4096]{0,1:T(8,128)(2,1)} %all-gather.6.cloned.1.call-done, bf16[4096,512]{1,0:T(8,128)(2,1)} %all-gather.8.cloned.1.call-done), kind=kOutput, calls=%fused_computation.21 | convolution fusion | flops 2147745792 | bytes 8912896 | tf_op jit(solution)/shard_map/dot_general | solution.py:121
  256.2 25.8 %all_to_all.10 = bf16[16,32,512]{2,1,0:T(8,128)(2,1)S(1)} all-to-all(bf16[16,32,512]{2,1,0:T(8,128)(2,1)S(1)} %bitcast.104), channel_id=1, replica_groups=mesh['ctx'=16,'tp'=16] {'tp'}, dimensions={0} | all-to-all | bytes 1048576 | tf_op jit(solution)/shard_map/all_to_all | solution.py:125
  (140 shorter events, 52.4 us)
Async XLA Ops:
  6.5 74.8 %all-gather.4.cloned.1.call-start = ((), (), s32[]{:S(2)}) async-start(), calls=%async_computation.2 | async-start | bytes 4456448 | tf_op jit(solution)/shard_map/all_gather | solution.py:56
  8.8 8.5 %collective-permute-start = (bf16[512,64]{0,1:T(8,128)(2,1)S(1)}, bf16[512,64]{0,1:T(8,128)(2,1)S(1)}, u32[]{:S(2)}, u32[]{:S(2)}) collective-permute-start(bf16[512,64]{0,1:T(8,128)(2,1)S(1)} %constant_dynamic-update-slice_fusion), channel_id=1, source_target_pairs={{0,16},{16,32},{32,48},{48,64},{64,80},{80,96},{96,112},{112,128},... | collective-permute-start | bytes 196616 | tf_op jit(solution)/shard_map/ppermute | solution.py:51
  8.8 9.8 %collective-permute-start.1 = (bf16[512,64]{0,1:T(8,128)(2,1)S(1)}, bf16[512,64]{0,1:T(8,128)(2,1)S(1)}, u32[]{:S(2)}, u32[]{:S(2)}) collective-permute-start(bf16[512,64]{0,1:T(8,128)(2,1)S(1)} %constant_dynamic-update-slice_fusion), channel_id=1, source_target_pairs={{0,32},{16,48},{32,64},{48,80},{64,96},{80,112},{96,128},{112,144}... | collective-permute-start | bytes 196616 | tf_op jit(solution)/shard_map/ppermute | solution.py:51
  10.6 9.3 %collective-permute-start.2 = (bf16[512,64]{0,1:T(8,128)(2,1)S(1)}, bf16[512,64]{0,1:T(8,128)(2,1)S(1)}, u32[]{:S(2)}, u32[]{:S(2)}) collective-permute-start(bf16[512,64]{0,1:T(8,128)(2,1)S(1)} %constant_dynamic-update-slice_fusion), channel_id=1, source_target_pairs={{0,48},{16,64},{32,80},{48,96},{64,112},{80,128},{96,144},{112,160... | collective-permute-start | bytes 196616 | tf_op jit(solution)/shard_map/ppermute | solution.py:51
  13.0 8.4 %collective-permute-start.3 = (bf16[512,64]{0,1:T(8,128)(2,1)S(1)}, bf16[512,64]{0,1:T(8,128)(2,1)S(1)}, u32[]{:S(2)}, u32[]{:S(2)}) collective-permute-start(bf16[512,64]{0,1:T(8,128)(2,1)S(1)} %constant_dynamic-update-slice_fusion), channel_id=1, source_target_pairs={{0,64},{16,80},{32,96},{48,112},{64,128},{80,144},{96,160},{112,17... | collective-permute-start | bytes 196616 | tf_op jit(solution)/shard_map/ppermute | solution.py:51
  21.5 8.2 %collective-permute-start.8 = (bf16[512,64]{0,1:T(8,128)(2,1)S(1)}, bf16[512,64]{0,1:T(8,128)(2,1)S(1)}, u32[]{:S(2)}, u32[]{:S(2)}) collective-permute-start(bf16[512,64]{0,1:T(8,128)(2,1)S(1)} %constant_dynamic-update-slice_fusion), channel_id=1, source_target_pairs={{0,144},{16,160},{32,176},{48,192},{64,208},{80,224},{96,240},{112... | collective-permute-start | bytes 196616 | tf_op jit(solution)/shard_map/ppermute | solution.py:51
  21.6 8.4 %collective-permute-start.9 = (bf16[512,64]{0,1:T(8,128)(2,1)S(1)}, bf16[512,64]{0,1:T(8,128)(2,1)S(1)}, u32[]{:S(2)}, u32[]{:S(2)}) collective-permute-start(bf16[512,64]{0,1:T(8,128)(2,1)S(1)} %constant_dynamic-update-slice_fusion), channel_id=1, source_target_pairs={{0,160},{16,176},{32,192},{48,208},{64,224},{80,240},{96,0},{112,1... | collective-permute-start | bytes 196616 | tf_op jit(solution)/shard_map/ppermute | solution.py:51
  24.3 7.6 %collective-permute-start.10 = (bf16[512,64]{0,1:T(8,128)(2,1)S(1)}, bf16[512,64]{0,1:T(8,128)(2,1)S(1)}, u32[]{:S(2)}, u32[]{:S(2)}) collective-permute-start(bf16[512,64]{0,1:T(8,128)(2,1)S(1)} %constant_dynamic-update-slice_fusion), channel_id=1, source_target_pairs={{0,176},{16,192},{32,208},{48,224},{64,240},{80,0},{96,16},{112,32... | collective-permute-start | bytes 196616 | tf_op jit(solution)/shard_map/ppermute | solution.py:51
  25.8 16.4 %collective-permute-start.11 = (bf16[512,64]{0,1:T(8,128)(2,1)S(1)}, bf16[512,64]{0,1:T(8,128)(2,1)S(1)}, u32[]{:S(2)}, u32[]{:S(2)}) collective-permute-start(bf16[512,64]{0,1:T(8,128)(2,1)S(1)} %constant_dynamic-update-slice_fusion), channel_id=1, source_target_pairs={{0,192},{16,208},{32,224},{48,240},{64,0},{80,16},{96,32},{112,48}... | collective-permute-start | bytes 196616 | tf_op jit(solution)/shard_map/ppermute | solution.py:51
  27.5 14.8 %collective-permute-start.12 = (bf16[512,64]{0,1:T(8,128)(2,1)S(1)}, bf16[512,64]{0,1:T(8,128)(2,1)S(1)}, u32[]{:S(2)}, u32[]{:S(2)}) collective-permute-start(bf16[512,64]{0,1:T(8,128)(2,1)S(1)} %constant_dynamic-update-slice_fusion), channel_id=1, source_target_pairs={{0,208},{16,224},{32,240},{48,0},{64,16},{80,32},{96,48},{112,64},... | collective-permute-start | bytes 196616 | tf_op jit(solution)/shard_map/ppermute | solution.py:51
  29.6 14.4 %collective-permute-start.13 = (bf16[512,64]{0,1:T(8,128)(2,1)S(1)}, bf16[512,64]{0,1:T(8,128)(2,1)S(1)}, u32[]{:S(2)}, u32[]{:S(2)}) collective-permute-start(bf16[512,64]{0,1:T(8,128)(2,1)S(1)} %constant_dynamic-update-slice_fusion), channel_id=1, source_target_pairs={{0,224},{16,240},{32,0},{48,16},{64,32},{80,48},{96,64},{112,80},{... | collective-permute-start | bytes 196616 | tf_op jit(solution)/shard_map/ppermute | solution.py:51
  30.0 14.1 %collective-permute-start.14 = (bf16[512,64]{0,1:T(8,128)(2,1)S(1)}, bf16[512,64]{0,1:T(8,128)(2,1)S(1)}, u32[]{:S(2)}, u32[]{:S(2)}) collective-permute-start(bf16[512,64]{0,1:T(8,128)(2,1)S(1)} %constant_dynamic-update-slice_fusion), channel_id=1, source_target_pairs={{0,240},{16,0},{32,16},{48,32},{64,48},{80,64},{96,80},{112,96},{1... | collective-permute-start | bytes 196616 | tf_op jit(solution)/shard_map/ppermute | solution.py:51
  31.9 61.8 %collective-permute-start.23 = (bf16[256,512]{1,0:T(8,128)(2,1)}, bf16[256,512]{1,0:T(8,128)(2,1)S(1)}, u32[]{:S(2)}, u32[]{:S(2)}) collective-permute-start(bf16[256,512]{1,0:T(8,128)(2,1)} %param.13), channel_id=1, source_target_pairs={{0,0},{1,16},{2,32},{3,48},{4,64},{5,80},{6,96},{7,112},{8,128},{9... | collective-permute-start | bytes 786440 | tf_op jit(solution)/shard_map/ppermute | solution.py:114
  52.4 28.3 %all-to-all-start = ((bf16[16,512,2,8]{1,3,2,0:T(8,128)(2,1)}), bf16[16,512,2,8]{1,3,2,0:T(8,128)(2,1)S(1)}, u32[]{:S(2)}, u32[]{:S(2)}) async-start(bf16[16,512,2,8]{1,3,2,0:T(8,128)(2,1)} %broadcast_select_fusion), calls=%async_computation | async-start | bytes 524288 | tf_op jit(solution)/shard_map/all_to_all | solution.py:68
  67.6 108.7 %all-gather.8.cloned.1.call-start = ((), (), s32[]{:S(2)}) async-start(), calls=%async_computation.4 | async-start | bytes 4456448 | tf_op jit(solution)/shard_map/all_gather | solution.py:119
  88.4 11.6 %collective-permute-start.15 = (bf16[512,256]{0,1:T(8,128)(2,1)S(1)}, bf16[512,256]{0,1:T(8,128)(2,1)S(1)}, u32[]{:S(2)}, u32[]{:S(2)}) collective-permute-start(bf16[512,256]{0,1:T(8,128)(2,1)S(1)} %pad_maximum_fusion), channel_id=1, source_target_pairs={{0,128},{16,144},{32,160},{48,176},{64,192},{80,208},{96,224},{112... | collective-permute-start | bytes 786440 | tf_op jit(solution)/shard_map/ppermute | solution.py:81
  90.4 11.7 %collective-permute-start.16 = (bf16[512,256]{0,1:T(8,128)(2,1)S(1)}, bf16[512,256]{0,1:T(8,128)(2,1)S(1)}, u32[]{:S(2)}, u32[]{:S(2)}) collective-permute-start(bf16[512,256]{0,1:T(8,128)(2,1)S(1)} %pad_maximum_fusion), channel_id=1, source_target_pairs={{0,112},{16,128},{32,144},{48,160},{64,176},{80,192},{96,208},{112... | collective-permute-start | bytes 786440 | tf_op jit(solution)/shard_map/ppermute | solution.py:81
  91.8 21.7 %collective-permute-start.17 = (bf16[512,256]{0,1:T(8,128)(2,1)S(1)}, bf16[512,256]{0,1:T(8,128)(2,1)S(1)}, u32[]{:S(2)}, u32[]{:S(2)}) collective-permute-start(bf16[512,256]{0,1:T(8,128)(2,1)S(1)} %pad_maximum_fusion), channel_id=1, source_target_pairs={{0,96},{16,112},{32,128},{48,144},{64,160},{80,176},{96,192},{112,... | collective-permute-start | bytes 786440 | tf_op jit(solution)/shard_map/ppermute | solution.py:81
  94.5 155.9 %all-gather.6.cloned.1.call-start = ((), (), s32[]{:S(2)}) async-start(), calls=%async_computation.3 | async-start | bytes 4456448 | tf_op jit(solution)/shard_map/all_gather | solution.py:120
  94.6 26.1 %collective-permute-start.18 = (bf16[512,256]{0,1:T(8,128)(2,1)S(1)}, bf16[512,256]{0,1:T(8,128)(2,1)S(1)}, u32[]{:S(2)}, u32[]{:S(2)}) collective-permute-start(bf16[512,256]{0,1:T(8,128)(2,1)S(1)} %pad_maximum_fusion), channel_id=1, source_target_pairs={{0,80},{16,96},{32,112},{48,128},{64,144},{80,160},{96,176},{112,1... | collective-permute-start | bytes 786440 | tf_op jit(solution)/shard_map/ppermute | solution.py:81
  96.5 35.5 %collective-permute-start.19 = (bf16[512,256]{0,1:T(8,128)(2,1)S(1)}, bf16[512,256]{0,1:T(8,128)(2,1)S(1)}, u32[]{:S(2)}, u32[]{:S(2)}) collective-permute-start(bf16[512,256]{0,1:T(8,128)(2,1)S(1)} %pad_maximum_fusion), channel_id=1, source_target_pairs={{0,64},{16,80},{32,96},{48,112},{64,128},{80,144},{96,160},{112,17... | collective-permute-start | bytes 786440 | tf_op jit(solution)/shard_map/ppermute | solution.py:81
  100.0 43.2 %collective-permute-start.20 = (bf16[512,256]{0,1:T(8,128)(2,1)S(1)}, bf16[512,256]{0,1:T(8,128)(2,1)S(1)}, u32[]{:S(2)}, u32[]{:S(2)}) collective-permute-start(bf16[512,256]{0,1:T(8,128)(2,1)S(1)} %pad_maximum_fusion), channel_id=1, source_target_pairs={{0,48},{16,64},{32,80},{48,96},{64,112},{80,128},{96,144},{112,160... | collective-permute-start | bytes 786440 | tf_op jit(solution)/shard_map/ppermute | solution.py:81
  102.1 47.7 %collective-permute-start.21 = (bf16[512,256]{0,1:T(8,128)(2,1)S(1)}, bf16[512,256]{0,1:T(8,128)(2,1)S(1)}, u32[]{:S(2)}, u32[]{:S(2)}) collective-permute-start(bf16[512,256]{0,1:T(8,128)(2,1)S(1)} %pad_maximum_fusion), channel_id=1, source_target_pairs={{0,32},{16,48},{32,64},{48,80},{64,96},{80,112},{96,128},{112,144}... | collective-permute-start | bytes 786440 | tf_op jit(solution)/shard_map/ppermute | solution.py:81
  113.5 36.3 %collective-permute-start.22 = (bf16[512,256]{0,1:T(8,128)(2,1)S(1)}, bf16[512,256]{0,1:T(8,128)(2,1)S(1)}, u32[]{:S(2)}, u32[]{:S(2)}) collective-permute-start(bf16[512,256]{0,1:T(8,128)(2,1)S(1)} %pad_maximum_fusion), channel_id=1, source_target_pairs={{0,16},{16,32},{32,48},{48,64},{64,80},{80,96},{96,112},{112,128},... | collective-permute-start | bytes 786440 | tf_op jit(solution)/shard_map/ppermute | solution.py:81
  (9 other events, 37.6 us)
Sparse Core Ops, SparseCore 0:
  9.2 57.2 all-gather.3
  94.6 52.1 all-gather.7
  176.4 73.9 all-gather.5

commit v9 on v7

--- a/solution.py
+++ b/solution.py
@@ -106,17 +106,25 @@
         mixed = jnp.dot(expo.astype(jnp.bfloat16), value_win, preferred_element_type=jnp.float32)
         return (mixed / row_total).astype(jnp.bfloat16)
 
-    attended = lax.map(one_part, (q_parts, pos_parts, doc_parts))
-    attended = attended.reshape(heads_dev, tok_rows, HD)
-    attended = jnp.transpose(attended, (1, 0, 2)).reshape(tok_rows, heads_dev * HD)
-
     w_moved = lax.ppermute(
         w_output,
         ("ctx", "tp"),
         [(c * n_tp + t, t * n_tp + c) for c in range(n_ctx_all) for t in range(n_tp)],
     )
     w_chunk = lax.all_gather(w_moved, "ctx", axis=0, tiled=True)
-    attended_all = lax.all_gather(attended, "tp", axis=1, tiled=True)
+    per_head = []
+    for head in range(heads_dev):
+        sl = slice(head * n_split, (head + 1) * n_split)
+        one = lax.map(one_part, (q_parts[sl], pos_parts[sl], doc_parts[sl]))
+        per_head.append(one.reshape(tok_rows, HD))
+    first = heads_dev // 2
+    early = jnp.stack(per_head[:first], axis=1)
+    late = jnp.stack(per_head[first:], axis=1)
+    early_all = lax.all_gather(early, "tp", axis=0, tiled=False)
+    late_copies = jnp.broadcast_to(late[None], (n_tp,) + late.shape)
+    late_all = lax.all_to_all(late_copies, "tp", 0, 0, tiled=False)
+    both = jnp.concatenate([early_all, late_all], axis=2)
+    attended_all = jnp.transpose(both, (1, 0, 2, 3)).reshape(tok_rows, n_tp * heads_dev * HD)
     out_chunk = jnp.dot(attended_all, w_chunk, preferred_element_type=jnp.float32).astype(jnp.bfloat16)
     chunk = out_chunk.shape[1]
     out_rows = tok_rows // n_tp

time: 284 us -> 315 us (1.11)
  waiting for transfers between devices: 134 us -> 162 us
  starting transfers between devices: 60.7 us -> 53.6 us
  local copies, waits for them, and re-layouts: 7.47 us -> 13.7 us
    all_gather x1, waiting for transfers between devices: 0.02 us -> 31.7 us  [on_device(): w_chunk = lax.all_gather(w_moved, 'ctx', axis=0, tiled=True)]
    ppermute x1, waiting for transfers between devices: 0.01 us -> 19.8 us  [on_device(): lax.ppermute(w_output, ('ctx', 'tp'), [(c * n_tp + t, t * n_tp + c) for c...]
    ppermute x8, waiting for transfers between devices: 44.5 us -> 27.2 us  [on_device(): lax.ppermute(kv_rows_local, 'ctx', [(i, i + shift) for i in range(n_ctx -...]
    all_gather x1, waiting for transfers between devices: 74.1 us -> 61.5 us  [on_device(): early_all = lax.all_gather(early, 'tp', axis=0, tiled=False)]
    ppermute x1, starting transfers between devices: 10.3 us -> 2.14 us  [on_device(): lax.ppermute(w_output, ('ctx', 'tp'), [(c * n_tp + t, t * n_tp + c) for c...]
    ppermute x15, waiting for transfers between devices: 3.04 us -> 7.83 us  [on_device(): lax.ppermute(w_kv, 'ctx', [(i, (i + shift) % n_ctx_all) for i in range(n_...]
    all_to_all x1, starting transfers between devices: 15.2 us -> 10.5 us  [on_device(): got = lax.all_to_all(pieces, 'tp', 0, 0, tiled=False)]
    concatenate x0 -> x1, other arithmetic: none -> 4 us  [on_device(): both = jnp.concatenate([early_all, late_all], axis=2)]
  transfers between devices with their start and end apart: 28 -> 29, of which waited for: 10 -> 14; matrix products, arithmetic and copies ran while one was open for 15% -> 10% of each run, Pallas kernels for 0% -> 0%
where the time goes in v9:
time: 315 us; the launch traced here: 312 us
  waiting for transfers between devices  162 us (51%)
  starting transfers between devices  53.6 us (17%)
  matrix products  30.4 us (10%)
  blocking collectives  25 us (8%)
  local copies, waits for them, and re-layouts  13.7 us (4%)
  between operations  13.7 us (4%)
  other arithmetic  13.6 us (4%)
    all_gather x1, waiting for transfers between devices, on_device(): early_all = lax.all_gather(early, 'tp', axis=0, tiled=False)  61.5 us
    all_gather x1, waiting for transfers between devices, on_device(): w_chunk = lax.all_gather(w_moved, 'ctx', axis=0, tiled=True)  31.7 us
    ppermute x8, waiting for transfers between devices, on_device(): lax.ppermute(kv_rows_local, 'ctx', [(i, i + shift) for i in range(n_ctx -...  27.2 us
    all_to_all x1, blocking collectives, on_device(): got_rows = lax.all_to_all(sent, 'tp', 0, 0, tiled=False)  25 us
    ppermute x15, starting transfers between devices, on_device(): lax.ppermute(w_kv, 'ctx', [(i, (i + shift) % n_ctx_all) for i in range(n_...  20.2 us
    ppermute x1, waiting for transfers between devices, on_device(): lax.ppermute(w_output, ('ctx', 'tp'), [(c * n_tp + t, t * n_tp + c) for c...  19.8 us
    ppermute x8, starting transfers between devices, on_device(): lax.ppermute(kv_rows_local, 'ctx', [(i, i + shift) for i in range(n_ctx -...  16.9 us
    all_to_all x1, waiting for transfers between devices, on_device(): got = lax.all_to_all(pieces, 'tp', 0, 0, tiled=False)  12.5 us
  transfers between devices with their start and end apart: 29, of which 14 were waited for; matrix products, arithmetic and copies ran while one was open for 10% of the time, Pallas kernels for 0%

profile of v9, /device:TPU:6, one launch (start us, length us, event | category | flops | bytes accessed | tf_op | source)
XLA Modules:
  0.0 312.0 jit_solution(2379696403202659983)
XLA Ops:
  9.9 2.4 collective-permute-start.2
  12.3 2.4 collective-permute-start.3
  20.9 2.7 collective-permute-start.9
  34.5 3.5 %collective-permute-done.13 = bf16[512,64]{0,1:T(8,128)(2,1)S(1)} collective-permute-done((bf16[512,64]{0,1:T(8,128)(2,1)S(1)}, bf16[512,64]{0,1:T(8,128)(2,1)S(1)}, u32[]{:S(2)}, u32[]{:S(2)}) %collective-permute-start.13) | collective-permute-done | bytes 65568 | tf_op jit(solution)/shard_map/ppermute | solution.py:51
  38.7 6.2 %fusion.46 = bf16[512,64]{0,1:T(8,128)(2,1)S(1)} fusion(bf16[512,8192]{1,0:T(8,128)(2,1)} %param.10, bf16[8192,64]{0,1:T(8,128)(2,1)S(1)} %bitcast.128, pred[8192]{0:T(1024)(128)(4,1)S(1)} %bitcast.148), kind=kOutput, calls=%fused_computation.43 | convolution fusion | flops 537427968 | bytes 9510912 | tf_op jit(solution)/shard_map/dot_general | solution.py:55
  46.3 10.5 %all-to-all-start = ((bf16[16,512,2,8]{1,3,2,0:T(8,128)(2,1)}), bf16[16,512,2,8]{1,3,2,0:T(8,128)(2,1)S(1)}, u32[]{:S(2)}, u32[]{:S(2)}) async-start(bf16[16,512,2,8]{1,3,2,0:T(8,128)(2,1)} %broadcast_select_fusion), calls=%async_computation | async-start | bytes 524288 | tf_op jit(solution)/shard_map/all_to_all | solution.py:68
  57.6 12.5 %all-to-all-done = bf16[16,512,2,8]{1,3,2,0:T(8,128)(2,1)S(1)} async-done(((bf16[16,512,2,8]{1,3,2,0:T(8,128)(2,1)}), bf16[16,512,2,8]{1,3,2,0:T(8,128)(2,1)S(1)}, u32[]{:S(2)}, u32[]{:S(2)}) %all-to-all-start) | async-done | bytes 262176 | tf_op jit(solution)/shard_map/all_to_all | solution.py:68
  70.8 3.0 collective-permute-start.15
  79.3 2.6 collective-permute-start.19
  81.9 2.1 collective-permute-start.20
  88.0 12.3 %collective-permute-done.17 = bf16[512,256]{0,1:T(8,128)(2,1)S(1)} collective-permute-done((bf16[512,256]{0,1:T(8,128)(2,1)S(1)}, bf16[512,256]{0,1:T(8,128)(2,1)S(1)}, u32[]{:S(2)}, u32[]{:S(2)}) %collective-permute-start.17) | collective-permute-done | bytes 262176 | tf_op jit(solution)/shard_map/ppermute | solution.py:80
  103.5 6.2 %collective-permute-done.20 = bf16[512,256]{0,1:T(8,128)(2,1)S(1)} collective-permute-done((bf16[512,256]{0,1:T(8,128)(2,1)S(1)}, bf16[512,256]{0,1:T(8,128)(2,1)S(1)}, u32[]{:S(2)}, u32[]{:S(2)}) %collective-permute-start.20) | collective-permute-done | bytes 262176 | tf_op jit(solution)/shard_map/ppermute | solution.py:80
  109.7 5.6 %collective-permute-done.21 = bf16[512,256]{0,1:T(8,128)(2,1)S(1)} collective-permute-done((bf16[512,256]{0,1:T(8,128)(2,1)S(1)}, bf16[512,256]{0,1:T(8,128)(2,1)S(1)}, u32[]{:S(2)}, u32[]{:S(2)}) %collective-permute-start.21) | collective-permute-done | bytes 262176 | tf_op jit(solution)/shard_map/ppermute | solution.py:80
  117.8 7.0 %fusion.68 = f32[512,256]{0,1:T(8,128)S(1)} fusion(bf16[512,8192]{1,0:T(8,128)(2,1)} %param.10, bf16[8192,256]{1,0:T(8,128)(2,1)} %all-gather.4.cloned.1.call-done), kind=kOutput, calls=%fused_computation.136 | convolution fusion | flops 2147483648 | bytes 13107200 | tf_op jit(solution)/shard_map/dot_general | solution.py:57
  125.2 8.6 %while.22 = (s32[]{:T(128)}, bf16[2,256,128]{2,1,0:T(8,128)(2,1)S(1)}, s32[2,256]{1,0:T(2,128)S(1)}, s32[4608]{0:T(1024)S(1)}, s32[2,256]{1,0:T(2,128)S(1)}, /*i...) while((s32[]{:T(128)}, ...), condition=%wide.region_6.7_spmd.clone, body=%wide.region_3.6_spmd.clone.sunk | while | flops 625283072 | bytes 16798836 | solution.py:118
  136.7 19.8 %collective-permute-done.23 = bf16[256,512]{1,0:T(8,128)(2,1)S(1)} collective-permute-done((bf16[256,512]{1,0:T(8,128)(2,1)S(1)}, bf16[256,512]{1,0:T(8,128)(2,1)S(1)}, u32[]{:S(2)}, u32[]{:S(2)}) %collective-permute-start.23) | collective-permute-done | bytes 262176 | tf_op jit(solution)/shard_map/ppermute | solution.py:109
  157.4 8.6 %while.23 = (s32[]{:T(128)}, bf16[2,256,128]{2,1,0:T(8,128)(2,1)S(1)}, s32[2,256]{1,0:T(2,128)S(1)}, s32[4608]{0:T(1024)S(1)}, s32[2,256]{1,0:T(2,128)S(1)}, /*i...) while((s32[]{:T(128)}, ...), condition=%wide.region_10.11_spmd.clone, body=%wide.region_7.10_spmd.clone.sunk | while | flops 625283072 | bytes 16798836 | solution.py:118
  167.7 3.7 %all-to-all-start.1 = ((bf16[16,512,1,128]{1,3,2,0:T(8,128)(2,1)}), bf16[16,512,1,128]{1,3,2,0:T(8,128)(2,1)S(1)}, u32[]{:S(2)}, u32[]{:S(2)}) async-start(bf16[16,512,1,128]{1,3,2,0:T(8,128)(2,1)} %broadcast_in_dim.88), calls=%async_computation.1 | async-start | bytes 4194304 | tf_op jit(solution)/shard_map/all_to_all | solution.py:125
  171.4 61.5 %all-gather.6.cloned.1.call-done = bf16[16,512,1,128]{3,1,2,0:T(8,128)(2,1)} async-done(((bf16[1,512,1,128]{3,1,2,0:T(8,128)(2,1)}), bf16[16,512,1,128]{3,1,2,0:T(8,128)(2,1)}) %all-gather.6.cloned.1.call-update) | async-done | bytes 2097168 | tf_op jit(solution)/shard_map/all_gather | solution.py:123
  233.0 3.9 %copy.45 = bf16[16,512,1,128]{1,3,2,0:T(8,128)(2,1)} copy(bf16[16,512,1,128]{3,1,2,0:T(8,128)(2,1)} %all-gather.6.cloned.1.call-done) | data formatting | bytes 4194304 | tf_op jit(solution)/shard_map/all_gather | solution.py:123
  238.1 4.0 %pad_maximum_fusion = bf16[16,512,2,128]{1,3,2,0:T(8,128)(2,1)} fusion(bf16[16,512,1,128]{1,3,2,0:T(8,128)(2,1)S(1)} %all-to-all-done.1, bf16[16,512,1,128]{1,3,2,0:T(8,128)(2,1)} %copy.45), kind=kLoop, calls=%fused_computation.40 | loop fusion | flops 2097152 | bytes 8388608 | tf_op jit(solution)/shard_map/concatenate | solution.py:126
  242.1 31.7 %all-gather.8.cloned.1.call-done = bf16[4096,512]{1,0:T(8,128)(2,1)} async-done(((bf16[256,512]{1,0:T(8,128)(2,1)}), bf16[4096,512]{1,0:T(8,128)(2,1)}) %all-gather.8.cloned.1.call-update) | async-done | bytes 4194320 | tf_op jit(solution)/shard_map/all_gather | solution.py:114
  273.8 5.8 %convolution_convert_fusion = bf16[512,512]{1,0:T(8,128)(2,1)S(1)} fusion(bf16[512,4096]{0,1:T(8,128)(2,1)} %bitcast.127, bf16[4096,512]{1,0:T(8,128)(2,1)} %all-gather.8.cloned.1.call-done), kind=kOutput, calls=%fused_computation.41 | convolution fusion | flops 2147745792 | bytes 8912896 | tf_op jit(solution)/shard_map/dot_general | solution.py:128
  279.6 25.0 %all_to_all.15 = bf16[16,32,512]{2,1,0:T(8,128)(2,1)S(1)} all-to-all(bf16[16,32,512]{2,1,0:T(8,128)(2,1)S(1)} %bitcast.131), channel_id=1, replica_groups=mesh['ctx'=16,'tp'=16] {'tp'}, dimensions={0} | all-to-all | bytes 1048576 | tf_op jit(solution)/shard_map/all_to_all | solution.py:132
  (143 shorter events, 63.7 us)
Async XLA Ops:
  6.5 111.2 %all-gather.4.cloned.1.call-start = ((), (), s32[]{:S(2)}) async-start(), calls=%async_computation.3 | async-start | bytes 4456448 | tf_op jit(solution)/shard_map/all_gather | solution.py:56
  8.1 8.5 %collective-permute-start = (bf16[512,64]{0,1:T(8,128)(2,1)S(1)}, bf16[512,64]{0,1:T(8,128)(2,1)S(1)}, u32[]{:S(2)}, u32[]{:S(2)}) collective-permute-start(bf16[512,64]{0,1:T(8,128)(2,1)S(1)} %constant_dynamic-update-slice_fusion), channel_id=1, source_target_pairs={{0,16},{16,32},{32,48},{48,64},{64,80},{80,96},{96,112},{112,128},... | collective-permute-start | bytes 196616 | tf_op jit(solution)/shard_map/ppermute | solution.py:51
  8.1 9.9 %collective-permute-start.1 = (bf16[512,64]{0,1:T(8,128)(2,1)S(1)}, bf16[512,64]{0,1:T(8,128)(2,1)S(1)}, u32[]{:S(2)}, u32[]{:S(2)}) collective-permute-start(bf16[512,64]{0,1:T(8,128)(2,1)S(1)} %constant_dynamic-update-slice_fusion), channel_id=1, source_target_pairs={{0,32},{16,48},{32,64},{48,80},{64,96},{80,112},{96,128},{112,144}... | collective-permute-start | bytes 196616 | tf_op jit(solution)/shard_map/ppermute | solution.py:51
  9.9 9.4 %collective-permute-start.2 = (bf16[512,64]{0,1:T(8,128)(2,1)S(1)}, bf16[512,64]{0,1:T(8,128)(2,1)S(1)}, u32[]{:S(2)}, u32[]{:S(2)}) collective-permute-start(bf16[512,64]{0,1:T(8,128)(2,1)S(1)} %constant_dynamic-update-slice_fusion), channel_id=1, source_target_pairs={{0,48},{16,64},{32,80},{48,96},{64,112},{80,128},{96,144},{112,160... | collective-permute-start | bytes 196616 | tf_op jit(solution)/shard_map/ppermute | solution.py:51
  12.3 8.5 %collective-permute-start.3 = (bf16[512,64]{0,1:T(8,128)(2,1)S(1)}, bf16[512,64]{0,1:T(8,128)(2,1)S(1)}, u32[]{:S(2)}, u32[]{:S(2)}) collective-permute-start(bf16[512,64]{0,1:T(8,128)(2,1)S(1)} %constant_dynamic-update-slice_fusion), channel_id=1, source_target_pairs={{0,64},{16,80},{32,96},{48,112},{64,128},{80,144},{96,160},{112,17... | collective-permute-start | bytes 196616 | tf_op jit(solution)/shard_map/ppermute | solution.py:51
  20.8 8.2 %collective-permute-start.8 = (bf16[512,64]{0,1:T(8,128)(2,1)S(1)}, bf16[512,64]{0,1:T(8,128)(2,1)S(1)}, u32[]{:S(2)}, u32[]{:S(2)}) collective-permute-start(bf16[512,64]{0,1:T(8,128)(2,1)S(1)} %constant_dynamic-update-slice_fusion), channel_id=1, source_target_pairs={{0,144},{16,160},{32,176},{48,192},{64,208},{80,224},{96,240},{112... | collective-permute-start | bytes 196616 | tf_op jit(solution)/shard_map/ppermute | solution.py:51
  20.9 8.4 %collective-permute-start.9 = (bf16[512,64]{0,1:T(8,128)(2,1)S(1)}, bf16[512,64]{0,1:T(8,128)(2,1)S(1)}, u32[]{:S(2)}, u32[]{:S(2)}) collective-permute-start(bf16[512,64]{0,1:T(8,128)(2,1)S(1)} %constant_dynamic-update-slice_fusion), channel_id=1, source_target_pairs={{0,160},{16,176},{32,192},{48,208},{64,224},{80,240},{96,0},{112,1... | collective-permute-start | bytes 196616 | tf_op jit(solution)/shard_map/ppermute | solution.py:51
  25.1 7.8 %collective-permute-start.11 = (bf16[512,64]{0,1:T(8,128)(2,1)S(1)}, bf16[512,64]{0,1:T(8,128)(2,1)S(1)}, u32[]{:S(2)}, u32[]{:S(2)}) collective-permute-start(bf16[512,64]{0,1:T(8,128)(2,1)S(1)} %constant_dynamic-update-slice_fusion), channel_id=1, source_target_pairs={{0,192},{16,208},{32,224},{48,240},{64,0},{80,16},{96,32},{112,48}... | collective-permute-start | bytes 196616 | tf_op jit(solution)/shard_map/ppermute | solution.py:51
  26.8 7.7 %collective-permute-start.12 = (bf16[512,64]{0,1:T(8,128)(2,1)S(1)}, bf16[512,64]{0,1:T(8,128)(2,1)S(1)}, u32[]{:S(2)}, u32[]{:S(2)}) collective-permute-start(bf16[512,64]{0,1:T(8,128)(2,1)S(1)} %constant_dynamic-update-slice_fusion), channel_id=1, source_target_pairs={{0,208},{16,224},{32,240},{48,0},{64,16},{80,32},{96,48},{112,64},... | collective-permute-start | bytes 196616 | tf_op jit(solution)/shard_map/ppermute | solution.py:51
  28.9 9.0 %collective-permute-start.13 = (bf16[512,64]{0,1:T(8,128)(2,1)S(1)}, bf16[512,64]{0,1:T(8,128)(2,1)S(1)}, u32[]{:S(2)}, u32[]{:S(2)}) collective-permute-start(bf16[512,64]{0,1:T(8,128)(2,1)S(1)} %constant_dynamic-update-slice_fusion), channel_id=1, source_target_pairs={{0,224},{16,240},{32,0},{48,16},{64,32},{80,48},{96,64},{112,80},{... | collective-permute-start | bytes 196616 | tf_op jit(solution)/shard_map/ppermute | solution.py:51
  29.3 8.7 %collective-permute-start.14 = (bf16[512,64]{0,1:T(8,128)(2,1)S(1)}, bf16[512,64]{0,1:T(8,128)(2,1)S(1)}, u32[]{:S(2)}, u32[]{:S(2)}) collective-permute-start(bf16[512,64]{0,1:T(8,128)(2,1)S(1)} %constant_dynamic-update-slice_fusion), channel_id=1, source_target_pairs={{0,240},{16,0},{32,16},{48,32},{64,48},{80,64},{96,80},{112,96},{1... | collective-permute-start | bytes 196616 | tf_op jit(solution)/shard_map/ppermute | solution.py:51
  46.3 23.8 %all-to-all-start = ((bf16[16,512,2,8]{1,3,2,0:T(8,128)(2,1)}), bf16[16,512,2,8]{1,3,2,0:T(8,128)(2,1)S(1)}, u32[]{:S(2)}, u32[]{:S(2)}) async-start(bf16[16,512,2,8]{1,3,2,0:T(8,128)(2,1)} %broadcast_select_fusion), calls=%async_computation | async-start | bytes 524288 | tf_op jit(solution)/shard_map/all_to_all | solution.py:68
  56.8 176.1 %all-gather.6.cloned.1.call-start = ((), (), s32[]{:S(2)}) async-start(), calls=%async_computation.4 | async-start | bytes 2228224 | tf_op jit(solution)/shard_map/all_gather | solution.py:123
  70.8 11.1 %collective-permute-start.15 = (bf16[512,256]{0,1:T(8,128)(2,1)S(1)}, bf16[512,256]{0,1:T(8,128)(2,1)S(1)}, u32[]{:S(2)}, u32[]{:S(2)}) collective-permute-start(bf16[512,256]{0,1:T(8,128)(2,1)S(1)} %pad_maximum_fusion.1), channel_id=1, source_target_pairs={{0,128},{16,144},{32,160},{48,176},{64,192},{80,208},{96,224},{112... | collective-permute-start | bytes 786440 | tf_op jit(solution)/shard_map/ppermute | solution.py:80
  73.8 12.3 %collective-permute-start.16 = (bf16[512,256]{0,1:T(8,128)(2,1)S(1)}, bf16[512,256]{0,1:T(8,128)(2,1)S(1)}, u32[]{:S(2)}, u32[]{:S(2)}) collective-permute-start(bf16[512,256]{0,1:T(8,128)(2,1)S(1)} %pad_maximum_fusion.1), channel_id=1, source_target_pairs={{0,112},{16,128},{32,144},{48,160},{64,176},{80,192},{96,208},{112... | collective-permute-start | bytes 786440 | tf_op jit(solution)/shard_map/ppermute | solution.py:80
  75.5 24.8 %collective-permute-start.17 = (bf16[512,256]{0,1:T(8,128)(2,1)S(1)}, bf16[512,256]{0,1:T(8,128)(2,1)S(1)}, u32[]{:S(2)}, u32[]{:S(2)}) collective-permute-start(bf16[512,256]{0,1:T(8,128)(2,1)S(1)} %pad_maximum_fusion.1), channel_id=1, source_target_pairs={{0,96},{16,112},{32,128},{48,144},{64,160},{80,176},{96,192},{112,... | collective-permute-start | bytes 786440 | tf_op jit(solution)/shard_map/ppermute | solution.py:80
  77.4 24.8 %collective-permute-start.18 = (bf16[512,256]{0,1:T(8,128)(2,1)S(1)}, bf16[512,256]{0,1:T(8,128)(2,1)S(1)}, u32[]{:S(2)}, u32[]{:S(2)}) collective-permute-start(bf16[512,256]{0,1:T(8,128)(2,1)S(1)} %pad_maximum_fusion.1), channel_id=1, source_target_pairs={{0,80},{16,96},{32,112},{48,128},{64,144},{80,160},{96,176},{112,1... | collective-permute-start | bytes 786440 | tf_op jit(solution)/shard_map/ppermute | solution.py:80
  79.3 24.1 %collective-permute-start.19 = (bf16[512,256]{0,1:T(8,128)(2,1)S(1)}, bf16[512,256]{0,1:T(8,128)(2,1)S(1)}, u32[]{:S(2)}, u32[]{:S(2)}) collective-permute-start(bf16[512,256]{0,1:T(8,128)(2,1)S(1)} %pad_maximum_fusion.1), channel_id=1, source_target_pairs={{0,64},{16,80},{32,96},{48,112},{64,128},{80,144},{96,160},{112,17... | collective-permute-start | bytes 786440 | tf_op jit(solution)/shard_map/ppermute | solution.py:80
  81.9 27.7 %collective-permute-start.20 = (bf16[512,256]{0,1:T(8,128)(2,1)S(1)}, bf16[512,256]{0,1:T(8,128)(2,1)S(1)}, u32[]{:S(2)}, u32[]{:S(2)}) collective-permute-start(bf16[512,256]{0,1:T(8,128)(2,1)S(1)} %pad_maximum_fusion.1), channel_id=1, source_target_pairs={{0,48},{16,64},{32,80},{48,96},{64,112},{80,128},{96,144},{112,160... | collective-permute-start | bytes 786440 | tf_op jit(solution)/shard_map/ppermute | solution.py:80
  86.1 29.2 %collective-permute-start.21 = (bf16[512,256]{0,1:T(8,128)(2,1)S(1)}, bf16[512,256]{0,1:T(8,128)(2,1)S(1)}, u32[]{:S(2)}, u32[]{:S(2)}) collective-permute-start(bf16[512,256]{0,1:T(8,128)(2,1)S(1)} %pad_maximum_fusion.1), channel_id=1, source_target_pairs={{0,32},{16,48},{32,64},{48,80},{64,96},{80,112},{96,128},{112,144}... | collective-permute-start | bytes 786440 | tf_op jit(solution)/shard_map/ppermute | solution.py:80
  100.3 15.0 %collective-permute-start.22 = (bf16[512,256]{0,1:T(8,128)(2,1)S(1)}, bf16[512,256]{0,1:T(8,128)(2,1)S(1)}, u32[]{:S(2)}, u32[]{:S(2)}) collective-permute-start(bf16[512,256]{0,1:T(8,128)(2,1)S(1)} %pad_maximum_fusion.1), channel_id=1, source_target_pairs={{0,16},{16,32},{32,48},{48,64},{64,80},{80,96},{96,112},{112,128},... | collective-permute-start | bytes 786440 | tf_op jit(solution)/shard_map/ppermute | solution.py:80
  134.5 139.3 %all-gather.8.cloned.1.call-start = ((), (), s32[]{:S(2)}) async-start(), calls=%async_computation.5 | async-start | bytes 4456448 | tf_op jit(solution)/shard_map/all_gather | solution.py:114
  134.5 22.0 %collective-permute-start.23 = (bf16[256,512]{1,0:T(8,128)(2,1)S(1)}, bf16[256,512]{1,0:T(8,128)(2,1)S(1)}, u32[]{:S(2)}, u32[]{:S(2)}) collective-permute-start(bf16[256,512]{1,0:T(8,128)(2,1)S(1)} %copy-done.3), channel_id=1, source_target_pairs={{0,0},{1,16},{2,32},{3,48},{4,64},{5,80},{6,96},{7,112},{8,128},{9... | collective-permute-start | bytes 786440 | tf_op jit(solution)/shard_map/ppermute | solution.py:109
  167.7 70.4 %all-to-all-start.1 = ((bf16[16,512,1,128]{1,3,2,0:T(8,128)(2,1)}), bf16[16,512,1,128]{1,3,2,0:T(8,128)(2,1)S(1)}, u32[]{:S(2)}, u32[]{:S(2)}) async-start(bf16[16,512,1,128]{1,3,2,0:T(8,128)(2,1)} %broadcast_in_dim.88), calls=%async_computation.1 | async-start | bytes 4194304 | tf_op jit(solution)/shard_map/all_to_all | solution.py:125
  (9 other events, 53.7 us)
Sparse Core Ops, SparseCore 0:
  15.0 44.5 all-gather.3
  134.6 98.3 all-gather.5
  234.8 38.9 all-gather.7

commit v10 on v7

--- a/solution.py
+++ b/solution.py
@@ -116,8 +116,11 @@
         [(c * n_tp + t, t * n_tp + c) for c in range(n_ctx_all) for t in range(n_tp)],
     )
     w_chunk = lax.all_gather(w_moved, "ctx", axis=0, tiled=True)
-    attended_all = lax.all_gather(attended, "tp", axis=1, tiled=True)
-    out_chunk = jnp.dot(attended_all, w_chunk, preferred_element_type=jnp.float32).astype(jnp.bfloat16)
+    from_peers = lax.all_gather(attended, "tp", axis=0, tiled=False)
+    w_by_peer = w_chunk.reshape(n_tp, attended.shape[1], w_chunk.shape[1])
+    out_chunk = jnp.einsum(
+        "trj,tjc->rc", from_peers, w_by_peer, preferred_element_type=jnp.float32
+    ).astype(jnp.bfloat16)
     chunk = out_chunk.shape[1]
     out_rows = tok_rows // n_tp
     sent = out_chunk.reshape(n_tp, out_rows, chunk)

time: 284 us -> 284 us (level)
  no operation moved by 1% of the time
where the time goes in v10:
time: 284 us; the launch traced here: 283 us
  waiting for transfers between devices  134 us (47%)
  starting transfers between devices  60.7 us (21%)
  matrix products  30.2 us (11%)
  blocking collectives  25.6 us (9%)
  between operations  13.7 us (5%)
  other arithmetic  11.1 us (4%)
  local copies, waits for them, and re-layouts  7.76 us (3%)
    all_gather x1, waiting for transfers between devices, on_device(): from_peers = lax.all_gather(attended, 'tp', axis=0, tiled=False)  74.1 us
    ppermute x8, waiting for transfers between devices, on_device(): lax.ppermute(kv_rows_local, 'ctx', [(i, i + shift) for i in range(n_ctx -...  44.5 us
    all_to_all x1, blocking collectives, on_device(): got_rows = lax.all_to_all(sent, 'tp', 0, 0, tiled=False)  25.6 us
    ppermute x15, starting transfers between devices, on_device(): lax.ppermute(w_kv, 'ctx', [(i, (i + shift) % n_ctx_all) for i in range(n_...  20.1 us
    all_to_all x1, starting transfers between devices, on_device(): got = lax.all_to_all(pieces, 'tp', 0, 0, tiled=False)  15.2 us
    ppermute x8, starting transfers between devices, on_device(): lax.ppermute(kv_rows_local, 'ctx', [(i, i + shift) for i in range(n_ctx -...  15 us
    all_to_all x1, waiting for transfers between devices, on_device(): got = lax.all_to_all(pieces, 'tp', 0, 0, tiled=False)  11.6 us
    ppermute x1, starting transfers between devices, on_device(): lax.ppermute(w_output, ('ctx', 'tp'), [(c * n_tp + t, t * n_tp + c) for c...  10.3 us
  transfers between devices with their start and end apart: 28, of which 10 were waited for; matrix products, arithmetic and copies ran while one was open for 15% of the time, Pallas kernels for 0%

profile of v10, /device:TPU:6, one launch (start us, length us, event | category | flops | bytes accessed | tf_op | source)
XLA Modules:
  0.0 283.2 jit_solution(16134633824449877317)
XLA Ops:
  10.6 2.4 collective-permute-start.2
  13.0 2.4 collective-permute-start.3
  21.6 2.7 collective-permute-start.9
  27.5 2.1 collective-permute-start.12
  31.9 10.3 %collective-permute-start.23 = (bf16[256,512]{1,0:T(8,128)(2,1)}, bf16[256,512]{1,0:T(8,128)(2,1)S(1)}, u32[]{:S(2)}, u32[]{:S(2)}) collective-permute-start(bf16[256,512]{1,0:T(8,128)(2,1)} %param.13), channel_id=1, source_target_pairs={{0,0},{1,16},{2,32},{3,48},{4,64},{5,80},{6,96},{7,112},{8,128},{9... | collective-permute-start | bytes 786440 | tf_op jit(solution)/shard_map/ppermute | solution.py:113
  44.8 6.2 %fusion.24 = bf16[512,64]{0,1:T(8,128)(2,1)S(1)} fusion(bf16[512,8192]{1,0:T(8,128)(2,1)} %param.8, bf16[8192,64]{0,1:T(8,128)(2,1)S(1)} %bitcast.105, pred[8192]{0:T(1024)(128)(4,1)S(1)} %bitcast.118), kind=kOutput, calls=%fused_computation.24 | convolution fusion | flops 537427968 | bytes 9510912 | tf_op jit(solution)/shard_map/dot_general | solution.py:55
  52.4 15.2 %all-to-all-start = ((bf16[16,512,2,8]{1,3,2,0:T(8,128)(2,1)}), bf16[16,512,2,8]{1,3,2,0:T(8,128)(2,1)S(1)}, u32[]{:S(2)}, u32[]{:S(2)}) async-start(bf16[16,512,2,8]{1,3,2,0:T(8,128)(2,1)} %broadcast_select_fusion), calls=%async_computation | async-start | bytes 524288 | tf_op jit(solution)/shard_map/all_to_all | solution.py:68
  69.0 11.6 %all-to-all-done = bf16[16,512,2,8]{1,3,2,0:T(8,128)(2,1)S(1)} async-done(((bf16[16,512,2,8]{1,3,2,0:T(8,128)(2,1)}), bf16[16,512,2,8]{1,3,2,0:T(8,128)(2,1)S(1)}, u32[]{:S(2)}, u32[]{:S(2)}) %all-to-all-start) | async-done | bytes 262176 | tf_op jit(solution)/shard_map/all_to_all | solution.py:68
  84.7 1.9 collective-permute-start.17
  87.5 1.9 collective-permute-start.18
  89.4 2.7 collective-permute-start.19
  92.1 2.0 collective-permute-start.20
  94.9 2.0 collective-permute-start.21
  97.0 9.4 %collective-permute-done.17 = bf16[512,256]{0,1:T(8,128)(2,1)S(1)} collective-permute-done((bf16[512,256]{0,1:T(8,128)(2,1)S(1)}, bf16[512,256]{0,1:T(8,128)(2,1)S(1)}, u32[]{:S(2)}, u32[]{:S(2)}) %collective-permute-start.17) | collective-permute-done | bytes 262176 | tf_op jit(solution)/shard_map/ppermute | solution.py:80
  106.4 1.9 collective-permute-start.22
  108.3 5.3 %collective-permute-done.18 = bf16[512,256]{0,1:T(8,128)(2,1)S(1)} collective-permute-done((bf16[512,256]{0,1:T(8,128)(2,1)S(1)}, bf16[512,256]{0,1:T(8,128)(2,1)S(1)}, u32[]{:S(2)}, u32[]{:S(2)}) %collective-permute-start.18) | collective-permute-done | bytes 262176 | tf_op jit(solution)/shard_map/ppermute | solution.py:80
  113.6 11.2 %collective-permute-done.19 = bf16[512,256]{0,1:T(8,128)(2,1)S(1)} collective-permute-done((bf16[512,256]{0,1:T(8,128)(2,1)S(1)}, bf16[512,256]{0,1:T(8,128)(2,1)S(1)}, u32[]{:S(2)}, u32[]{:S(2)}) %collective-permute-start.19) | collective-permute-done | bytes 262176 | tf_op jit(solution)/shard_map/ppermute | solution.py:80
  124.8 11.4 %collective-permute-done.20 = bf16[512,256]{0,1:T(8,128)(2,1)S(1)} collective-permute-done((bf16[512,256]{0,1:T(8,128)(2,1)S(1)}, bf16[512,256]{0,1:T(8,128)(2,1)S(1)}, u32[]{:S(2)}, u32[]{:S(2)}) %collective-permute-start.20) | collective-permute-done | bytes 262176 | tf_op jit(solution)/shard_map/ppermute | solution.py:80
  136.2 6.4 %collective-permute-done.21 = bf16[512,256]{0,1:T(8,128)(2,1)S(1)} collective-permute-done((bf16[512,256]{0,1:T(8,128)(2,1)S(1)}, bf16[512,256]{0,1:T(8,128)(2,1)S(1)}, u32[]{:S(2)}, u32[]{:S(2)}) %collective-permute-start.21) | collective-permute-done | bytes 262176 | tf_op jit(solution)/shard_map/ppermute | solution.py:80
  144.5 7.0 %fusion.44 = f32[512,256]{0,1:T(8,128)S(1)} fusion(bf16[512,8192]{1,0:T(8,128)(2,1)} %param.8, bf16[8192,256]{1,0:T(8,128)(2,1)} %all-gather.4.cloned.1.call-done), kind=kOutput, calls=%fused_computation.116 | convolution fusion | flops 2147483648 | bytes 13107200 | tf_op jit(solution)/shard_map/dot_general | solution.py:57
  151.9 17.3 %while.11 = (s32[]{:T(128)}, bf16[4,256,128]{2,1,0:T(8,128)(2,1)S(1)}, s32[4,256]{1,0:T(4,128)S(1)}, s32[4608]{0:T(1024)S(1)}, s32[4,256]{1,0:T(4,128)S(1)}, /*i...) while((s32[]{:T(128)}, ...), condition=%wide.region_6.7_spmd.clone, body=%wide.region_3.6_spmd.clone.sunk | while | flops 625283072 | bytes 16798836 | solution.py:109
  170.3 74.1 %all-gather.6.cloned.1.call-done = bf16[16,512,256]{2,1,0:T(8,128)(2,1)} async-done(((bf16[1,512,256]{2,1,0:T(8,128)(2,1)}), bf16[16,512,256]{2,1,0:T(8,128)(2,1)}) %all-gather.6.cloned.1.call-update) | async-done | bytes 4194320 | tf_op jit(solution)/shard_map/all_gather | solution.py:119
  244.5 5.8 %fusion.23 = bf16[512,512]{1,0:T(8,128)(2,1)S(1)} fusion(bf16[16,512,256]{2,1,0:T(8,128)(2,1)} %all-gather.6.cloned.1.call-done, bf16[16,256,512]{2,1,0:T(8,128)(2,1)} %bitcast.119), kind=kOutput, calls=%fused_computation.22 | convolution fusion | flops 2147745792 | bytes 8912896 | tf_op jit(solution)/shard_map/trj,tjc->rc/dot_general | solution.py:121
  250.2 25.6 %all_to_all.10 = bf16[16,32,512]{2,1,0:T(8,128)(2,1)S(1)} all-to-all(bf16[16,32,512]{2,1,0:T(8,128)(2,1)S(1)} %bitcast.109), channel_id=1, replica_groups=mesh['ctx'=16,'tp'=16] {'tp'}, dimensions={0} | all-to-all | bytes 1048576 | tf_op jit(solution)/shard_map/all_to_all | solution.py:127
  (141 shorter events, 47.9 us)
Async XLA Ops:
  6.5 137.9 %all-gather.4.cloned.1.call-start = ((), (), s32[]{:S(2)}) async-start(), calls=%async_computation.2 | async-start | bytes 4456448 | tf_op jit(solution)/shard_map/all_gather | solution.py:56
  8.8 8.5 %collective-permute-start = (bf16[512,64]{0,1:T(8,128)(2,1)S(1)}, bf16[512,64]{0,1:T(8,128)(2,1)S(1)}, u32[]{:S(2)}, u32[]{:S(2)}) collective-permute-start(bf16[512,64]{0,1:T(8,128)(2,1)S(1)} %constant_dynamic-update-slice_fusion), channel_id=1, source_target_pairs={{0,16},{16,32},{32,48},{48,64},{64,80},{80,96},{96,112},{112,128},... | collective-permute-start | bytes 196616 | tf_op jit(solution)/shard_map/ppermute | solution.py:51
  8.8 9.8 %collective-permute-start.1 = (bf16[512,64]{0,1:T(8,128)(2,1)S(1)}, bf16[512,64]{0,1:T(8,128)(2,1)S(1)}, u32[]{:S(2)}, u32[]{:S(2)}) collective-permute-start(bf16[512,64]{0,1:T(8,128)(2,1)S(1)} %constant_dynamic-update-slice_fusion), channel_id=1, source_target_pairs={{0,32},{16,48},{32,64},{48,80},{64,96},{80,112},{96,128},{112,144}... | collective-permute-start | bytes 196616 | tf_op jit(solution)/shard_map/ppermute | solution.py:51
  10.6 9.3 %collective-permute-start.2 = (bf16[512,64]{0,1:T(8,128)(2,1)S(1)}, bf16[512,64]{0,1:T(8,128)(2,1)S(1)}, u32[]{:S(2)}, u32[]{:S(2)}) collective-permute-start(bf16[512,64]{0,1:T(8,128)(2,1)S(1)} %constant_dynamic-update-slice_fusion), channel_id=1, source_target_pairs={{0,48},{16,64},{32,80},{48,96},{64,112},{80,128},{96,144},{112,160... | collective-permute-start | bytes 196616 | tf_op jit(solution)/shard_map/ppermute | solution.py:51
  13.0 8.4 %collective-permute-start.3 = (bf16[512,64]{0,1:T(8,128)(2,1)S(1)}, bf16[512,64]{0,1:T(8,128)(2,1)S(1)}, u32[]{:S(2)}, u32[]{:S(2)}) collective-permute-start(bf16[512,64]{0,1:T(8,128)(2,1)S(1)} %constant_dynamic-update-slice_fusion), channel_id=1, source_target_pairs={{0,64},{16,80},{32,96},{48,112},{64,128},{80,144},{96,160},{112,17... | collective-permute-start | bytes 196616 | tf_op jit(solution)/shard_map/ppermute | solution.py:51
  21.5 8.2 %collective-permute-start.8 = (bf16[512,64]{0,1:T(8,128)(2,1)S(1)}, bf16[512,64]{0,1:T(8,128)(2,1)S(1)}, u32[]{:S(2)}, u32[]{:S(2)}) collective-permute-start(bf16[512,64]{0,1:T(8,128)(2,1)S(1)} %constant_dynamic-update-slice_fusion), channel_id=1, source_target_pairs={{0,144},{16,160},{32,176},{48,192},{64,208},{80,224},{96,240},{112... | collective-permute-start | bytes 196616 | tf_op jit(solution)/shard_map/ppermute | solution.py:51
  21.6 8.4 %collective-permute-start.9 = (bf16[512,64]{0,1:T(8,128)(2,1)S(1)}, bf16[512,64]{0,1:T(8,128)(2,1)S(1)}, u32[]{:S(2)}, u32[]{:S(2)}) collective-permute-start(bf16[512,64]{0,1:T(8,128)(2,1)S(1)} %constant_dynamic-update-slice_fusion), channel_id=1, source_target_pairs={{0,160},{16,176},{32,192},{48,208},{64,224},{80,240},{96,0},{112,1... | collective-permute-start | bytes 196616 | tf_op jit(solution)/shard_map/ppermute | solution.py:51
  24.3 7.6 %collective-permute-start.10 = (bf16[512,64]{0,1:T(8,128)(2,1)S(1)}, bf16[512,64]{0,1:T(8,128)(2,1)S(1)}, u32[]{:S(2)}, u32[]{:S(2)}) collective-permute-start(bf16[512,64]{0,1:T(8,128)(2,1)S(1)} %constant_dynamic-update-slice_fusion), channel_id=1, source_target_pairs={{0,176},{16,192},{32,208},{48,224},{64,240},{80,0},{96,16},{112,32... | collective-permute-start | bytes 196616 | tf_op jit(solution)/shard_map/ppermute | solution.py:51
  25.8 16.4 %collective-permute-start.11 = (bf16[512,64]{0,1:T(8,128)(2,1)S(1)}, bf16[512,64]{0,1:T(8,128)(2,1)S(1)}, u32[]{:S(2)}, u32[]{:S(2)}) collective-permute-start(bf16[512,64]{0,1:T(8,128)(2,1)S(1)} %constant_dynamic-update-slice_fusion), channel_id=1, source_target_pairs={{0,192},{16,208},{32,224},{48,240},{64,0},{80,16},{96,32},{112,48}... | collective-permute-start | bytes 196616 | tf_op jit(solution)/shard_map/ppermute | solution.py:51
  27.5 14.8 %collective-permute-start.12 = (bf16[512,64]{0,1:T(8,128)(2,1)S(1)}, bf16[512,64]{0,1:T(8,128)(2,1)S(1)}, u32[]{:S(2)}, u32[]{:S(2)}) collective-permute-start(bf16[512,64]{0,1:T(8,128)(2,1)S(1)} %constant_dynamic-update-slice_fusion), channel_id=1, source_target_pairs={{0,208},{16,224},{32,240},{48,0},{64,16},{80,32},{96,48},{112,64},... | collective-permute-start | bytes 196616 | tf_op jit(solution)/shard_map/ppermute | solution.py:51
  29.6 14.4 %collective-permute-start.13 = (bf16[512,64]{0,1:T(8,128)(2,1)S(1)}, bf16[512,64]{0,1:T(8,128)(2,1)S(1)}, u32[]{:S(2)}, u32[]{:S(2)}) collective-permute-start(bf16[512,64]{0,1:T(8,128)(2,1)S(1)} %constant_dynamic-update-slice_fusion), channel_id=1, source_target_pairs={{0,224},{16,240},{32,0},{48,16},{64,32},{80,48},{96,64},{112,80},{... | collective-permute-start | bytes 196616 | tf_op jit(solution)/shard_map/ppermute | solution.py:51
  30.0 14.1 %collective-permute-start.14 = (bf16[512,64]{0,1:T(8,128)(2,1)S(1)}, bf16[512,64]{0,1:T(8,128)(2,1)S(1)}, u32[]{:S(2)}, u32[]{:S(2)}) collective-permute-start(bf16[512,64]{0,1:T(8,128)(2,1)S(1)} %constant_dynamic-update-slice_fusion), channel_id=1, source_target_pairs={{0,240},{16,0},{32,16},{48,32},{64,48},{80,64},{96,80},{112,96},{1... | collective-permute-start | bytes 196616 | tf_op jit(solution)/shard_map/ppermute | solution.py:51
  31.9 54.7 %collective-permute-start.23 = (bf16[256,512]{1,0:T(8,128)(2,1)}, bf16[256,512]{1,0:T(8,128)(2,1)S(1)}, u32[]{:S(2)}, u32[]{:S(2)}) collective-permute-start(bf16[256,512]{1,0:T(8,128)(2,1)} %param.13), channel_id=1, source_target_pairs={{0,0},{1,16},{2,32},{3,48},{4,64},{5,80},{6,96},{7,112},{8,128},{9... | collective-permute-start | bytes 786440 | tf_op jit(solution)/shard_map/ppermute | solution.py:113
  52.4 28.3 %all-to-all-start = ((bf16[16,512,2,8]{1,3,2,0:T(8,128)(2,1)}), bf16[16,512,2,8]{1,3,2,0:T(8,128)(2,1)S(1)}, u32[]{:S(2)}, u32[]{:S(2)}) async-start(bf16[16,512,2,8]{1,3,2,0:T(8,128)(2,1)} %broadcast_select_fusion), calls=%async_computation | async-start | bytes 524288 | tf_op jit(solution)/shard_map/all_to_all | solution.py:68
  67.6 102.8 %all-gather.8.cloned.1.call-start = ((), (), s32[]{:S(2)}) async-start(), calls=%async_computation.4 | async-start | bytes 4456448 | tf_op jit(solution)/shard_map/all_gather | solution.py:118
  81.3 10.8 %collective-permute-start.15 = (bf16[512,256]{0,1:T(8,128)(2,1)S(1)}, bf16[512,256]{0,1:T(8,128)(2,1)S(1)}, u32[]{:S(2)}, u32[]{:S(2)}) collective-permute-start(bf16[512,256]{0,1:T(8,128)(2,1)S(1)} %pad_maximum_fusion), channel_id=1, source_target_pairs={{0,128},{16,144},{32,160},{48,176},{64,192},{80,208},{96,224},{112... | collective-permute-start | bytes 786440 | tf_op jit(solution)/shard_map/ppermute | solution.py:80
  83.3 11.7 %collective-permute-start.16 = (bf16[512,256]{0,1:T(8,128)(2,1)S(1)}, bf16[512,256]{0,1:T(8,128)(2,1)S(1)}, u32[]{:S(2)}, u32[]{:S(2)}) collective-permute-start(bf16[512,256]{0,1:T(8,128)(2,1)S(1)} %pad_maximum_fusion), channel_id=1, source_target_pairs={{0,112},{16,128},{32,144},{48,160},{64,176},{80,192},{96,208},{112... | collective-permute-start | bytes 786440 | tf_op jit(solution)/shard_map/ppermute | solution.py:80
  84.7 21.7 %collective-permute-start.17 = (bf16[512,256]{0,1:T(8,128)(2,1)S(1)}, bf16[512,256]{0,1:T(8,128)(2,1)S(1)}, u32[]{:S(2)}, u32[]{:S(2)}) collective-permute-start(bf16[512,256]{0,1:T(8,128)(2,1)S(1)} %pad_maximum_fusion), channel_id=1, source_target_pairs={{0,96},{16,112},{32,128},{48,144},{64,160},{80,176},{96,192},{112,... | collective-permute-start | bytes 786440 | tf_op jit(solution)/shard_map/ppermute | solution.py:80
  87.4 157.0 %all-gather.6.cloned.1.call-start = ((), (), s32[]{:S(2)}) async-start(), calls=%async_computation.3 | async-start | bytes 4456448 | tf_op jit(solution)/shard_map/all_gather | solution.py:119
  87.5 26.1 %collective-permute-start.18 = (bf16[512,256]{0,1:T(8,128)(2,1)S(1)}, bf16[512,256]{0,1:T(8,128)(2,1)S(1)}, u32[]{:S(2)}, u32[]{:S(2)}) collective-permute-start(bf16[512,256]{0,1:T(8,128)(2,1)S(1)} %pad_maximum_fusion), channel_id=1, source_target_pairs={{0,80},{16,96},{32,112},{48,128},{64,144},{80,160},{96,176},{112,1... | collective-permute-start | bytes 786440 | tf_op jit(solution)/shard_map/ppermute | solution.py:80
  89.4 35.4 %collective-permute-start.19 = (bf16[512,256]{0,1:T(8,128)(2,1)S(1)}, bf16[512,256]{0,1:T(8,128)(2,1)S(1)}, u32[]{:S(2)}, u32[]{:S(2)}) collective-permute-start(bf16[512,256]{0,1:T(8,128)(2,1)S(1)} %pad_maximum_fusion), channel_id=1, source_target_pairs={{0,64},{16,80},{32,96},{48,112},{64,128},{80,144},{96,160},{112,17... | collective-permute-start | bytes 786440 | tf_op jit(solution)/shard_map/ppermute | solution.py:80
  92.1 44.1 %collective-permute-start.20 = (bf16[512,256]{0,1:T(8,128)(2,1)S(1)}, bf16[512,256]{0,1:T(8,128)(2,1)S(1)}, u32[]{:S(2)}, u32[]{:S(2)}) collective-permute-start(bf16[512,256]{0,1:T(8,128)(2,1)S(1)} %pad_maximum_fusion), channel_id=1, source_target_pairs={{0,48},{16,64},{32,80},{48,96},{64,112},{80,128},{96,144},{112,160... | collective-permute-start | bytes 786440 | tf_op jit(solution)/shard_map/ppermute | solution.py:80
  94.9 47.8 %collective-permute-start.21 = (bf16[512,256]{0,1:T(8,128)(2,1)S(1)}, bf16[512,256]{0,1:T(8,128)(2,1)S(1)}, u32[]{:S(2)}, u32[]{:S(2)}) collective-permute-start(bf16[512,256]{0,1:T(8,128)(2,1)S(1)} %pad_maximum_fusion), channel_id=1, source_target_pairs={{0,32},{16,48},{32,64},{48,80},{64,96},{80,112},{96,128},{112,144}... | collective-permute-start | bytes 786440 | tf_op jit(solution)/shard_map/ppermute | solution.py:80
  106.4 36.3 %collective-permute-start.22 = (bf16[512,256]{0,1:T(8,128)(2,1)S(1)}, bf16[512,256]{0,1:T(8,128)(2,1)S(1)}, u32[]{:S(2)}, u32[]{:S(2)}) collective-permute-start(bf16[512,256]{0,1:T(8,128)(2,1)S(1)} %pad_maximum_fusion), channel_id=1, source_target_pairs={{0,16},{16,32},{32,48},{48,64},{64,80},{80,96},{96,112},{112,128},... | collective-permute-start | bytes 786440 | tf_op jit(solution)/shard_map/ppermute | solution.py:80
  (9 other events, 57.8 us)
Sparse Core Ops, SparseCore 0:
  9.2 57.2 all-gather.3
  87.5 52.1 all-gather.7
  170.4 73.9 all-gather.5
